TPU v7x, 256 devices: a whole 4x4x8 slice. The times are simulated.
256 devices in a mesh: doc: 16 (over z_hi, x, core), word: 16 (over y, z_lo).
Axes of the slice: x: 4, y: 4, z: 8 (z_hi: 2, z_lo: 4; z = z_hi * 4 + z_lo), core: 2. Of those that a mesh axis runs over, the one named last changes fastest.
Arguments:
- counts: int32 [8192, 8192], P('doc', 'word'), may hold values from 0 to 29
- topics: float32 [8192, 256], P(('word', 'doc')), may hold values from 0.05 to 0.5
- latent: float32 [8192, 8192], P('doc', 'word'), may hold values from 0.5 to 30
- dual_latent: float32 [8192, 8192], P('doc', 'word'), may hold values from -3 to 3
- doc_plus: float32 [8192, 256], P(('doc', 'word')), may hold values from 0 to 0.5
- topic_plus: float32 [8192, 256], P(('word', 'doc')), may hold values from 0 to 3
- dual_doc: float32 [8192, 256], P(('doc', 'word')), may hold values from -2 to 2
- dual_topic: float32 [8192, 256], P(('word', 'doc')), may hold values from -2 to 2
Outputs:
- doc_factor_out: float32 [8192, 256], P(('doc', 'word'))
- topics_out: float32 [8192, 256], P(('word', 'doc'))
- latent_out: float32 [8192, 8192], P('doc', 'word')
- dual_latent_out: float32 [8192, 8192], P('doc', 'word')
- doc_plus_out: float32 [8192, 256], P(('doc', 'word'))
- topic_plus_out: float32 [8192, 256], P(('word', 'doc'))
- dual_doc_out: float32 [8192, 256], P(('doc', 'word'))
- dual_topic_out: float32 [8192, 256], P(('word', 'doc'))
All inputs are finite; a program needn't handle non-finite values. Where the computation divides by a largest or mean magnitude, that divisor is 1e-20 or more.
Results may differ from a plain program's by a relative error of at most 0.00075.
Values sent between devices are 32-bit elements; how exact they have to be, the bound alone decides.
No kernel may reach another device: no remote copies, remote signals or barrier semaphores. Data moves between devices by JAX's collectives and lax.ppermute only.
A program may use at most 64 MiB of HBM per device.

v0:
```python
import jax
import jax.numpy as jnp
from jax import lax
from jax.sharding import PartitionSpec as P

ITERS = 2
NEWTON = 18


def joined_along(pieces, dim):
    pieces = jnp.moveaxis(pieces, 0, dim)
    dims = pieces.shape
    return pieces.reshape(*dims[:dim], dims[dim] * dims[dim + 1], *dims[dim + 2 :])


def copy_for_each(x, axis):
    count = lax.axis_size(axis)
    return lax.all_to_all(jnp.broadcast_to(x[None], (count, *x.shape)), axis, 0, 0, tiled=True)


def gathered_copies(x, axis, dim):
    return joined_along(copy_for_each(x, axis), dim)


def split_up(x, dim, count):
    dims = x.shape
    pieces = x.reshape(*dims[:dim], count, dims[dim] // count, *dims[dim + 1 :])
    return jnp.moveaxis(pieces, dim, 0)


def summed_on_arrival(x, axis, dim):
    count = lax.axis_size(axis)
    pieces = lax.all_to_all(split_up(x, dim, count), axis, 0, 0, tiled=True)
    return jnp.sum(pieces, axis=0)


def rows_for(lines, count):
    spare = -len(lines) % count
    return jnp.pad(lines, [(0, spare)] + [(0, 0)] * (lines.ndim - 1))


def nested_sum(x, axes):
    lines = x.reshape(-1, x.shape[-1])
    own = summed_on_arrival(rows_for(lines, lax.axis_size(axes)), axes, 0)
    whole = gathered_copies(own, axes, 0)
    return whole[: len(lines)].reshape(x.shape)


def product(left, right):
    return jnp.dot(left, right, precision=lax.Precision.HIGHEST, preferred_element_type=jnp.float32)


def product_left(left, right):
    return lax.dot_general(
        left,
        right,
        (((0,), (0,)), ((), ())),
        precision=lax.Precision.HIGHEST,
        preferred_element_type=jnp.float32,
    )


def product_right(left, right):
    return lax.dot_general(
        left,
        right,
        (((1,), (1,)), ((), ())),
        precision=lax.Precision.HIGHEST,
        preferred_element_type=jnp.float32,
    )


def invert(gram):
    identity_mat = jnp.eye(gram.shape[0], dtype=jnp.float32)
    matrix = gram + identity_mat
    row_bound = jnp.max(jnp.sum(jnp.abs(matrix), axis=1))
    approx = identity_mat / row_bound
    for newton_step in range(NEWTON):
        approx = product(approx, 2.0 * identity_mat - product(matrix, approx))
    return approx


def gather_topics(topics):
    return gathered_copies(topics, "doc", 0)


def per_device(counts, topics, latent, dual_latent, doc_plus, topic_plus, dual_doc, dual_topic):
    counts_float = counts.astype(jnp.float32)
    doc_factor = doc_plus
    topic_tile = gather_topics(topics)
    for iteration in range(ITERS):
        merged = latent + dual_latent
        gram_topic = nested_sum(product_left(topic_tile, topic_tile), "word")

        def doc_term(first_row, row_count, merged=merged, topic_tile=topic_tile):
            return product(merged, topic_tile)

        doc_sums = summed_on_arrival(
            doc_term(jnp.int32(0), doc_plus.shape[0] * lax.axis_size("word")), "word", 0
        )
        doc_factor = product(doc_sums + doc_plus - dual_doc, invert(gram_topic))
        doc_tile = gathered_copies(doc_factor, "word", 0)
        gram_doc = nested_sum(product_left(doc_tile, doc_tile), "doc")
        inverse_doc = invert(gram_doc)

        def word_term(first_row, row_count, merged=merged, doc_tile=doc_tile):
            return product_left(merged, doc_tile)

        word_sums = summed_on_arrival(
            word_term(jnp.int32(0), topics.shape[0] * lax.axis_size("doc")), "doc", 0
        )
        topics = product(word_sums + topic_plus - dual_topic, inverse_doc)
        topic_tile = gather_topics(topics)
        rebuilt = product_right(doc_tile, topic_tile)
        shifted = rebuilt - dual_latent - 1.0
        latent = 0.5 * (shifted + jnp.sqrt(shifted * shifted + 4.0 * counts_float))
        doc_plus = jnp.maximum(doc_factor + dual_doc, 0.0)
        topic_plus = jnp.maximum(topics + dual_topic, 0.0)
        dual_latent = dual_latent + latent - rebuilt
        dual_doc = dual_doc + doc_factor - doc_plus
        dual_topic = dual_topic + topics - topic_plus
    return (doc_factor, topics, latent, dual_latent, doc_plus, topic_plus, dual_doc, dual_topic)


def solution(mesh):
    in_specs = (
        P("doc", "word"),
        P(("word", "doc"), None),
        P("doc", "word"),
        P("doc", "word"),
        P(("doc", "word"), None),
        P(("word", "doc"), None),
        P(("doc", "word"), None),
        P(("word", "doc"), None),
    )
    out_specs = (
        P(("doc", "word"), None),
        P(("word", "doc"), None),
        P("doc", "word"),
        P("doc", "word"),
        P(("doc", "word"), None),
        P(("word", "doc"), None),
        P(("doc", "word"), None),
        P(("word", "doc"), None),
    )
    return jax.shard_map(
        per_device, mesh=mesh, in_specs=in_specs, out_specs=out_specs, check_vma=False
    )
```

profile of v0, /device:TPU:65, one launch (start us, length us, event | category | flops | bytes accessed | tf_op | source)
XLA Modules:
  0.0 349.9 jit_solution(12616732271446020429)
XLA Ops:
  1.4 28.9 %all_to_all.85 = f32[16,32,256]{2,1,0:T(8,128)S(1)} all-to-all(f32[16,32,256]{2,1,0:T(8,128)S(1)} %broadcast_in_dim.18), channel_id=1, replica_groups=mesh['doc'=16,'word'=16] {'doc'}, dimensions={0} | all-to-all | bytes 1048576 | tf_op jit(solution)/shard_map/all_to_all | solution.py:18
  31.2 13.9 %all_to_all.86 = f32[16,16,256]{2,1,0:T(8,128)S(1)} all-to-all(f32[16,16,256]{2,1,0:T(8,128)S(1)} %fusion.68), channel_id=1, replica_groups=mesh['doc'=16,'word'=16] {'word'}, dimensions={0} | all-to-all | bytes 524288 | tf_op jit(solution)/shard_map/all_to_all | solution.py:33
  45.8 5.9 %all-to-all-start.3 = ((f32[16,16,256]{2,1,0:T(8,128)}), f32[16,16,256]{2,1,0:T(8,128)S(1)}, u32[]{:S(2)}, u32[]{:S(2)}) async-start(f32[16,16,256]{2,1,0:T(8,128)} %broadcast_in_dim.19), calls=%async_computation.3 | async-start | bytes 524288 | tf_op jit(solution)/shard_map/all_to_all | solution.py:18
  54.9 4.1 %all-to-all-done.3 = f32[16,16,256]{2,1,0:T(8,128)S(1)} async-done(((f32[16,16,256]{2,1,0:T(8,128)}), f32[16,16,256]{2,1,0:T(8,128)S(1)}, u32[]{:S(2)}, u32[]{:S(2)}) %all-to-all-start.3) | async-done | bytes 262176 | tf_op jit(solution)/shard_map/all_to_all | solution.py:18
  59.0 6.3 %all-to-all-start.1 = ((f32[16,32,256]{2,1,0:T(8,128)}), f32[16,32,256]{2,1,0:T(8,128)S(1)}, u32[]{:S(2)}, u32[]{:S(2)}) async-start(f32[16,32,256]{2,1,0:T(8,128)} %fusion.67), calls=%async_computation.1 | async-start | bytes 1048576 | tf_op jit(solution)/shard_map/all_to_all | solution.py:33
  82.5 19.4 %all_to_all.87 = f32[16,32,256]{2,1,0:T(8,128)S(1)} all-to-all(f32[16,32,256]{2,1,0:T(8,128)S(1)} %broadcast_in_dim.20), channel_id=1, replica_groups=mesh['doc'=16,'word'=16] {'word'}, dimensions={0} | all-to-all | bytes 1048576 | tf_op jit(solution)/shard_map/all_to_all | solution.py:18
  102.7 19.6 %all_to_all.88 = f32[16,16,256]{2,1,0:T(8,128)S(1)} all-to-all(f32[16,16,256]{2,1,0:T(8,128)S(1)} %fusion.87), channel_id=1, replica_groups=mesh['doc'=16,'word'=16] {'doc'}, dimensions={0} | all-to-all | bytes 524288 | tf_op jit(solution)/shard_map/all_to_all | solution.py:33
  123.1 4.5 %all-to-all-start.7 = ((f32[16,16,256]{2,1,0:T(8,128)}), f32[16,16,256]{2,1,0:T(8,128)S(1)}, u32[]{:S(2)}, u32[]{:S(2)}) async-start(f32[16,16,256]{2,1,0:T(8,128)} %broadcast_in_dim.21), calls=%async_computation.7 | async-start | bytes 524288 | tf_op jit(solution)/shard_map/all_to_all | solution.py:18
  128.9 3.0 fusion.86
  131.9 9.6 %all-to-all-done.7 = f32[16,16,256]{2,1,0:T(8,128)S(1)} async-done(((f32[16,16,256]{2,1,0:T(8,128)}), f32[16,16,256]{2,1,0:T(8,128)S(1)}, u32[]{:S(2)}, u32[]{:S(2)}) %all-to-all-start.7) | async-done | bytes 262176 | tf_op jit(solution)/shard_map/all_to_all | solution.py:18
  141.5 4.4 %all-to-all-start.5 = ((f32[16,32,256]{2,1,0:T(8,128)}), f32[16,32,256]{2,1,0:T(8,128)S(1)}, u32[]{:S(2)}, u32[]{:S(2)}) async-start(f32[16,32,256]{2,1,0:T(8,128)} %fusion.86), calls=%async_computation.5 | async-start | bytes 1048576 | tf_op jit(solution)/shard_map/all_to_all | solution.py:33
  164.0 25.9 %all_to_all.89 = f32[16,32,256]{2,1,0:T(8,128)S(1)} all-to-all(f32[16,32,256]{2,1,0:T(8,128)S(1)} %broadcast_in_dim.22), channel_id=1, replica_groups=mesh['doc'=16,'word'=16] {'doc'}, dimensions={0} | all-to-all | bytes 1048576 | tf_op jit(solution)/shard_map/all_to_all | solution.py:18
  190.7 11.8 %all_to_all.90 = f32[16,16,256]{2,1,0:T(8,128)S(1)} all-to-all(f32[16,16,256]{2,1,0:T(8,128)S(1)} %fusion.106), channel_id=1, replica_groups=mesh['doc'=16,'word'=16] {'word'}, dimensions={0} | all-to-all | bytes 524288 | tf_op jit(solution)/shard_map/all_to_all | solution.py:33
  203.2 5.2 %all-to-all-start.11 = ((f32[16,16,256]{2,1,0:T(8,128)}), f32[16,16,256]{2,1,0:T(8,128)S(1)}, u32[]{:S(2)}, u32[]{:S(2)}) async-start(f32[16,16,256]{2,1,0:T(8,128)} %broadcast_in_dim.23), calls=%async_computation.11 | async-start | bytes 524288 | tf_op jit(solution)/shard_map/all_to_all | solution.py:18
  208.5 3.8 %fusion = (f32[512,512]{1,0:T(8,128)S(1)}, f32[512,512]{1,0:T(8,128)}) fusion(s32[512,512]{1,0:T(8,128)} %param.8, f32[512,512]{1,0:T(8,128)S(1)} %copy-done, f32[512,256]{1,0:T(8,128)S(1)} %bitcast.346, f32[512,256]{1,0:T(8,128)S(1)} %bitcast.349), kind=kOutput, calls=%fused_computation.85 | convolution fusion | flops 808189952 | bytes 5242880 | tf_op jit(solution)/shard_map/dot_general | solution.py:64
  216.1 5.9 %all-to-all-start.9 = ((f32[16,32,256]{2,1,0:T(8,128)}), f32[16,32,256]{2,1,0:T(8,128)S(1)}, u32[]{:S(2)}, u32[]{:S(2)}) async-start(f32[16,32,256]{2,1,0:T(8,128)} %fusion.105), calls=%async_computation.9 | async-start | bytes 1048576 | tf_op jit(solution)/shard_map/all_to_all | solution.py:33
  239.4 19.4 %all_to_all.91 = f32[16,32,256]{2,1,0:T(8,128)S(1)} all-to-all(f32[16,32,256]{2,1,0:T(8,128)S(1)} %broadcast_in_dim.24), channel_id=1, replica_groups=mesh['doc'=16,'word'=16] {'word'}, dimensions={0} | all-to-all | bytes 1048576 | tf_op jit(solution)/shard_map/all_to_all | solution.py:18
  259.6 18.8 %all_to_all.92 = f32[16,16,256]{2,1,0:T(8,128)S(1)} all-to-all(f32[16,16,256]{2,1,0:T(8,128)S(1)} %fusion.125), channel_id=1, replica_groups=mesh['doc'=16,'word'=16] {'doc'}, dimensions={0} | all-to-all | bytes 524288 | tf_op jit(solution)/shard_map/all_to_all | solution.py:33
  279.1 4.5 %all-to-all-start.15 = ((f32[16,16,256]{2,1,0:T(8,128)}), f32[16,16,256]{2,1,0:T(8,128)S(1)}, u32[]{:S(2)}, u32[]{:S(2)}) async-start(f32[16,16,256]{2,1,0:T(8,128)} %broadcast_in_dim.25), calls=%async_computation.15 | async-start | bytes 524288 | tf_op jit(solution)/shard_map/all_to_all | solution.py:18
  284.9 3.0 fusion.124
  287.9 9.6 %all-to-all-done.15 = f32[16,16,256]{2,1,0:T(8,128)S(1)} async-done(((f32[16,16,256]{2,1,0:T(8,128)}), f32[16,16,256]{2,1,0:T(8,128)S(1)}, u32[]{:S(2)}, u32[]{:S(2)}) %all-to-all-start.15) | async-done | bytes 262176 | tf_op jit(solution)/shard_map/all_to_all | solution.py:18
  297.6 4.4 %all-to-all-start.13 = ((f32[16,32,256]{2,1,0:T(8,128)}), f32[16,32,256]{2,1,0:T(8,128)S(1)}, u32[]{:S(2)}, u32[]{:S(2)}) async-start(f32[16,32,256]{2,1,0:T(8,128)} %fusion.124), calls=%async_computation.13 | async-start | bytes 1048576 | tf_op jit(solution)/shard_map/all_to_all | solution.py:33
  321.2 25.1 %all_to_all.93 = f32[16,32,256]{2,1,0:T(8,128)S(1)} all-to-all(f32[16,32,256]{2,1,0:T(8,128)S(1)} %broadcast_in_dim.26), channel_id=1, replica_groups=mesh['doc'=16,'word'=16] {'doc'}, dimensions={0} | all-to-all | bytes 1048576 | tf_op jit(solution)/shard_map/all_to_all | solution.py:18
  346.4 3.3 add_subtract_fusion
  (214 shorter events, 84.5 us)
Async XLA Ops:
  31.2 20.5 %copy-start = (f32[512,512]{1,0:T(8,128)S(1)}, f32[512,512]{1,0:T(8,128)}, u32[]{:S(2)}) copy-start(f32[512,512]{1,0:T(8,128)} %param.11) | copy-start | bytes 3145732
  45.8 13.2 %all-to-all-start.3 = ((f32[16,16,256]{2,1,0:T(8,128)}), f32[16,16,256]{2,1,0:T(8,128)S(1)}, u32[]{:S(2)}, u32[]{:S(2)}) async-start(f32[16,16,256]{2,1,0:T(8,128)} %broadcast_in_dim.19), calls=%async_computation.3 | async-start | bytes 524288 | tf_op jit(solution)/shard_map/all_to_all | solution.py:18
  59.0 22.5 %all-to-all-start.1 = ((f32[16,32,256]{2,1,0:T(8,128)}), f32[16,32,256]{2,1,0:T(8,128)S(1)}, u32[]{:S(2)}, u32[]{:S(2)}) async-start(f32[16,32,256]{2,1,0:T(8,128)} %fusion.67), calls=%async_computation.1 | async-start | bytes 1048576 | tf_op jit(solution)/shard_map/all_to_all | solution.py:33
  81.5 0.8 copy-start.3
  81.5 0.8 copy-start.7
  123.1 18.4 %all-to-all-start.7 = ((f32[16,16,256]{2,1,0:T(8,128)}), f32[16,16,256]{2,1,0:T(8,128)S(1)}, u32[]{:S(2)}, u32[]{:S(2)}) async-start(f32[16,16,256]{2,1,0:T(8,128)} %broadcast_in_dim.21), calls=%async_computation.7 | async-start | bytes 524288 | tf_op jit(solution)/shard_map/all_to_all | solution.py:18
  141.5 22.1 %all-to-all-start.5 = ((f32[16,32,256]{2,1,0:T(8,128)}), f32[16,32,256]{2,1,0:T(8,128)S(1)}, u32[]{:S(2)}, u32[]{:S(2)}) async-start(f32[16,32,256]{2,1,0:T(8,128)} %fusion.86), calls=%async_computation.5 | async-start | bytes 1048576 | tf_op jit(solution)/shard_map/all_to_all | solution.py:33
  161.5 2.1 copy-start.4
  161.6 2.1 copy-start.8
  203.2 12.9 %all-to-all-start.11 = ((f32[16,16,256]{2,1,0:T(8,128)}), f32[16,16,256]{2,1,0:T(8,128)S(1)}, u32[]{:S(2)}, u32[]{:S(2)}) async-start(f32[16,16,256]{2,1,0:T(8,128)} %broadcast_in_dim.23), calls=%async_computation.11 | async-start | bytes 524288 | tf_op jit(solution)/shard_map/all_to_all | solution.py:18
  216.1 21.8 %all-to-all-start.9 = ((f32[16,32,256]{2,1,0:T(8,128)}), f32[16,32,256]{2,1,0:T(8,128)S(1)}, u32[]{:S(2)}, u32[]{:S(2)}) async-start(f32[16,32,256]{2,1,0:T(8,128)} %fusion.105), calls=%async_computation.9 | async-start | bytes 1048576 | tf_op jit(solution)/shard_map/all_to_all | solution.py:33
  238.8 0.6 copy-start.5
  279.1 18.4 %all-to-all-start.15 = ((f32[16,16,256]{2,1,0:T(8,128)}), f32[16,16,256]{2,1,0:T(8,128)S(1)}, u32[]{:S(2)}, u32[]{:S(2)}) async-start(f32[16,16,256]{2,1,0:T(8,128)} %broadcast_in_dim.25), calls=%async_computation.15 | async-start | bytes 524288 | tf_op jit(solution)/shard_map/all_to_all | solution.py:18
  297.6 22.1 %all-to-all-start.13 = ((f32[16,32,256]{2,1,0:T(8,128)}), f32[16,32,256]{2,1,0:T(8,128)S(1)}, u32[]{:S(2)}, u32[]{:S(2)}) async-start(f32[16,32,256]{2,1,0:T(8,128)} %fusion.124), calls=%async_computation.13 | async-start | bytes 1048576 | tf_op jit(solution)/shard_map/all_to_all | solution.py:33
  319.7 26.7 %copy-start.2 = (f32[512,512]{1,0:T(8,128)S(1)}, f32[512,512]{1,0:T(8,128)}, u32[]{:S(2)}) copy-start(f32[512,512]{1,0:T(8,128)} %get-tuple-element.15) | copy-start | bytes 3145732
  319.7 26.6 %copy-start.1 = (s32[512,512]{1,0:T(8,128)S(1)}, s32[512,512]{1,0:T(8,128)}, u32[]{:S(2)}) copy-start(s32[512,512]{1,0:T(8,128)} %param.8) | copy-start | bytes 3145732
  320.6 0.6 copy-start.6
where the time goes:
time: 354 us; the launch traced here: 350 us
  blocking collectives  183 us (52%)
  matrix products  77.3 us (22%)
  starting transfers between devices  41.1 us (12%)
  waiting for transfers between devices  29.6 us (8%)
  local copies, waits for them, and re-layouts  9.13 us (3%)
  between operations  5.04 us (1%)
  other arithmetic  4.95 us (1%)
    all_to_all x5, blocking collectives, copy_for_each(): lax.all_to_all(jnp.broadcast_to(x[None], (count, *x.shape)), axis, 0, 0,...  119 us
    all_to_all x4, blocking collectives, summed_on_arrival(): pieces = lax.all_to_all(split_up(x, dim, count), axis, 0, 0, tiled=True)  64.1 us
    dot_general x150, matrix products, product(): jnp.dot(left, right, precision=lax.Precision.HIGHEST, preferred_element_t...  61.8 us
    all_to_all x4, waiting for transfers between devices, copy_for_each(): lax.all_to_all(jnp.broadcast_to(x[None], (count, *x.shape)), axis, 0, 0,...  25.4 us
    all_to_all x4, starting transfers between devices, summed_on_arrival(): pieces = lax.all_to_all(split_up(x, dim, count), axis, 0, 0, tiled=True)  21 us
    all_to_all x4, starting transfers between devices, copy_for_each(): lax.all_to_all(jnp.broadcast_to(x[None], (count, *x.shape)), axis, 0, 0,...  20.1 us
    dot_general x6, matrix products, product_left(): lax.dot_general(left, right, (((0,), (0,)), ((), ())), precision=lax.Prec...  8.36 us
    dot_general x2, matrix products, product_right(): lax.dot_general(left, right, (((1,), (1,)), ((), ())), precision=lax.Prec...  7.1 us
  transfers between devices with their start and end apart: 8, of which 6 were waited for; matrix products, arithmetic and copies ran while one was open for 22% of the time, Pallas kernels for 0%

commit v1 on v0

v1 whole, which is shorter than its diff:
```python
import jax
import jax.numpy as jnp
from jax import lax
from jax.sharding import PartitionSpec as P

ITERS = 2
NEWTON = 18
ALL = ("doc", "word")


def partners(axis, bit):
    return [(i, i ^ bit) for i in range(lax.axis_size(axis))]


def exchanged_sum(x, axis):
    bit = 1
    while bit < lax.axis_size(axis):
        x = x + lax.ppermute(x, axis, partners(axis, bit))
        bit *= 2
    return x


def exchanged_gather(x, axis):
    me = lax.axis_index(axis)
    bit = 1
    while bit < lax.axis_size(axis):
        other = lax.ppermute(x, axis, partners(axis, bit))
        x = jnp.where((me & bit) == 0, jnp.concatenate([x, other]), jnp.concatenate([other, x]))
        bit *= 2
    return x


def own_rows(tile, axis, rows):
    return lax.dynamic_slice_in_dim(tile, lax.axis_index(axis) * rows, rows, 0)


def product(left, right):
    return jnp.dot(left, right, precision=lax.Precision.HIGHEST, preferred_element_type=jnp.float32)


def product_left(left, right):
    return lax.dot_general(
        left,
        right,
        (((0,), (0,)), ((), ())),
        precision=lax.Precision.HIGHEST,
        preferred_element_type=jnp.float32,
    )


def product_right(left, right):
    return lax.dot_general(
        left,
        right,
        (((1,), (1,)), ((), ())),
        precision=lax.Precision.HIGHEST,
        preferred_element_type=jnp.float32,
    )


def invert(gram):
    identity_mat = jnp.eye(gram.shape[0], dtype=jnp.float32)
    matrix = gram + identity_mat
    row_bound = jnp.max(jnp.sum(jnp.abs(matrix), axis=1))
    approx = identity_mat / row_bound
    for newton_step in range(NEWTON):
        approx = product(approx, 2.0 * identity_mat - product(matrix, approx))
    return approx


def per_device(counts, topics, latent, dual_latent, doc_plus, topic_plus, dual_doc, dual_topic):
    counts_float = counts.astype(jnp.float32)
    rows, k = topics.shape
    topic_side = exchanged_gather(jnp.concatenate([topics, topic_plus, dual_topic], axis=1), "doc")
    topic_tile, topic_plus_tile, dual_topic_tile = (topic_side[:, i * k : (i + 1) * k] for i in range(3))
    doc_side = exchanged_gather(jnp.concatenate([doc_plus, dual_doc], axis=1), "word")
    doc_plus_tile, dual_doc_tile = doc_side[:, :k], doc_side[:, k:]
    gram_topic = exchanged_sum(product_left(topic_tile, topic_tile), "word")
    for iteration in range(ITERS):
        merged = latent + dual_latent
        inverse_topic = invert(gram_topic)
        doc_rhs_tile = exchanged_sum(product(merged, topic_tile), "word") + doc_plus_tile - dual_doc_tile
        doc_tile = product(doc_rhs_tile, inverse_topic)
        gram_doc = exchanged_sum(product_left(doc_tile, doc_tile), "doc")
        inverse_doc = invert(gram_doc)
        topic_rhs_tile = exchanged_sum(product_left(merged, doc_tile), "doc") + topic_plus_tile - dual_topic_tile
        topic_tile = product(topic_rhs_tile, inverse_doc)
        if iteration + 1 < ITERS:
            gram_topic = exchanged_sum(product_left(topic_tile, topic_tile), "word")
        rebuilt = product_right(doc_tile, topic_tile)
        shifted = rebuilt - dual_latent - 1.0
        latent = 0.5 * (shifted + jnp.sqrt(shifted * shifted + 4.0 * counts_float))
        doc_plus_tile = jnp.maximum(doc_tile + dual_doc_tile, 0.0)
        topic_plus_tile = jnp.maximum(topic_tile + dual_topic_tile, 0.0)
        dual_latent = dual_latent + latent - rebuilt
        dual_doc_tile = dual_doc_tile + doc_tile - doc_plus_tile
        dual_topic_tile = dual_topic_tile + topic_tile - topic_plus_tile
    doc_rows = [own_rows(t, "word", rows) for t in (doc_tile, doc_plus_tile, dual_doc_tile)]
    topic_rows = [own_rows(t, "doc", rows) for t in (topic_tile, topic_plus_tile, dual_topic_tile)]
    return (doc_rows[0], topic_rows[0], latent, dual_latent, doc_rows[1], topic_rows[1], doc_rows[2], topic_rows[2])


def solution(mesh):
    in_specs = (
        P("doc", "word"),
        P(("word", "doc"), None),
        P("doc", "word"),
        P("doc", "word"),
        P(("doc", "word"), None),
        P(("word", "doc"), None),
        P(("doc", "word"), None),
        P(("word", "doc"), None),
    )
    out_specs = (
        P(("doc", "word"), None),
        P(("word", "doc"), None),
        P("doc", "word"),
        P("doc", "word"),
        P(("doc", "word"), None),
        P(("word", "doc"), None),
        P(("doc", "word"), None),
        P(("word", "doc"), None),
    )
    return jax.shard_map(
        per_device, mesh=mesh, in_specs=in_specs, out_specs=out_specs, check_vma=False
    )
```

time: 354 us -> 440 us (1.24)
  the two profiles are of different devices: /device:TPU:65 before, /device:TPU:96 now
where the time goes in v1:
time: 440 us; the launch traced here: 431 us
  waiting for transfers between devices  247 us (56%)
  matrix products  95.7 us (22%)
  starting transfers between devices  64.2 us (15%)
  other arithmetic  15.3 us (3%)
  between operations  5.24 us (1%)
    ppermute x32, waiting for transfers between devices, exchanged_sum(): x = x + lax.ppermute(x, axis, partners(axis, bit))  191 us
    dot_general x150, matrix products, product(): jnp.dot(left, right, precision=lax.Precision.HIGHEST, preferred_element_t...  82.2 us
    ppermute x8, waiting for transfers between devices, exchanged_gather(): other = lax.ppermute(x, axis, partners(axis, bit))  56.5 us
    ppermute x32, starting transfers between devices, exchanged_sum(): x = x + lax.ppermute(x, axis, partners(axis, bit))  48 us
    ppermute x8, starting transfers between devices, exchanged_gather(): other = lax.ppermute(x, axis, partners(axis, bit))  16.2 us
  transfers between devices with their start and end apart: 40, of which 29 were waited for; matrix products, arithmetic and copies ran while one was open for 22% of the time, Pallas kernels for 0%

profile of v1, /device:TPU:96, one launch (start us, length us, event | category | flops | bytes accessed | tf_op | source)
XLA Modules:
  0.0 431.3 jit_solution(7704711838701962396)
XLA Ops:
  5.8 5.5 %collective-permute-done.1 = f32[64,768]{1,0:T(8,128)S(1)} collective-permute-done((f32[64,768]{1,0:T(8,128)S(1)}, f32[64,768]{1,0:T(8,128)S(1)}, u32[]{:S(2)}, u32[]{:S(2)}) %collective-permute-start.1) | collective-permute-done | bytes 196640 | tf_op jit(solution)/shard_map/ppermute | solution.py:27
  14.5 8.8 %collective-permute-done.2 = f32[128,768]{1,0:T(8,128)S(1)} collective-permute-done((f32[128,768]{1,0:T(8,128)S(1)}, f32[128,768]{1,0:T(8,128)S(1)}, u32[]{:S(2)}, u32[]{:S(2)}) %collective-permute-start.2) | collective-permute-done | bytes 393248 | tf_op jit(solution)/shard_map/ppermute | solution.py:27
  23.4 4.6 %collective-permute-start.3 = (f32[256,768]{1,0:T(8,128)S(1)}, f32[256,768]{1,0:T(8,128)S(1)}, u32[]{:S(2)}, u32[]{:S(2)}) collective-permute-start(f32[256,768]{1,0:T(8,128)S(1)} %maximum_select_fusion.2), channel_id=1, source_target_pairs={{0,128},{16,144},{32,160},{48,176},{64,192},{80,208},{96,224},{112... | collective-permute-start | bytes 2359304 | tf_op jit(solution)/shard_map/ppermute | solution.py:27
  29.1 34.0 %collective-permute-done.8 = f32[32,512]{1,0:T(8,128)S(1)} collective-permute-done((f32[32,512]{1,0:T(8,128)S(1)}, f32[32,512]{1,0:T(8,128)S(1)}, u32[]{:S(2)}, u32[]{:S(2)}) %collective-permute-start.8) | collective-permute-done | bytes 65568 | tf_op jit(solution)/shard_map/ppermute | solution.py:27
  63.8 6.0 %collective-permute-done.9 = f32[64,512]{1,0:T(8,128)S(1)} collective-permute-done((f32[64,512]{1,0:T(8,128)S(1)}, f32[64,512]{1,0:T(8,128)S(1)}, u32[]{:S(2)}, u32[]{:S(2)}) %collective-permute-start.9) | collective-permute-done | bytes 131104 | tf_op jit(solution)/shard_map/ppermute | solution.py:27
  86.3 5.2 %collective-permute-done.13 = f32[256,256]{0,1:T(8,128)S(1)} collective-permute-done((f32[256,256]{0,1:T(8,128)S(1)}, f32[256,256]{0,1:T(8,128)S(1)}, u32[]{:S(2)}, u32[]{:S(2)}) %collective-permute-start.13) | collective-permute-done | bytes 262176 | tf_op jit(solution)/shard_map/ppermute | solution.py:18
  93.0 7.7 %collective-permute-done.14 = f32[256,256]{0,1:T(8,128)S(1)} collective-permute-done((f32[256,256]{0,1:T(8,128)S(1)}, f32[256,256]{0,1:T(8,128)S(1)}, u32[]{:S(2)}, u32[]{:S(2)}) %collective-permute-start.14) | collective-permute-done | bytes 262176 | tf_op jit(solution)/shard_map/ppermute | solution.py:18
  130.9 10.6 %collective-permute-done.6 = f32[512,256]{1,0:T(8,128)S(1)} collective-permute-done((f32[512,256]{1,0:T(8,128)S(1)}, f32[512,256]{1,0:T(8,128)S(1)}, u32[]{:S(2)}, u32[]{:S(2)}) %collective-permute-start.6) | collective-permute-done | bytes 524320 | tf_op jit(solution)/shard_map/ppermute | solution.py:18
  145.6 6.8 %collective-permute-done.7 = f32[512,256]{1,0:T(8,128)S(1)} collective-permute-done((f32[512,256]{1,0:T(8,128)S(1)}, f32[512,256]{1,0:T(8,128)S(1)}, u32[]{:S(2)}, u32[]{:S(2)}) %collective-permute-start.7) | collective-permute-done | bytes 524320 | tf_op jit(solution)/shard_map/ppermute | solution.py:18
  160.7 6.8 %collective-permute-done.21 = f32[256,256]{0,1:T(8,128)S(1)} collective-permute-done((f32[256,256]{0,1:T(8,128)S(1)}, f32[256,256]{0,1:T(8,128)S(1)}, u32[]{:S(2)}, u32[]{:S(2)}) %collective-permute-start.21) | collective-permute-done | bytes 262176 | tf_op jit(solution)/shard_map/ppermute | solution.py:18
  169.9 15.1 %collective-permute-done.22 = f32[256,256]{0,1:T(8,128)S(1)} collective-permute-done((f32[256,256]{0,1:T(8,128)S(1)}, f32[256,256]{0,1:T(8,128)S(1)}, u32[]{:S(2)}, u32[]{:S(2)}) %collective-permute-start.22) | collective-permute-done | bytes 262176 | tf_op jit(solution)/shard_map/ppermute | solution.py:18
  185.0 12.7 %collective-permute-start.23 = (f32[256,256]{0,1:T(8,128)S(1)}, f32[256,256]{0,1:T(8,128)S(1)}, u32[]{:S(2)}, u32[]{:S(2)}) collective-permute-start(f32[256,256]{0,1:T(8,128)S(1)} %add.190), channel_id=1, source_target_pairs={{0,128},{16,144},{32,160},{48,176},{64,192},{80,208},{96,224},{112... | collective-permute-start | bytes 786440 | tf_op jit(solution)/shard_map/ppermute | solution.py:18
  198.7 10.5 %collective-permute-done.23 = f32[256,256]{0,1:T(8,128)S(1)} collective-permute-done((f32[256,256]{0,1:T(8,128)S(1)}, f32[256,256]{0,1:T(8,128)S(1)}, u32[]{:S(2)}, u32[]{:S(2)}) %collective-permute-start.23) | collective-permute-done | bytes 262176 | tf_op jit(solution)/shard_map/ppermute | solution.py:18
  232.2 20.8 %collective-permute-done.19 = f32[512,256]{1,0:T(8,128)S(1)} collective-permute-done((f32[512,256]{1,0:T(8,128)S(1)}, f32[512,256]{1,0:T(8,128)S(1)}, u32[]{:S(2)}, u32[]{:S(2)}) %collective-permute-start.19) | collective-permute-done | bytes 524320 | tf_op jit(solution)/shard_map/ppermute | solution.py:18
  264.5 11.4 %collective-permute-done.29 = f32[256,256]{0,1:T(8,128)S(1)} collective-permute-done((f32[256,256]{0,1:T(8,128)S(1)}, f32[256,256]{0,1:T(8,128)S(1)}, u32[]{:S(2)}, u32[]{:S(2)}) %collective-permute-start.29) | collective-permute-done | bytes 262176 | tf_op jit(solution)/shard_map/ppermute | solution.py:18
  276.6 7.7 %collective-permute-done.30 = f32[256,256]{0,1:T(8,128)S(1)} collective-permute-done((f32[256,256]{0,1:T(8,128)S(1)}, f32[256,256]{0,1:T(8,128)S(1)}, u32[]{:S(2)}, u32[]{:S(2)}) %collective-permute-start.30) | collective-permute-done | bytes 262176 | tf_op jit(solution)/shard_map/ppermute | solution.py:18
  288.8 5.3 %collective-permute-done.31 = f32[256,256]{0,1:T(8,128)S(1)} collective-permute-done((f32[256,256]{0,1:T(8,128)S(1)}, f32[256,256]{0,1:T(8,128)S(1)}, u32[]{:S(2)}, u32[]{:S(2)}) %collective-permute-start.31) | collective-permute-done | bytes 262176 | tf_op jit(solution)/shard_map/ppermute | solution.py:18
  313.9 10.7 %collective-permute-done.26 = f32[512,256]{1,0:T(8,128)S(1)} collective-permute-done((f32[512,256]{1,0:T(8,128)S(1)}, f32[512,256]{1,0:T(8,128)S(1)}, u32[]{:S(2)}, u32[]{:S(2)}) %collective-permute-start.26) | collective-permute-done | bytes 524320 | tf_op jit(solution)/shard_map/ppermute | solution.py:18
  329.1 8.6 %collective-permute-done.27 = f32[512,256]{1,0:T(8,128)S(1)} collective-permute-done((f32[512,256]{1,0:T(8,128)S(1)}, f32[512,256]{1,0:T(8,128)S(1)}, u32[]{:S(2)}, u32[]{:S(2)}) %collective-permute-start.27) | collective-permute-done | bytes 524320 | tf_op jit(solution)/shard_map/ppermute | solution.py:18
  344.3 6.2 %collective-permute-done.37 = f32[256,256]{0,1:T(8,128)S(1)} collective-permute-done((f32[256,256]{0,1:T(8,128)S(1)}, f32[256,256]{0,1:T(8,128)S(1)}, u32[]{:S(2)}, u32[]{:S(2)}) %collective-permute-start.37) | collective-permute-done | bytes 262176 | tf_op jit(solution)/shard_map/ppermute | solution.py:18
  351.6 8.2 %collective-permute-done.38 = f32[256,256]{0,1:T(8,128)S(1)} collective-permute-done((f32[256,256]{0,1:T(8,128)S(1)}, f32[256,256]{0,1:T(8,128)S(1)}, u32[]{:S(2)}, u32[]{:S(2)}) %collective-permute-start.38) | collective-permute-done | bytes 262176 | tf_op jit(solution)/shard_map/ppermute | solution.py:18
  362.5 10.9 %collective-permute-done.39 = f32[256,256]{0,1:T(8,128)S(1)} collective-permute-done((f32[256,256]{0,1:T(8,128)S(1)}, f32[256,256]{0,1:T(8,128)S(1)}, u32[]{:S(2)}, u32[]{:S(2)}) %collective-permute-start.39) | collective-permute-done | bytes 262176 | tf_op jit(solution)/shard_map/ppermute | solution.py:18
  392.8 10.7 %collective-permute-done.34 = f32[512,256]{1,0:T(8,128)S(1)} collective-permute-done((f32[512,256]{1,0:T(8,128)S(1)}, f32[512,256]{1,0:T(8,128)S(1)}, u32[]{:S(2)}, u32[]{:S(2)}) %collective-permute-start.34) | collective-permute-done | bytes 524320 | tf_op jit(solution)/shard_map/ppermute | solution.py:18
  406.0 19.1 %collective-permute-done.35 = f32[512,256]{1,0:T(8,128)S(1)} collective-permute-done((f32[512,256]{1,0:T(8,128)S(1)}, f32[512,256]{1,0:T(8,128)S(1)}, u32[]{:S(2)}, u32[]{:S(2)}) %collective-permute-start.35) | collective-permute-done | bytes 524320 | tf_op jit(solution)/shard_map/ppermute | solution.py:18
  (284 shorter events, 172.2 us)
Async XLA Ops:
  11.3 11.9 %collective-permute-start.2 = (f32[128,768]{1,0:T(8,128)S(1)}, f32[128,768]{1,0:T(8,128)S(1)}, u32[]{:S(2)}, u32[]{:S(2)}) collective-permute-start(f32[128,768]{1,0:T(8,128)S(1)} %maximum_select_fusion.4), channel_id=1, source_target_pairs={{0,64},{16,80},{32,96},{48,112},{64,0},{80,16},{96,32},{112,48},{1... | collective-permute-start | bytes 1179656 | tf_op jit(solution)/shard_map/ppermute | solution.py:27
  23.4 48.1 %collective-permute-start.3 = (f32[256,768]{1,0:T(8,128)S(1)}, f32[256,768]{1,0:T(8,128)S(1)}, u32[]{:S(2)}, u32[]{:S(2)}) collective-permute-start(f32[256,768]{1,0:T(8,128)S(1)} %maximum_select_fusion.2), channel_id=1, source_target_pairs={{0,128},{16,144},{32,160},{48,176},{64,192},{80,208},{96,224},{112... | collective-permute-start | bytes 2359304 | tf_op jit(solution)/shard_map/ppermute | solution.py:27
  28.0 35.1 %collective-permute-start.8 = (f32[32,512]{1,0:T(8,128)S(1)}, f32[32,512]{1,0:T(8,128)S(1)}, u32[]{:S(2)}, u32[]{:S(2)}) collective-permute-start(f32[32,512]{1,0:T(8,128)S(1)} %constant_dynamic-update-slice_fusion.3), channel_id=1, source_target_pairs={{0,1},{1,0},{2,3},{3,2},{4,5},{5,4},{6,7},{7,6},{8,9},{9,8},{10,11... | collective-permute-start | bytes 196616 | tf_op jit(solution)/shard_map/ppermute | solution.py:27
  77.4 25.6 %collective-permute-start.11 = (f32[256,512]{1,0:T(8,128)S(1)}, f32[256,512]{1,0:T(8,128)}, u32[]{:S(2)}, u32[]{:S(2)}) collective-permute-start(f32[256,512]{1,0:T(8,128)S(1)} %maximum_select_fusion.3), channel_id=1, source_target_pairs={{0,8},{1,9},{2,10},{3,11},{4,12},{5,13},{6,14},{7,15},{8,0},{9,1},... | collective-permute-start | bytes 1572872 | tf_op jit(solution)/shard_map/ppermute | solution.py:27
  81.4 10.1 %collective-permute-start.13 = (f32[256,256]{0,1:T(8,128)S(1)}, f32[256,256]{0,1:T(8,128)S(1)}, u32[]{:S(2)}, u32[]{:S(2)}) collective-permute-start(f32[256,256]{0,1:T(8,128)S(1)} %add.178), channel_id=1, source_target_pairs={{0,2},{1,3},{2,0},{3,1},{4,6},{5,7},{6,4},{7,5},{8,10},{9,11},{10,... | collective-permute-start | bytes 786440 | tf_op jit(solution)/shard_map/ppermute | solution.py:18
  84.5 20.8 %collective-permute-start.4 = (f32[512,256]{1,0:T(8,128)S(1)}, f32[512,256]{1,0:T(8,128)}, u32[]{:S(2)}, u32[]{:S(2)}) collective-permute-start(f32[512,256]{1,0:T(8,128)S(1)} %fusion.21), channel_id=1, source_target_pairs={{0,1},{1,0},{2,3},{3,2},{4,5},{5,4},{6,7},{7,6},{8,9},{9,8},{10,11... | collective-permute-start | bytes 1572872 | tf_op jit(solution)/shard_map/ppermute | solution.py:18
  106.6 20.0 %collective-permute-start.5 = (f32[512,256]{1,0:T(8,128)S(1)}, f32[512,256]{1,0:T(8,128)}, u32[]{:S(2)}, u32[]{:S(2)}) collective-permute-start(f32[512,256]{1,0:T(8,128)S(1)} %add.173), channel_id=1, source_target_pairs={{0,2},{1,3},{2,0},{3,1},{4,6},{5,7},{6,4},{7,5},{8,10},{9,11},{10,... | collective-permute-start | bytes 1572872 | tf_op jit(solution)/shard_map/ppermute | solution.py:18
  127.8 13.7 %collective-permute-start.6 = (f32[512,256]{1,0:T(8,128)S(1)}, f32[512,256]{1,0:T(8,128)S(1)}, u32[]{:S(2)}, u32[]{:S(2)}) collective-permute-start(f32[512,256]{1,0:T(8,128)S(1)} %add.174), channel_id=1, source_target_pairs={{0,4},{1,5},{2,6},{3,7},{4,0},{5,1},{6,2},{7,3},{8,12},{9,13},{10,... | collective-permute-start | bytes 1572872 | tf_op jit(solution)/shard_map/ppermute | solution.py:18
  141.6 10.8 %collective-permute-start.7 = (f32[512,256]{1,0:T(8,128)S(1)}, f32[512,256]{1,0:T(8,128)S(1)}, u32[]{:S(2)}, u32[]{:S(2)}) collective-permute-start(f32[512,256]{1,0:T(8,128)S(1)} %add.175), channel_id=1, source_target_pairs={{0,8},{1,9},{2,10},{3,11},{4,12},{5,13},{6,14},{7,15},{8,0},{9,1},... | collective-permute-start | bytes 1572872 | tf_op jit(solution)/shard_map/ppermute | solution.py:18
  159.2 38.5 %collective-permute-start.17 = (f32[512,256]{1,0:T(8,128)S(1)}, f32[512,256]{1,0:T(8,128)S(1)}, u32[]{:S(2)}, u32[]{:S(2)}) collective-permute-start(f32[512,256]{1,0:T(8,128)S(1)} %add.183), channel_id=1, source_target_pairs={{0,32},{16,48},{32,0},{48,16},{64,96},{80,112},{96,64},{112,80},{1... | collective-permute-start | bytes 1572872 | tf_op jit(solution)/shard_map/ppermute | solution.py:18
  167.5 17.5 %collective-permute-start.22 = (f32[256,256]{0,1:T(8,128)S(1)}, f32[256,256]{0,1:T(8,128)S(1)}, u32[]{:S(2)}, u32[]{:S(2)}) collective-permute-start(f32[256,256]{0,1:T(8,128)S(1)} %add.189), channel_id=1, source_target_pairs={{0,64},{16,80},{32,96},{48,112},{64,0},{80,16},{96,32},{112,48},{1... | collective-permute-start | bytes 786440 | tf_op jit(solution)/shard_map/ppermute | solution.py:18
  185.0 24.2 %collective-permute-start.23 = (f32[256,256]{0,1:T(8,128)S(1)}, f32[256,256]{0,1:T(8,128)S(1)}, u32[]{:S(2)}, u32[]{:S(2)}) collective-permute-start(f32[256,256]{0,1:T(8,128)S(1)} %add.190), channel_id=1, source_target_pairs={{0,128},{16,144},{32,160},{48,176},{64,192},{80,208},{96,224},{112... | collective-permute-start | bytes 786440 | tf_op jit(solution)/shard_map/ppermute | solution.py:18
  197.8 30.0 %collective-permute-start.18 = (f32[512,256]{1,0:T(8,128)S(1)}, f32[512,256]{1,0:T(8,128)S(1)}, u32[]{:S(2)}, u32[]{:S(2)}) collective-permute-start(f32[512,256]{1,0:T(8,128)S(1)} %add.184), channel_id=1, source_target_pairs={{0,64},{16,80},{32,96},{48,112},{64,0},{80,16},{96,32},{112,48},{1... | collective-permute-start | bytes 1572872 | tf_op jit(solution)/shard_map/ppermute | solution.py:18
  227.9 25.1 %collective-permute-start.19 = (f32[512,256]{1,0:T(8,128)S(1)}, f32[512,256]{1,0:T(8,128)S(1)}, u32[]{:S(2)}, u32[]{:S(2)}) collective-permute-start(f32[512,256]{1,0:T(8,128)S(1)} %add.185), channel_id=1, source_target_pairs={{0,128},{16,144},{32,160},{48,176},{64,192},{80,208},{96,224},{112... | collective-permute-start | bytes 1572872 | tf_op jit(solution)/shard_map/ppermute | solution.py:18
  263.0 12.9 %collective-permute-start.29 = (f32[256,256]{0,1:T(8,128)S(1)}, f32[256,256]{0,1:T(8,128)S(1)}, u32[]{:S(2)}, u32[]{:S(2)}) collective-permute-start(f32[256,256]{0,1:T(8,128)S(1)} %add.203), channel_id=1, source_target_pairs={{0,2},{1,3},{2,0},{3,1},{4,6},{5,7},{6,4},{7,5},{8,10},{9,11},{10,... | collective-permute-start | bytes 786440 | tf_op jit(solution)/shard_map/ppermute | solution.py:18
  264.1 24.6 %collective-permute-start.24 = (f32[512,256]{1,0:T(8,128)S(1)}, f32[512,256]{1,0:T(8,128)S(1)}, u32[]{:S(2)}, u32[]{:S(2)}) collective-permute-start(f32[512,256]{1,0:T(8,128)S(1)} %fusion.103), channel_id=1, source_target_pairs={{0,1},{1,0},{2,3},{3,2},{4,5},{5,4},{6,7},{7,6},{8,9},{9,8},{10,11... | collective-permute-start | bytes 1572872 | tf_op jit(solution)/shard_map/ppermute | solution.py:18
  288.7 22.4 %collective-permute-start.25 = (f32[512,256]{1,0:T(8,128)S(1)}, f32[512,256]{1,0:T(8,128)}, u32[]{:S(2)}, u32[]{:S(2)}) collective-permute-start(f32[512,256]{1,0:T(8,128)S(1)} %add.197), channel_id=1, source_target_pairs={{0,2},{1,3},{2,0},{3,1},{4,6},{5,7},{6,4},{7,5},{8,10},{9,11},{10,... | collective-permute-start | bytes 1572872 | tf_op jit(solution)/shard_map/ppermute | solution.py:18
  312.2 12.4 %collective-permute-start.26 = (f32[512,256]{1,0:T(8,128)S(1)}, f32[512,256]{1,0:T(8,128)S(1)}, u32[]{:S(2)}, u32[]{:S(2)}) collective-permute-start(f32[512,256]{1,0:T(8,128)S(1)} %add.198), channel_id=1, source_target_pairs={{0,4},{1,5},{2,6},{3,7},{4,0},{5,1},{6,2},{7,3},{8,12},{9,13},{10,... | collective-permute-start | bytes 1572872 | tf_op jit(solution)/shard_map/ppermute | solution.py:18
  324.7 13.0 %collective-permute-start.27 = (f32[512,256]{1,0:T(8,128)S(1)}, f32[512,256]{1,0:T(8,128)S(1)}, u32[]{:S(2)}, u32[]{:S(2)}) collective-permute-start(f32[512,256]{1,0:T(8,128)S(1)} %add.199), channel_id=1, source_target_pairs={{0,8},{1,9},{2,10},{3,11},{4,12},{5,13},{6,14},{7,15},{8,0},{9,1},... | collective-permute-start | bytes 1572872 | tf_op jit(solution)/shard_map/ppermute | solution.py:18
  344.2 17.8 %collective-permute-start.32 = (f32[512,256]{1,0:T(8,128)S(1)}, f32[512,256]{1,0:T(8,128)S(1)}, u32[]{:S(2)}, u32[]{:S(2)}) collective-permute-start(f32[512,256]{1,0:T(8,128)S(1)} %fusion.122), channel_id=1, source_target_pairs={{0,16},{16,0},{32,48},{48,32},{64,80},{80,64},{96,112},{112,96},{1... | collective-permute-start | bytes 1572872 | tf_op jit(solution)/shard_map/ppermute | solution.py:18
  359.8 13.6 %collective-permute-start.39 = (f32[256,256]{0,1:T(8,128)S(1)}, f32[256,256]{0,1:T(8,128)S(1)}, u32[]{:S(2)}, u32[]{:S(2)}) collective-permute-start(f32[256,256]{0,1:T(8,128)S(1)} %add.217), channel_id=1, source_target_pairs={{0,128},{16,144},{32,160},{48,176},{64,192},{80,208},{96,224},{112... | collective-permute-start | bytes 786440 | tf_op jit(solution)/shard_map/ppermute | solution.py:18
  362.0 28.1 %collective-permute-start.33 = (f32[512,256]{1,0:T(8,128)S(1)}, f32[512,256]{1,0:T(8,128)S(1)}, u32[]{:S(2)}, u32[]{:S(2)}) collective-permute-start(f32[512,256]{1,0:T(8,128)S(1)} %add.209), channel_id=1, source_target_pairs={{0,32},{16,48},{32,0},{48,16},{64,96},{80,112},{96,64},{112,80},{1... | collective-permute-start | bytes 1572872 | tf_op jit(solution)/shard_map/ppermute | solution.py:18
  390.2 13.3 %collective-permute-start.34 = (f32[512,256]{1,0:T(8,128)S(1)}, f32[512,256]{1,0:T(8,128)S(1)}, u32[]{:S(2)}, u32[]{:S(2)}) collective-permute-start(f32[512,256]{1,0:T(8,128)S(1)} %add.210), channel_id=1, source_target_pairs={{0,64},{16,80},{32,96},{48,112},{64,0},{80,16},{96,32},{112,48},{1... | collective-permute-start | bytes 1572872 | tf_op jit(solution)/shard_map/ppermute | solution.py:18
  403.6 21.5 %collective-permute-start.35 = (f32[512,256]{1,0:T(8,128)S(1)}, f32[512,256]{1,0:T(8,128)S(1)}, u32[]{:S(2)}, u32[]{:S(2)}) collective-permute-start(f32[512,256]{1,0:T(8,128)S(1)} %add.211), channel_id=1, source_target_pairs={{0,128},{16,144},{32,160},{48,176},{64,192},{80,208},{96,224},{112... | collective-permute-start | bytes 1572872 | tf_op jit(solution)/shard_map/ppermute | solution.py:18
  (27 other events, 297.6 us)

commit v2 on v1

--- a/solution.py
+++ b/solution.py
@@ -8,26 +8,26 @@
 ALL = ("doc", "word")
 
 
-def partners(axis, bit):
-    return [(i, i ^ bit) for i in range(lax.axis_size(axis))]
+def joined_along(pieces, dim):
+    pieces = jnp.moveaxis(pieces, 0, dim)
+    dims = pieces.shape
+    return pieces.reshape(*dims[:dim], dims[dim] * dims[dim + 1], *dims[dim + 2 :])
 
 
-def exchanged_sum(x, axis):
-    bit = 1
-    while bit < lax.axis_size(axis):
-        x = x + lax.ppermute(x, axis, partners(axis, bit))
-        bit *= 2
-    return x
+def gathered_copies(x, axis):
+    count = lax.axis_size(axis)
+    pieces = lax.all_to_all(jnp.broadcast_to(x[None], (count, *x.shape)), axis, 0, 0, tiled=True)
+    return joined_along(pieces, 0)
 
 
-def exchanged_gather(x, axis):
-    me = lax.axis_index(axis)
-    bit = 1
-    while bit < lax.axis_size(axis):
-        other = lax.ppermute(x, axis, partners(axis, bit))
-        x = jnp.where((me & bit) == 0, jnp.concatenate([x, other]), jnp.concatenate([other, x]))
-        bit *= 2
-    return x
+def summed_on_arrival(x, axis):
+    count = lax.axis_size(axis)
+    pieces = lax.all_to_all(x.reshape(count, x.shape[0] // count, *x.shape[1:]), axis, 0, 0, tiled=True)
+    return jnp.sum(pieces, axis=0)
+
+
+def summed_everywhere(x, axis):
+    return gathered_copies(summed_on_arrival(x, axis), axis)
 
 
 def own_rows(tile, axis, rows):
@@ -71,22 +71,24 @@
 def per_device(counts, topics, latent, dual_latent, doc_plus, topic_plus, dual_doc, dual_topic):
     counts_float = counts.astype(jnp.float32)
     rows, k = topics.shape
-    topic_side = exchanged_gather(jnp.concatenate([topics, topic_plus, dual_topic], axis=1), "doc")
+    topic_side = gathered_copies(jnp.concatenate([topics, topic_plus, dual_topic], axis=1), "doc")
     topic_tile, topic_plus_tile, dual_topic_tile = (topic_side[:, i * k : (i + 1) * k] for i in range(3))
-    doc_side = exchanged_gather(jnp.concatenate([doc_plus, dual_doc], axis=1), "word")
+    doc_side = gathered_copies(jnp.concatenate([doc_plus, dual_doc], axis=1), "word")
     doc_plus_tile, dual_doc_tile = doc_side[:, :k], doc_side[:, k:]
-    gram_topic = exchanged_sum(product_left(topic_tile, topic_tile), "word")
     for iteration in range(ITERS):
         merged = latent + dual_latent
-        inverse_topic = invert(gram_topic)
-        doc_rhs_tile = exchanged_sum(product(merged, topic_tile), "word") + doc_plus_tile - dual_doc_tile
+        word_summed = summed_everywhere(
+            jnp.concatenate([product(merged, topic_tile), product_left(topic_tile, topic_tile)]), "word"
+        )
+        doc_rhs_tile = word_summed[: merged.shape[0]] + doc_plus_tile - dual_doc_tile
+        inverse_topic = invert(word_summed[merged.shape[0] :])
         doc_tile = product(doc_rhs_tile, inverse_topic)
-        gram_doc = exchanged_sum(product_left(doc_tile, doc_tile), "doc")
-        inverse_doc = invert(gram_doc)
-        topic_rhs_tile = exchanged_sum(product_left(merged, doc_tile), "doc") + topic_plus_tile - dual_topic_tile
+        doc_summed = summed_everywhere(
+            jnp.concatenate([product_left(merged, doc_tile), product_left(doc_tile, doc_tile)]), "doc"
+        )
+        topic_rhs_tile = doc_summed[: merged.shape[1]] + topic_plus_tile - dual_topic_tile
+        inverse_doc = invert(doc_summed[merged.shape[1] :])
         topic_tile = product(topic_rhs_tile, inverse_doc)
-        if iteration + 1 < ITERS:
-            gram_topic = exchanged_sum(product_left(topic_tile, topic_tile), "word")
         rebuilt = product_right(doc_tile, topic_tile)
         shifted = rebuilt - dual_latent - 1.0
         latent = 0.5 * (shifted + jnp.sqrt(shifted * shifted + 4.0 * counts_float))

time: 440 us -> 386 us (0.88)
  the two profiles are of different devices: /device:TPU:96 before, /device:TPU:65 now
where the time goes in v2:
time: 386 us; the launch traced here: 380 us
  blocking collectives  165 us (43%)
  waiting for transfers between devices  88.9 us (23%)
  matrix products  81.3 us (21%)
  starting transfers between devices  26.9 us (7%)
  other arithmetic  7.92 us (2%)
  between operations  4.99 us (1%)
  local copies, waits for them, and re-layouts  4.62 us (1%)
    all_to_all x4, blocking collectives, summed_on_arrival(): lax.all_to_all(x.reshape(count, x.shape[0] // count, *x.shape[1:]), axis,...  114 us
    all_to_all x4, waiting for transfers between devices, gathered_copies(): lax.all_to_all(jnp.broadcast_to(x[None], (count, *x.shape)), axis, 0, 0,...  88.9 us
    dot_general x150, matrix products, product(): jnp.dot(left, right, precision=lax.Precision.HIGHEST, preferred_element_t...  67.7 us
    all_to_all x2, blocking collectives, gathered_copies(): lax.all_to_all(jnp.broadcast_to(x[None], (count, *x.shape)), axis, 0, 0,...  51.1 us
    all_to_all x4, starting transfers between devices, gathered_copies(): lax.all_to_all(jnp.broadcast_to(x[None], (count, *x.shape)), axis, 0, 0,...  26.9 us
  transfers between devices with their start and end apart: 4, of which 4 were waited for; matrix products, arithmetic and copies ran while one was open for 5% of the time, Pallas kernels for 0%

profile of v2, /device:TPU:65, one launch (start us, length us, event | category | flops | bytes accessed | tf_op | source)
XLA Modules:
  0.0 379.7 jit_solution(2786581990958360956)
XLA Ops:
  2.7 9.8 %all-to-all-start = ((f32[16,32,768]{2,1,0:T(8,128)}), f32[16,32,768]{2,1,0:T(8,128)S(1)}, u32[]{:S(2)}, u32[]{:S(2)}) async-start(f32[16,32,768]{2,1,0:T(8,128)} %broadcast_in_dim.12), calls=%async_computation | async-start | bytes 3145728 | tf_op jit(solution)/shard_map/all_to_all | solution.py:19
  12.6 1.7 add.76
  14.3 40.3 %all-to-all-done = f32[16,32,768]{2,1,0:T(8,128)S(1)} async-done(((f32[16,32,768]{2,1,0:T(8,128)}), f32[16,32,768]{2,1,0:T(8,128)S(1)}, u32[]{:S(2)}, u32[]{:S(2)}) %all-to-all-start) | async-done | bytes 1572896 | tf_op jit(solution)/shard_map/all_to_all | solution.py:19
  56.7 25.7 %all_to_all.50 = f32[16,48,256]{2,1,0:T(8,128)S(1)} all-to-all(f32[16,48,256]{2,1,0:T(8,128)S(1)} %bitcast.323), channel_id=1, replica_groups=mesh['doc'=16,'word'=16] {'word'}, dimensions={0} | all-to-all | bytes 1572864 | tf_op jit(solution)/shard_map/all_to_all | solution.py:25
  83.4 5.5 %all-to-all-start.2 = ((f32[16,48,256]{2,1,0:T(8,128)}), f32[16,48,256]{2,1,0:T(8,128)S(1)}, u32[]{:S(2)}, u32[]{:S(2)}) async-start(f32[16,48,256]{2,1,0:T(8,128)} %broadcast_in_dim.13), calls=%async_computation.2 | async-start | bytes 1572864 | tf_op jit(solution)/shard_map/all_to_all | solution.py:19
  88.9 18.4 %all-to-all-done.2 = f32[16,48,256]{2,1,0:T(8,128)S(1)} async-done(((f32[16,48,256]{2,1,0:T(8,128)}), f32[16,48,256]{2,1,0:T(8,128)S(1)}, u32[]{:S(2)}, u32[]{:S(2)}) %all-to-all-start.2) | async-done | bytes 786464 | tf_op jit(solution)/shard_map/all_to_all | solution.py:19
  108.5 7.2 %all-to-all-start.3 = ((f32[16,32,512]{2,1,0:T(8,128)}), f32[16,32,512]{2,1,0:T(8,128)}, u32[]{:S(2)}, u32[]{:S(2)}) async-start(f32[16,32,512]{2,1,0:T(8,128)} %broadcast_in_dim.14), calls=%async_computation.3 | async-start | bytes 2097152 | tf_op jit(solution)/shard_map/all_to_all | solution.py:19
  131.8 7.6 %all-to-all-done.3 = f32[16,32,512]{2,1,0:T(8,128)} async-done(((f32[16,32,512]{2,1,0:T(8,128)}), f32[16,32,512]{2,1,0:T(8,128)}, u32[]{:S(2)}, u32[]{:S(2)}) %all-to-all-start.3) | async-done | bytes 1048608 | tf_op jit(solution)/shard_map/all_to_all | solution.py:19
  139.4 1.8 fusion.14
  141.2 1.8 fusion.84
  144.1 22.6 %all_to_all.51 = f32[16,48,256]{2,1,0:T(8,128)S(1)} all-to-all(f32[16,48,256]{2,1,0:T(8,128)S(1)} %bitcast.324), channel_id=1, replica_groups=mesh['doc'=16,'word'=16] {'doc'}, dimensions={0} | all-to-all | bytes 1572864 | tf_op jit(solution)/shard_map/all_to_all | solution.py:25
  166.8 26.6 %all_to_all.52 = f32[16,48,256]{2,1,0:T(8,128)S(1)} all-to-all(f32[16,48,256]{2,1,0:T(8,128)S(1)} %broadcast_in_dim.15), channel_id=1, replica_groups=mesh['doc'=16,'word'=16] {'doc'}, dimensions={0} | all-to-all | bytes 1572864 | tf_op jit(solution)/shard_map/all_to_all | solution.py:19
  209.3 1.9 fusion.10
  212.3 2.6 fusion
  215.9 33.8 %all_to_all.53 = f32[16,48,256]{2,1,0:T(8,128)S(1)} all-to-all(f32[16,48,256]{2,1,0:T(8,128)S(1)} %bitcast.325), channel_id=1, replica_groups=mesh['doc'=16,'word'=16] {'word'}, dimensions={0} | all-to-all | bytes 1572864 | tf_op jit(solution)/shard_map/all_to_all | solution.py:25
  249.8 24.5 %all_to_all.54 = f32[16,48,256]{2,1,0:T(8,128)S(1)} all-to-all(f32[16,48,256]{2,1,0:T(8,128)S(1)} %broadcast_in_dim.16), channel_id=1, replica_groups=mesh['doc'=16,'word'=16] {'word'}, dimensions={0} | all-to-all | bytes 1572864 | tf_op jit(solution)/shard_map/all_to_all | solution.py:19
  290.4 3.0 broadcast_maximum_fusion.1
  293.4 1.8 fusion.122
  296.3 31.9 %all_to_all.55 = f32[16,48,256]{2,1,0:T(8,128)S(1)} all-to-all(f32[16,48,256]{2,1,0:T(8,128)S(1)} %bitcast.326), channel_id=1, replica_groups=mesh['doc'=16,'word'=16] {'doc'}, dimensions={0} | all-to-all | bytes 1572864 | tf_op jit(solution)/shard_map/all_to_all | solution.py:25
  329.2 4.4 %all-to-all-start.9 = ((f32[16,48,256]{2,1,0:T(8,128)}), f32[16,48,256]{2,1,0:T(8,128)S(1)}, u32[]{:S(2)}, u32[]{:S(2)}) async-start(f32[16,48,256]{2,1,0:T(8,128)} %broadcast_in_dim.17), calls=%async_computation.9 | async-start | bytes 1572864 | tf_op jit(solution)/shard_map/all_to_all | solution.py:19
  333.5 1.4 dynamic-slice_subtract_fusion.1
  335.0 22.6 %all-to-all-done.9 = f32[16,48,256]{2,1,0:T(8,128)S(1)} async-done(((f32[16,48,256]{2,1,0:T(8,128)}), f32[16,48,256]{2,1,0:T(8,128)S(1)}, u32[]{:S(2)}, u32[]{:S(2)}) %all-to-all-start.9) | async-done | bytes 786464 | tf_op jit(solution)/shard_map/all_to_all | solution.py:19
  373.4 2.0 broadcast_maximum_fusion
  375.6 3.3 add_subtract_fusion
  (191 shorter events, 72.5 us)
Async XLA Ops:
  2.7 51.9 %all-to-all-start = ((f32[16,32,768]{2,1,0:T(8,128)}), f32[16,32,768]{2,1,0:T(8,128)S(1)}, u32[]{:S(2)}, u32[]{:S(2)}) async-start(f32[16,32,768]{2,1,0:T(8,128)} %broadcast_in_dim.12), calls=%async_computation | async-start | bytes 3145728 | tf_op jit(solution)/shard_map/all_to_all | solution.py:19
  54.6 2.1 copy-start
  82.4 6.5 %copy-start.6 = (f32[32,256]{1,0:T(8,128)S(1)}, f32[32,256]{1,0:T(8,128)}, u32[]{:S(2)}) copy-start(f32[32,256]{1,0:T(8,128)} %param.14) | copy-start | bytes 98308
  82.4 6.5 %copy-start.7 = (f32[32,256]{1,0:T(8,128)S(1)}, f32[32,256]{1,0:T(8,128)}, u32[]{:S(2)}) copy-start(f32[32,256]{1,0:T(8,128)} %param.12) | copy-start | bytes 98308
  83.4 24.0 %all-to-all-start.2 = ((f32[16,48,256]{2,1,0:T(8,128)}), f32[16,48,256]{2,1,0:T(8,128)S(1)}, u32[]{:S(2)}, u32[]{:S(2)}) async-start(f32[16,48,256]{2,1,0:T(8,128)} %broadcast_in_dim.13), calls=%async_computation.2 | async-start | bytes 1572864 | tf_op jit(solution)/shard_map/all_to_all | solution.py:19
  108.5 30.9 %all-to-all-start.3 = ((f32[16,32,512]{2,1,0:T(8,128)}), f32[16,32,512]{2,1,0:T(8,128)}, u32[]{:S(2)}, u32[]{:S(2)}) async-start(f32[16,32,512]{2,1,0:T(8,128)} %broadcast_in_dim.14), calls=%async_computation.3 | async-start | bytes 2097152 | tf_op jit(solution)/shard_map/all_to_all | solution.py:19
  209.3 3.0 copy-start.1
  209.3 3.0 copy-start.3
  329.2 28.4 %all-to-all-start.9 = ((f32[16,48,256]{2,1,0:T(8,128)}), f32[16,48,256]{2,1,0:T(8,128)S(1)}, u32[]{:S(2)}, u32[]{:S(2)}) async-start(f32[16,48,256]{2,1,0:T(8,128)} %broadcast_in_dim.17), calls=%async_computation.9 | async-start | bytes 1572864 | tf_op jit(solution)/shard_map/all_to_all | solution.py:19
  373.4 2.0 copy-start.2
  373.4 2.0 copy-start.4
  373.4 2.2 copy-start.5

commit v3 on v0

--- a/solution.py
+++ b/solution.py
@@ -75,9 +75,10 @@
     matrix = gram + identity_mat
     row_bound = jnp.max(jnp.sum(jnp.abs(matrix), axis=1))
     approx = identity_mat / row_bound
-    for newton_step in range(NEWTON):
-        approx = product(approx, 2.0 * identity_mat - product(matrix, approx))
-    return approx
+    def newton_step(step, approx):
+        return product(approx, 2.0 * identity_mat - product(matrix, approx))
+
+    return lax.fori_loop(0, NEWTON, newton_step, approx)
 
 
 def gather_topics(topics):

time: 354 us -> 373 us (1.054)
  matrix products: 77.3 us -> 95.2 us
  blocking collectives: 183 us -> 174 us
  waiting for transfers between devices: 29.6 us -> 33.8 us
    dot_general x150, matrix products: 61.8 us -> 79 us  [product(): jnp.dot(left, right, precision=lax.Precision.HIGHEST, preferred_element_t...]
    all_to_all x4 -> x3, blocking collectives: 64.1 us -> 52.3 us  [summed_on_arrival(): pieces = lax.all_to_all(split_up(x, dim, count), axis, 0, 0, tiled=True)]
    all_to_all x4 -> x5, waiting for transfers between devices: 4.18 us -> 8.4 us  [summed_on_arrival(): pieces = lax.all_to_all(split_up(x, dim, count), axis, 0, 0, tiled=True)]
    all_to_all x4 -> x5, starting transfers between devices: 21 us -> 24.4 us  [summed_on_arrival(): pieces = lax.all_to_all(split_up(x, dim, count), axis, 0, 0, tiled=True)]
  transfers between devices with their start and end apart: 8 -> 9, of which waited for: 6 -> 5; matrix products, arithmetic and copies ran while one was open for 22% -> 26% of each run, Pallas kernels for 0% -> 0%
where the time goes in v3:
time: 373 us; the launch traced here: 371 us
  blocking collectives  174 us (47%)
  matrix products  95.2 us (26%)
  starting transfers between devices  44.4 us (12%)
  waiting for transfers between devices  33.8 us (9%)
  local copies, waits for them, and re-layouts  11.7 us (3%)
  other arithmetic  5.03 us (1%)
  between operations  3.82 us (1%)
    all_to_all x5, blocking collectives, copy_for_each(): lax.all_to_all(jnp.broadcast_to(x[None], (count, *x.shape)), axis, 0, 0,...  122 us
    dot_general x150, matrix products, product(): jnp.dot(left, right, precision=lax.Precision.HIGHEST, preferred_element_t...  79 us
    all_to_all x3, blocking collectives, summed_on_arrival(): pieces = lax.all_to_all(split_up(x, dim, count), axis, 0, 0, tiled=True)  52.3 us
    all_to_all x4, waiting for transfers between devices, copy_for_each(): lax.all_to_all(jnp.broadcast_to(x[None], (count, *x.shape)), axis, 0, 0,...  25.4 us
    all_to_all x5, starting transfers between devices, summed_on_arrival(): pieces = lax.all_to_all(split_up(x, dim, count), axis, 0, 0, tiled=True)  24.4 us
    all_to_all x4, starting transfers between devices, copy_for_each(): lax.all_to_all(jnp.broadcast_to(x[None], (count, *x.shape)), axis, 0, 0,...  20.1 us
    dot_general x6, matrix products, product_left(): lax.dot_general(left, right, (((0,), (0,)), ((), ())), precision=lax.Prec...  9.07 us
    all_to_all x5, waiting for transfers between devices, summed_on_arrival(): pieces = lax.all_to_all(split_up(x, dim, count), axis, 0, 0, tiled=True)  8.4 us
  transfers between devices with their start and end apart: 9, of which 5 were waited for; matrix products, arithmetic and copies ran while one was open for 26% of the time, Pallas kernels for 0%

profile of v3, /device:TPU:65, one launch (start us, length us, event | category | flops | bytes accessed | tf_op | source)
XLA Modules:
  0.0 371.2 jit_solution(12449514931443033917)
XLA Ops:
  1.4 28.9 %all_to_all.85 = f32[16,32,256]{2,1,0:T(8,128)S(1)} all-to-all(f32[16,32,256]{2,1,0:T(8,128)S(1)} %broadcast_in_dim.18), channel_id=1, replica_groups=mesh['doc'=16,'word'=16] {'doc'}, dimensions={0} | all-to-all | bytes 1048576 | tf_op jit(solution)/shard_map/all_to_all | solution.py:18
  31.2 13.9 %all_to_all.86 = f32[16,16,256]{2,1,0:T(8,128)S(1)} all-to-all(f32[16,16,256]{2,1,0:T(8,128)S(1)} %fusion.44), channel_id=1, replica_groups=mesh['doc'=16,'word'=16] {'word'}, dimensions={0} | all-to-all | bytes 524288 | tf_op jit(solution)/shard_map/all_to_all | solution.py:33
  45.8 5.9 %all-to-all-start.3 = ((f32[16,16,256]{2,1,0:T(8,128)}), f32[16,16,256]{2,1,0:T(8,128)S(1)}, u32[]{:S(2)}, u32[]{:S(2)}) async-start(f32[16,16,256]{2,1,0:T(8,128)} %broadcast_in_dim.19), calls=%async_computation.3 | async-start | bytes 524288 | tf_op jit(solution)/shard_map/all_to_all | solution.py:18
  54.9 4.1 %all-to-all-done.3 = f32[16,16,256]{2,1,0:T(8,128)S(1)} async-done(((f32[16,16,256]{2,1,0:T(8,128)}), f32[16,16,256]{2,1,0:T(8,128)S(1)}, u32[]{:S(2)}, u32[]{:S(2)}) %all-to-all-start.3) | async-done | bytes 262176 | tf_op jit(solution)/shard_map/all_to_all | solution.py:18
  59.0 6.1 %all-to-all-start.1 = ((f32[16,32,256]{2,1,0:T(8,128)}), f32[16,32,256]{2,1,0:T(8,128)S(1)}, u32[]{:S(2)}, u32[]{:S(2)}) async-start(f32[16,32,256]{2,1,0:T(8,128)} %fusion.43), calls=%async_computation.1 | async-start | bytes 1048576 | tf_op jit(solution)/shard_map/all_to_all | solution.py:33
  66.8 19.2 %while.44 = (s32[]{:T(128)}, f32[256,256]{0,1:T(8,128)S(1)}, f32[256,256]{1,0:T(8,128)S(1)}, s32[]{:T(128)}) while((s32[]{:T(128)}, f32[256,256]{0,1:T(8,128)S(1)}, f32[256,256]{1,0:T(8,128)S(1)}, s32[]{:T(128)}) %tuple.95), condition=%wide.region_5.6_spmd.clone, body=%wide.region_4.5_spmd.clone.sunk | while | flops 402849792 | bytes 2097205 | solution.py:81
  87.2 19.4 %all_to_all.87 = f32[16,32,256]{2,1,0:T(8,128)S(1)} all-to-all(f32[16,32,256]{2,1,0:T(8,128)S(1)} %broadcast_in_dim.20), channel_id=1, replica_groups=mesh['doc'=16,'word'=16] {'word'}, dimensions={0} | all-to-all | bytes 1048576 | tf_op jit(solution)/shard_map/all_to_all | solution.py:18
  107.4 19.6 %all_to_all.88 = f32[16,16,256]{2,1,0:T(8,128)S(1)} all-to-all(f32[16,16,256]{2,1,0:T(8,128)S(1)} %fusion.46), channel_id=1, replica_groups=mesh['doc'=16,'word'=16] {'doc'}, dimensions={0} | all-to-all | bytes 524288 | tf_op jit(solution)/shard_map/all_to_all | solution.py:33
  127.8 4.5 %all-to-all-start.7 = ((f32[16,16,256]{2,1,0:T(8,128)}), f32[16,16,256]{2,1,0:T(8,128)S(1)}, u32[]{:S(2)}, u32[]{:S(2)}) async-start(f32[16,16,256]{2,1,0:T(8,128)} %broadcast_in_dim.21), calls=%async_computation.7 | async-start | bytes 524288 | tf_op jit(solution)/shard_map/all_to_all | solution.py:18
  136.6 9.6 %all-to-all-done.7 = f32[16,16,256]{2,1,0:T(8,128)S(1)} async-done(((f32[16,16,256]{2,1,0:T(8,128)}), f32[16,16,256]{2,1,0:T(8,128)S(1)}, u32[]{:S(2)}, u32[]{:S(2)}) %all-to-all-start.7) | async-done | bytes 262176 | tf_op jit(solution)/shard_map/all_to_all | solution.py:18
  146.2 4.4 %all-to-all-start.5 = ((f32[16,32,256]{2,1,0:T(8,128)}), f32[16,32,256]{2,1,0:T(8,128)S(1)}, u32[]{:S(2)}, u32[]{:S(2)}) async-start(f32[16,32,256]{2,1,0:T(8,128)} %fusion.45), calls=%async_computation.5 | async-start | bytes 1048576 | tf_op jit(solution)/shard_map/all_to_all | solution.py:33
  152.3 19.2 %while.45 = (s32[]{:T(128)}, f32[256,256]{0,1:T(8,128)S(1)}, f32[256,256]{1,0:T(8,128)S(1)}, s32[]{:T(128)}) while((s32[]{:T(128)}, f32[256,256]{0,1:T(8,128)S(1)}, f32[256,256]{1,0:T(8,128)S(1)}, s32[]{:T(128)}) %tuple.98), condition=%wide.region_11.12_spmd.clone, body=%wide.region_10.11_spmd.clone.sunk | while | flops 402849792 | bytes 2097205 | solution.py:81
  172.7 27.2 %all_to_all.89 = f32[16,32,256]{2,1,0:T(8,128)S(1)} all-to-all(f32[16,32,256]{2,1,0:T(8,128)S(1)} %broadcast_in_dim.22), channel_id=1, replica_groups=mesh['doc'=16,'word'=16] {'doc'}, dimensions={0} | all-to-all | bytes 1048576 | tf_op jit(solution)/shard_map/all_to_all | solution.py:18
  205.1 8.4 %all-to-all-done.10 = f32[16,16,256]{2,1,0:T(8,128)S(1)} async-done(((f32[16,16,256]{2,1,0:T(8,128)}), f32[16,16,256]{2,1,0:T(8,128)S(1)}, u32[]{:S(2)}, u32[]{:S(2)}) %all-to-all-start.10) | async-done | bytes 262176 | tf_op jit(solution)/shard_map/all_to_all | solution.py:33
  214.2 5.2 %all-to-all-start.11 = ((f32[16,16,256]{2,1,0:T(8,128)}), f32[16,16,256]{2,1,0:T(8,128)S(1)}, u32[]{:S(2)}, u32[]{:S(2)}) async-start(f32[16,16,256]{2,1,0:T(8,128)} %broadcast_in_dim.23), calls=%async_computation.11 | async-start | bytes 524288 | tf_op jit(solution)/shard_map/all_to_all | solution.py:18
  227.1 5.9 %all-to-all-start.9 = ((f32[16,32,256]{2,1,0:T(8,128)}), f32[16,32,256]{2,1,0:T(8,128)S(1)}, u32[]{:S(2)}, u32[]{:S(2)}) async-start(f32[16,32,256]{2,1,0:T(8,128)} %fusion.47), calls=%async_computation.9 | async-start | bytes 1048576 | tf_op jit(solution)/shard_map/all_to_all | solution.py:33
  234.7 19.2 %while.46 = (s32[]{:T(128)}, f32[256,256]{0,1:T(8,128)S(1)}, f32[256,256]{1,0:T(8,128)S(1)}, s32[]{:T(128)}) while((s32[]{:T(128)}, f32[256,256]{0,1:T(8,128)S(1)}, f32[256,256]{1,0:T(8,128)S(1)}, s32[]{:T(128)}) %tuple.101), condition=%wide.region_17.18_spmd.clone, body=%wide.region_16.17_spmd.clone.sunk | while | flops 402849792 | bytes 2097205 | solution.py:81
  255.6 19.4 %all_to_all.90 = f32[16,32,256]{2,1,0:T(8,128)S(1)} all-to-all(f32[16,32,256]{2,1,0:T(8,128)S(1)} %broadcast_in_dim.24), channel_id=1, replica_groups=mesh['doc'=16,'word'=16] {'word'}, dimensions={0} | all-to-all | bytes 1048576 | tf_op jit(solution)/shard_map/all_to_all | solution.py:18
  275.8 18.8 %all_to_all.91 = f32[16,16,256]{2,1,0:T(8,128)S(1)} all-to-all(f32[16,16,256]{2,1,0:T(8,128)S(1)} %fusion.50), channel_id=1, replica_groups=mesh['doc'=16,'word'=16] {'doc'}, dimensions={0} | all-to-all | bytes 524288 | tf_op jit(solution)/shard_map/all_to_all | solution.py:33
  295.3 4.5 %all-to-all-start.15 = ((f32[16,16,256]{2,1,0:T(8,128)}), f32[16,16,256]{2,1,0:T(8,128)S(1)}, u32[]{:S(2)}, u32[]{:S(2)}) async-start(f32[16,16,256]{2,1,0:T(8,128)} %broadcast_in_dim.25), calls=%async_computation.15 | async-start | bytes 524288 | tf_op jit(solution)/shard_map/all_to_all | solution.py:18
  304.1 9.6 %all-to-all-done.15 = f32[16,16,256]{2,1,0:T(8,128)S(1)} async-done(((f32[16,16,256]{2,1,0:T(8,128)}), f32[16,16,256]{2,1,0:T(8,128)S(1)}, u32[]{:S(2)}, u32[]{:S(2)}) %all-to-all-start.15) | async-done | bytes 262176 | tf_op jit(solution)/shard_map/all_to_all | solution.py:18
  313.7 4.4 %all-to-all-start.13 = ((f32[16,32,256]{2,1,0:T(8,128)}), f32[16,32,256]{2,1,0:T(8,128)S(1)}, u32[]{:S(2)}, u32[]{:S(2)}) async-start(f32[16,32,256]{2,1,0:T(8,128)} %fusion.49), calls=%async_computation.13 | async-start | bytes 1048576 | tf_op jit(solution)/shard_map/all_to_all | solution.py:33
  319.8 19.2 %while.47 = (s32[]{:T(128)}, f32[256,256]{0,1:T(8,128)S(1)}, f32[256,256]{1,0:T(8,128)S(1)}, s32[]{:T(128)}) while((s32[]{:T(128)}, f32[256,256]{0,1:T(8,128)S(1)}, f32[256,256]{1,0:T(8,128)S(1)}, s32[]{:T(128)}) %tuple.104), condition=%wide.region_23.24_spmd.clone, body=%wide.region_22.23_spmd.clone.sunk | while | flops 402849792 | bytes 2097205 | solution.py:81
  340.7 27.2 %all_to_all.92 = f32[16,32,256]{2,1,0:T(8,128)S(1)} all-to-all(f32[16,32,256]{2,1,0:T(8,128)S(1)} %broadcast_in_dim.26), channel_id=1, replica_groups=mesh['doc'=16,'word'=16] {'doc'}, dimensions={0} | all-to-all | bytes 1048576 | tf_op jit(solution)/shard_map/all_to_all | solution.py:18
  (299 shorter events, 117.7 us)
Async XLA Ops:
  31.2 20.5 %copy-start = (f32[512,512]{1,0:T(8,128)S(1)}, f32[512,512]{1,0:T(8,128)}, u32[]{:S(2)}) copy-start(f32[512,512]{1,0:T(8,128)} %param.19) | copy-start | bytes 3145732
  45.8 13.2 %all-to-all-start.3 = ((f32[16,16,256]{2,1,0:T(8,128)}), f32[16,16,256]{2,1,0:T(8,128)S(1)}, u32[]{:S(2)}, u32[]{:S(2)}) async-start(f32[16,16,256]{2,1,0:T(8,128)} %broadcast_in_dim.19), calls=%async_computation.3 | async-start | bytes 524288 | tf_op jit(solution)/shard_map/all_to_all | solution.py:18
  59.0 27.0 %all-to-all-start.1 = ((f32[16,32,256]{2,1,0:T(8,128)}), f32[16,32,256]{2,1,0:T(8,128)S(1)}, u32[]{:S(2)}, u32[]{:S(2)}) async-start(f32[16,32,256]{2,1,0:T(8,128)} %fusion.43), calls=%async_computation.1 | async-start | bytes 1048576 | tf_op jit(solution)/shard_map/all_to_all | solution.py:33
  86.0 0.8 copy-start.3
  86.0 0.8 copy-start.7
  127.8 18.4 %all-to-all-start.7 = ((f32[16,16,256]{2,1,0:T(8,128)}), f32[16,16,256]{2,1,0:T(8,128)S(1)}, u32[]{:S(2)}, u32[]{:S(2)}) async-start(f32[16,16,256]{2,1,0:T(8,128)} %broadcast_in_dim.21), calls=%async_computation.7 | async-start | bytes 524288 | tf_op jit(solution)/shard_map/all_to_all | solution.py:18
  146.2 25.3 %all-to-all-start.5 = ((f32[16,32,256]{2,1,0:T(8,128)}), f32[16,32,256]{2,1,0:T(8,128)S(1)}, u32[]{:S(2)}, u32[]{:S(2)}) async-start(f32[16,32,256]{2,1,0:T(8,128)} %fusion.45), calls=%async_computation.5 | async-start | bytes 1048576 | tf_op jit(solution)/shard_map/all_to_all | solution.py:33
  171.5 0.8 copy-start.4
  171.5 0.8 copy-start.8
  201.4 12.0 %all-to-all-start.10 = ((f32[16,16,256]{2,1,0:T(8,128)}), f32[16,16,256]{2,1,0:T(8,128)S(1)}, u32[]{:S(2)}, u32[]{:S(2)}) async-start(f32[16,16,256]{2,1,0:T(8,128)} %fusion.48), calls=%async_computation.10 | async-start | bytes 524288 | tf_op jit(solution)/shard_map/all_to_all | solution.py:33
  214.2 12.9 %all-to-all-start.11 = ((f32[16,16,256]{2,1,0:T(8,128)}), f32[16,16,256]{2,1,0:T(8,128)S(1)}, u32[]{:S(2)}, u32[]{:S(2)}) async-start(f32[16,16,256]{2,1,0:T(8,128)} %broadcast_in_dim.23), calls=%async_computation.11 | async-start | bytes 524288 | tf_op jit(solution)/shard_map/all_to_all | solution.py:18
  227.1 26.8 %all-to-all-start.9 = ((f32[16,32,256]{2,1,0:T(8,128)}), f32[16,32,256]{2,1,0:T(8,128)S(1)}, u32[]{:S(2)}, u32[]{:S(2)}) async-start(f32[16,32,256]{2,1,0:T(8,128)} %fusion.47), calls=%async_computation.9 | async-start | bytes 1048576 | tf_op jit(solution)/shard_map/all_to_all | solution.py:33
  255.0 0.6 copy-start.5
  295.3 18.4 %all-to-all-start.15 = ((f32[16,16,256]{2,1,0:T(8,128)}), f32[16,16,256]{2,1,0:T(8,128)S(1)}, u32[]{:S(2)}, u32[]{:S(2)}) async-start(f32[16,16,256]{2,1,0:T(8,128)} %broadcast_in_dim.25), calls=%async_computation.15 | async-start | bytes 524288 | tf_op jit(solution)/shard_map/all_to_all | solution.py:18
  313.7 25.3 %all-to-all-start.13 = ((f32[16,32,256]{2,1,0:T(8,128)}), f32[16,32,256]{2,1,0:T(8,128)S(1)}, u32[]{:S(2)}, u32[]{:S(2)}) async-start(f32[16,32,256]{2,1,0:T(8,128)} %fusion.49), calls=%async_computation.13 | async-start | bytes 1048576 | tf_op jit(solution)/shard_map/all_to_all | solution.py:33
  339.0 28.9 %copy-start.2 = (f32[512,512]{1,0:T(8,128)S(1)}, f32[512,512]{1,0:T(8,128)}, u32[]{:S(2)}) copy-start(f32[512,512]{1,0:T(8,128)} %get-tuple-element.211) | copy-start | bytes 3145732
  339.1 28.8 %copy-start.1 = (s32[512,512]{1,0:T(8,128)S(1)}, s32[512,512]{1,0:T(8,128)}, u32[]{:S(2)}) copy-start(s32[512,512]{1,0:T(8,128)} %param.16) | copy-start | bytes 3145732
  340.1 0.6 copy-start.6

commit v4 on v0

--- a/solution.py
+++ b/solution.py
@@ -98,8 +98,11 @@
         doc_sums = summed_on_arrival(
             doc_term(jnp.int32(0), doc_plus.shape[0] * lax.axis_size("word")), "word", 0
         )
-        doc_factor = product(doc_sums + doc_plus - dual_doc, invert(gram_topic))
-        doc_tile = gathered_copies(doc_factor, "word", 0)
+        doc_rhs = doc_sums + doc_plus - dual_doc
+        doc_rhs_tile = gathered_copies(doc_rhs, "word", 0)
+        inverse_topic = invert(gram_topic)
+        doc_factor = product(doc_rhs, inverse_topic)
+        doc_tile = product(doc_rhs_tile, inverse_topic)
         gram_doc = nested_sum(product_left(doc_tile, doc_tile), "doc")
         inverse_doc = invert(gram_doc)
 
@@ -109,8 +112,10 @@
         word_sums = summed_on_arrival(
             word_term(jnp.int32(0), topics.shape[0] * lax.axis_size("doc")), "doc", 0
         )
-        topics = product(word_sums + topic_plus - dual_topic, inverse_doc)
-        topic_tile = gather_topics(topics)
+        topic_rhs = word_sums + topic_plus - dual_topic
+        topic_rhs_tile = gathered_copies(topic_rhs, "doc", 0)
+        topics = product(topic_rhs, inverse_doc)
+        topic_tile = product(topic_rhs_tile, inverse_doc)
         rebuilt = product_right(doc_tile, topic_tile)
         shifted = rebuilt - dual_latent - 1.0
         latent = 0.5 * (shifted + jnp.sqrt(shifted * shifted + 4.0 * counts_float))

time: 354 us -> 369 us (1.042)
  blocking collectives: 183 us -> 74.3 us
  waiting for transfers between devices: 29.6 us -> 114 us
  starting transfers between devices: 41.1 us -> 72.6 us
  matrix products: 77.3 us -> 83.2 us
    all_to_all x5 -> x1, blocking collectives: 119 us -> 28.9 us  [copy_for_each(): lax.all_to_all(jnp.broadcast_to(x[None], (count, *x.shape)), axis, 0, 0,...]
    all_to_all x4 -> x8, waiting for transfers between devices: 25.4 us -> 78.8 us  [copy_for_each(): lax.all_to_all(jnp.broadcast_to(x[None], (count, *x.shape)), axis, 0, 0,...]
    all_to_all x4 -> x5, waiting for transfers between devices: 4.18 us -> 34.9 us  [summed_on_arrival(): pieces = lax.all_to_all(split_up(x, dim, count), axis, 0, 0, tiled=True)]
    all_to_all x4 -> x8, starting transfers between devices: 20.1 us -> 44.8 us  [copy_for_each(): lax.all_to_all(jnp.broadcast_to(x[None], (count, *x.shape)), axis, 0, 0,...]
    all_to_all x4 -> x3, blocking collectives: 64.1 us -> 45.3 us  [summed_on_arrival(): pieces = lax.all_to_all(split_up(x, dim, count), axis, 0, 0, tiled=True)]
    all_to_all x4 -> x5, starting transfers between devices: 21 us -> 27.8 us  [summed_on_arrival(): pieces = lax.all_to_all(split_up(x, dim, count), axis, 0, 0, tiled=True)]
    dot_general x150 -> x154, matrix products: 61.8 us -> 65.3 us  [product(): jnp.dot(left, right, precision=lax.Precision.HIGHEST, preferred_element_t...]
  transfers between devices with their start and end apart: 8 -> 13, of which waited for: 6 -> 11; matrix products, arithmetic and copies ran while one was open for 22% -> 17% of each run, Pallas kernels for 0% -> 0%
where the time goes in v4:
time: 369 us; the launch traced here: 364 us
  waiting for transfers between devices  114 us (31%)
  matrix products  83.2 us (23%)
  blocking collectives  74.3 us (20%)
  starting transfers between devices  72.6 us (20%)
  local copies, waits for them, and re-layouts  8.95 us (2%)
  other arithmetic  6.06 us (2%)
  between operations  5.11 us (1%)
    all_to_all x8, waiting for transfers between devices, copy_for_each(): lax.all_to_all(jnp.broadcast_to(x[None], (count, *x.shape)), axis, 0, 0,...  78.8 us
    dot_general x154, matrix products, product(): jnp.dot(left, right, precision=lax.Precision.HIGHEST, preferred_element_t...  65.3 us
    all_to_all x3, blocking collectives, summed_on_arrival(): pieces = lax.all_to_all(split_up(x, dim, count), axis, 0, 0, tiled=True)  45.3 us
    all_to_all x8, starting transfers between devices, copy_for_each(): lax.all_to_all(jnp.broadcast_to(x[None], (count, *x.shape)), axis, 0, 0,...  44.8 us
    all_to_all x5, waiting for transfers between devices, summed_on_arrival(): pieces = lax.all_to_all(split_up(x, dim, count), axis, 0, 0, tiled=True)  34.9 us
    all_to_all x1, blocking collectives, copy_for_each(): lax.all_to_all(jnp.broadcast_to(x[None], (count, *x.shape)), axis, 0, 0,...  28.9 us
    all_to_all x5, starting transfers between devices, summed_on_arrival(): pieces = lax.all_to_all(split_up(x, dim, count), axis, 0, 0, tiled=True)  27.8 us
    dot_general x6, matrix products, product_left(): lax.dot_general(left, right, (((0,), (0,)), ((), ())), precision=lax.Prec...  9.56 us
  transfers between devices with their start and end apart: 13, of which 11 were waited for; matrix products, arithmetic and copies ran while one was open for 17% of the time, Pallas kernels for 0%

profile of v4, /device:TPU:65, one launch (start us, length us, event | category | flops | bytes accessed | tf_op | source)
XLA Modules:
  0.0 363.8 jit_solution(2907151741411385399)
XLA Ops:
  1.4 28.9 %all_to_all.85 = f32[16,32,256]{2,1,0:T(8,128)S(1)} all-to-all(f32[16,32,256]{2,1,0:T(8,128)S(1)} %broadcast_in_dim.18), channel_id=1, replica_groups=mesh['doc'=16,'word'=16] {'doc'}, dimensions={0} | all-to-all | bytes 1048576 | tf_op jit(solution)/shard_map/all_to_all | solution.py:18
  31.2 13.9 %all_to_all.86 = f32[16,16,256]{2,1,0:T(8,128)S(1)} all-to-all(f32[16,16,256]{2,1,0:T(8,128)S(1)} %fusion.52), channel_id=1, replica_groups=mesh['doc'=16,'word'=16] {'word'}, dimensions={0} | all-to-all | bytes 524288 | tf_op jit(solution)/shard_map/all_to_all | solution.py:33
  45.8 5.9 %all-to-all-start.4 = ((f32[16,16,256]{2,1,0:T(8,128)}), f32[16,16,256]{2,1,0:T(8,128)S(1)}, u32[]{:S(2)}, u32[]{:S(2)}) async-start(f32[16,16,256]{2,1,0:T(8,128)} %broadcast_in_dim.20), calls=%async_computation.4 | async-start | bytes 524288 | tf_op jit(solution)/shard_map/all_to_all | solution.py:18
  59.0 6.3 %all-to-all-start.1 = ((f32[16,32,256]{2,1,0:T(8,128)}), f32[16,32,256]{2,1,0:T(8,128)S(1)}, u32[]{:S(2)}, u32[]{:S(2)}) async-start(f32[16,32,256]{2,1,0:T(8,128)} %fusion.51), calls=%async_computation.1 | async-start | bytes 1048576 | tf_op jit(solution)/shard_map/all_to_all | solution.py:33
  80.5 7.4 %all-to-all-start.2 = ((f32[16,32,256]{2,1,0:T(8,128)}), f32[16,32,256]{2,1,0:T(8,128)S(1)}, u32[]{:S(2)}, u32[]{:S(2)}) async-start(f32[16,32,256]{2,1,0:T(8,128)} %broadcast_in_dim.19), calls=%async_computation.2 | async-start | bytes 1048576 | tf_op jit(solution)/shard_map/all_to_all | solution.py:18
  89.9 10.6 %all-to-all-done.2 = f32[16,32,256]{2,1,0:T(8,128)S(1)} async-done(((f32[16,32,256]{2,1,0:T(8,128)}), f32[16,32,256]{2,1,0:T(8,128)S(1)}, u32[]{:S(2)}, u32[]{:S(2)}) %all-to-all-start.2) | async-done | bytes 524320 | tf_op jit(solution)/shard_map/all_to_all | solution.py:18
  102.2 19.6 %all_to_all.87 = f32[16,16,256]{2,1,0:T(8,128)S(1)} all-to-all(f32[16,16,256]{2,1,0:T(8,128)S(1)} %bitcast.350), channel_id=1, replica_groups=mesh['doc'=16,'word'=16] {'doc'}, dimensions={0} | all-to-all | bytes 524288 | tf_op jit(solution)/shard_map/all_to_all | solution.py:33
  122.5 4.5 %all-to-all-start.8 = ((f32[16,16,256]{2,1,0:T(8,128)}), f32[16,16,256]{2,1,0:T(8,128)S(1)}, u32[]{:S(2)}, u32[]{:S(2)}) async-start(f32[16,16,256]{2,1,0:T(8,128)} %broadcast_in_dim.22), calls=%async_computation.8 | async-start | bytes 524288 | tf_op jit(solution)/shard_map/all_to_all | solution.py:18
  129.6 11.3 %all-to-all-done.8 = f32[16,16,256]{2,1,0:T(8,128)S(1)} async-done(((f32[16,16,256]{2,1,0:T(8,128)}), f32[16,16,256]{2,1,0:T(8,128)S(1)}, u32[]{:S(2)}, u32[]{:S(2)}) %all-to-all-start.8) | async-done | bytes 262176 | tf_op jit(solution)/shard_map/all_to_all | solution.py:18
  164.0 6.5 %all-to-all-start.6 = ((f32[16,32,256]{2,1,0:T(8,128)}), f32[16,32,256]{2,1,0:T(8,128)S(1)}, u32[]{:S(2)}, u32[]{:S(2)}) async-start(f32[16,32,256]{2,1,0:T(8,128)} %broadcast_in_dim.21), calls=%async_computation.6 | async-start | bytes 1048576 | tf_op jit(solution)/shard_map/all_to_all | solution.py:18
  172.4 15.7 %all-to-all-done.6 = f32[16,32,256]{2,1,0:T(8,128)S(1)} async-done(((f32[16,32,256]{2,1,0:T(8,128)}), f32[16,32,256]{2,1,0:T(8,128)S(1)}, u32[]{:S(2)}, u32[]{:S(2)}) %all-to-all-start.6) | async-done | bytes 524320 | tf_op jit(solution)/shard_map/all_to_all | solution.py:18
  189.7 11.8 %all_to_all.88 = f32[16,16,256]{2,1,0:T(8,128)S(1)} all-to-all(f32[16,16,256]{2,1,0:T(8,128)S(1)} %bitcast.351), channel_id=1, replica_groups=mesh['doc'=16,'word'=16] {'word'}, dimensions={0} | all-to-all | bytes 524288 | tf_op jit(solution)/shard_map/all_to_all | solution.py:33
  202.3 5.2 %all-to-all-start.11 = ((f32[16,16,256]{2,1,0:T(8,128)}), f32[16,16,256]{2,1,0:T(8,128)S(1)}, u32[]{:S(2)}, u32[]{:S(2)}) async-start(f32[16,16,256]{2,1,0:T(8,128)} %broadcast_in_dim.23), calls=%async_computation.11 | async-start | bytes 524288 | tf_op jit(solution)/shard_map/all_to_all | solution.py:18
  215.2 6.4 %all-to-all-start.9 = ((f32[16,32,256]{2,1,0:T(8,128)}), f32[16,32,256]{2,1,0:T(8,128)}, u32[]{:S(2)}, u32[]{:S(2)}) async-start(f32[16,32,256]{2,1,0:T(8,128)} %bitcast.12), calls=%async_computation.9 | async-start | bytes 1048576 | tf_op jit(solution)/shard_map/all_to_all | solution.py:33
  238.7 7.0 %all-to-all-start.12 = ((f32[16,32,256]{2,1,0:T(8,128)}), f32[16,32,256]{2,1,0:T(8,128)S(1)}, u32[]{:S(2)}, u32[]{:S(2)}) async-start(f32[16,32,256]{2,1,0:T(8,128)} %broadcast_in_dim.24), calls=%async_computation.12 | async-start | bytes 1048576 | tf_op jit(solution)/shard_map/all_to_all | solution.py:18
  248.6 9.4 %all-to-all-done.12 = f32[16,32,256]{2,1,0:T(8,128)S(1)} async-done(((f32[16,32,256]{2,1,0:T(8,128)}), f32[16,32,256]{2,1,0:T(8,128)S(1)}, u32[]{:S(2)}, u32[]{:S(2)}) %all-to-all-start.12) | async-done | bytes 524320 | tf_op jit(solution)/shard_map/all_to_all | solution.py:18
  260.3 6.1 %all-to-all-start.14 = ((f32[16,16,256]{2,1,0:T(8,128)}), f32[16,16,256]{2,1,0:T(8,128)S(1)}, u32[]{:S(2)}, u32[]{:S(2)}) async-start(f32[16,16,256]{2,1,0:T(8,128)} %bitcast.17), calls=%async_computation.14 | async-start | bytes 524288 | tf_op jit(solution)/shard_map/all_to_all | solution.py:33
  269.0 11.2 %all-to-all-done.14 = f32[16,16,256]{2,1,0:T(8,128)S(1)} async-done(((f32[16,16,256]{2,1,0:T(8,128)}), f32[16,16,256]{2,1,0:T(8,128)S(1)}, u32[]{:S(2)}, u32[]{:S(2)}) %all-to-all-start.14) | async-done | bytes 262176 | tf_op jit(solution)/shard_map/all_to_all | solution.py:33
  280.2 4.5 %all-to-all-start.13 = ((f32[16,32,256]{2,1,0:T(8,128)}), f32[16,32,256]{2,1,0:T(8,128)S(1)}, u32[]{:S(2)}, u32[]{:S(2)}) async-start(f32[16,32,256]{2,1,0:T(8,128)} %bitcast.16), calls=%async_computation.13 | async-start | bytes 1048576 | tf_op jit(solution)/shard_map/all_to_all | solution.py:33
  284.8 19.5 %all-to-all-done.13 = f32[16,32,256]{2,1,0:T(8,128)S(1)} async-done(((f32[16,32,256]{2,1,0:T(8,128)}), f32[16,32,256]{2,1,0:T(8,128)S(1)}, u32[]{:S(2)}, u32[]{:S(2)}) %all-to-all-start.13) | async-done | bytes 524320 | tf_op jit(solution)/shard_map/all_to_all | solution.py:33
  305.0 4.5 %all-to-all-start.15 = ((f32[16,16,256]{2,1,0:T(8,128)}), f32[16,16,256]{2,1,0:T(8,128)S(1)}, u32[]{:S(2)}, u32[]{:S(2)}) async-start(f32[16,16,256]{2,1,0:T(8,128)} %broadcast_in_dim.25), calls=%async_computation.15 | async-start | bytes 524288 | tf_op jit(solution)/shard_map/all_to_all | solution.py:18
  311.6 10.1 %all-to-all-done.15 = f32[16,16,256]{2,1,0:T(8,128)S(1)} async-done(((f32[16,16,256]{2,1,0:T(8,128)}), f32[16,16,256]{2,1,0:T(8,128)S(1)}, u32[]{:S(2)}, u32[]{:S(2)}) %all-to-all-start.15) | async-done | bytes 262176 | tf_op jit(solution)/shard_map/all_to_all | solution.py:18
  343.0 15.5 %all-to-all-done.16 = f32[16,32,256]{2,1,0:T(8,128)S(1)} async-done(((f32[16,32,256]{2,1,0:T(8,128)}), f32[16,32,256]{2,1,0:T(8,128)S(1)}, u32[]{:S(2)}, u32[]{:S(2)}) %all-to-all-start.16) | async-done | bytes 524320 | tf_op jit(solution)/shard_map/all_to_all | solution.py:18
  359.1 4.5 %add_subtract_fusion = (f32[512,512]{1,0:T(8,128)}, f32[512,512]{1,0:T(8,128)}) fusion(f32[512,512]{1,0:T(8,128)} %get-tuple-element.15, f32[512,512]{1,0:T(8,128)S(1)} %copy-done, s32[512,512]{1,0:T(8,128)S(1)} %copy-done.5, f32[512,256]{1,0:T(8,128)S(1)} %fusion.110, f32[512,256]{1,0:T(8,128)S(1)} %fusion.130), kind=kOutput, calls=%fused_computation.74 | convolution fusion | flops 810024960 | bytes 6291456 | tf_op jit(solution)/shard_map/dot_general | solution.py:64
  (226 shorter events, 112.2 us)
Async XLA Ops:
  31.2 20.5 %copy-start = (f32[512,512]{1,0:T(8,128)S(1)}, f32[512,512]{1,0:T(8,128)}, u32[]{:S(2)}) copy-start(f32[512,512]{1,0:T(8,128)} %param.11) | copy-start | bytes 3145732
  45.8 13.2 %all-to-all-start.4 = ((f32[16,16,256]{2,1,0:T(8,128)}), f32[16,16,256]{2,1,0:T(8,128)S(1)}, u32[]{:S(2)}, u32[]{:S(2)}) async-start(f32[16,16,256]{2,1,0:T(8,128)} %broadcast_in_dim.20), calls=%async_computation.4 | async-start | bytes 524288 | tf_op jit(solution)/shard_map/all_to_all | solution.py:18
  59.0 19.9 %all-to-all-start.1 = ((f32[16,32,256]{2,1,0:T(8,128)}), f32[16,32,256]{2,1,0:T(8,128)S(1)}, u32[]{:S(2)}, u32[]{:S(2)}) async-start(f32[16,32,256]{2,1,0:T(8,128)} %fusion.51), calls=%async_computation.1 | async-start | bytes 1048576 | tf_op jit(solution)/shard_map/all_to_all | solution.py:33
  78.9 0.8 copy-start.10
  80.5 20.0 %all-to-all-start.2 = ((f32[16,32,256]{2,1,0:T(8,128)}), f32[16,32,256]{2,1,0:T(8,128)S(1)}, u32[]{:S(2)}, u32[]{:S(2)}) async-start(f32[16,32,256]{2,1,0:T(8,128)} %broadcast_in_dim.19), calls=%async_computation.2 | async-start | bytes 1048576 | tf_op jit(solution)/shard_map/all_to_all | solution.py:18
  89.9 11.2 %copy-start.1 = (f32[256,256]{1,0:T(8,128)}, f32[256,256]{1,0:T(8,128)S(1)}, u32[]{:S(2)}) copy-start(f32[256,256]{1,0:T(8,128)S(1)} %fusion.69) | copy-start | bytes 786436
  122.5 18.4 %all-to-all-start.8 = ((f32[16,16,256]{2,1,0:T(8,128)}), f32[16,16,256]{2,1,0:T(8,128)S(1)}, u32[]{:S(2)}, u32[]{:S(2)}) async-start(f32[16,16,256]{2,1,0:T(8,128)} %broadcast_in_dim.22), calls=%async_computation.8 | async-start | bytes 524288 | tf_op jit(solution)/shard_map/all_to_all | solution.py:18
  140.9 22.1 %all-to-all-start.5 = ((f32[16,32,256]{2,1,0:T(8,128)}), f32[16,32,256]{2,1,0:T(8,128)S(1)}, u32[]{:S(2)}, u32[]{:S(2)}) async-start(f32[16,32,256]{2,1,0:T(8,128)} %bitcast.8), calls=%async_computation.5 | async-start | bytes 1048576 | tf_op jit(solution)/shard_map/all_to_all | solution.py:33
  158.9 4.2 %copy-start.7 = (f32[32,256]{1,0:T(8,128)S(1)}, f32[32,256]{1,0:T(8,128)}, u32[]{:S(2)}) copy-start(f32[32,256]{1,0:T(8,128)} %param.15) | copy-start | bytes 98308
  158.9 4.2 %copy-start.11 = (f32[32,256]{1,0:T(8,128)S(1)}, f32[32,256]{1,0:T(8,128)}, u32[]{:S(2)}) copy-start(f32[32,256]{1,0:T(8,128)} %param.13) | copy-start | bytes 98308
  164.0 24.1 %all-to-all-start.6 = ((f32[16,32,256]{2,1,0:T(8,128)}), f32[16,32,256]{2,1,0:T(8,128)S(1)}, u32[]{:S(2)}, u32[]{:S(2)}) async-start(f32[16,32,256]{2,1,0:T(8,128)} %broadcast_in_dim.21), calls=%async_computation.6 | async-start | bytes 1048576 | tf_op jit(solution)/shard_map/all_to_all | solution.py:18
  172.4 16.2 %copy-start.3 = (f32[256,256]{1,0:T(8,128)}, f32[256,256]{1,0:T(8,128)S(1)}, u32[]{:S(2)}) copy-start(f32[256,256]{1,0:T(8,128)S(1)} %fusion.89) | copy-start | bytes 786436
  202.3 12.9 %all-to-all-start.11 = ((f32[16,16,256]{2,1,0:T(8,128)}), f32[16,16,256]{2,1,0:T(8,128)S(1)}, u32[]{:S(2)}, u32[]{:S(2)}) async-start(f32[16,16,256]{2,1,0:T(8,128)} %broadcast_in_dim.23), calls=%async_computation.11 | async-start | bytes 524288 | tf_op jit(solution)/shard_map/all_to_all | solution.py:18
  215.2 20.7 %all-to-all-start.9 = ((f32[16,32,256]{2,1,0:T(8,128)}), f32[16,32,256]{2,1,0:T(8,128)}, u32[]{:S(2)}, u32[]{:S(2)}) async-start(f32[16,32,256]{2,1,0:T(8,128)} %bitcast.12), calls=%async_computation.9 | async-start | bytes 1048576 | tf_op jit(solution)/shard_map/all_to_all | solution.py:33
  235.9 1.1 copy-start.2
  238.7 19.3 %all-to-all-start.12 = ((f32[16,32,256]{2,1,0:T(8,128)}), f32[16,32,256]{2,1,0:T(8,128)S(1)}, u32[]{:S(2)}, u32[]{:S(2)}) async-start(f32[16,32,256]{2,1,0:T(8,128)} %broadcast_in_dim.24), calls=%async_computation.12 | async-start | bytes 1048576 | tf_op jit(solution)/shard_map/all_to_all | solution.py:18
  260.3 19.9 %all-to-all-start.14 = ((f32[16,16,256]{2,1,0:T(8,128)}), f32[16,16,256]{2,1,0:T(8,128)S(1)}, u32[]{:S(2)}, u32[]{:S(2)}) async-start(f32[16,16,256]{2,1,0:T(8,128)} %bitcast.17), calls=%async_computation.14 | async-start | bytes 524288 | tf_op jit(solution)/shard_map/all_to_all | solution.py:33
  280.2 24.0 %all-to-all-start.13 = ((f32[16,32,256]{2,1,0:T(8,128)}), f32[16,32,256]{2,1,0:T(8,128)S(1)}, u32[]{:S(2)}, u32[]{:S(2)}) async-start(f32[16,32,256]{2,1,0:T(8,128)} %bitcast.16), calls=%async_computation.13 | async-start | bytes 1048576 | tf_op jit(solution)/shard_map/all_to_all | solution.py:33
  305.0 4.5 %copy-start.9 = (f32[32,256]{1,0:T(8,128)S(1)}, f32[32,256]{1,0:T(8,128)}, u32[]{:S(2)}) copy-start(f32[32,256]{1,0:T(8,128)} %get-tuple-element.17) | copy-start | bytes 98308
  305.0 16.7 %all-to-all-start.15 = ((f32[16,16,256]{2,1,0:T(8,128)}), f32[16,16,256]{2,1,0:T(8,128)S(1)}, u32[]{:S(2)}, u32[]{:S(2)}) async-start(f32[16,16,256]{2,1,0:T(8,128)} %broadcast_in_dim.25), calls=%async_computation.15 | async-start | bytes 524288 | tf_op jit(solution)/shard_map/all_to_all | solution.py:18
  310.4 0.9 copy-start.4
  310.4 1.0 copy-start.8
  336.7 21.8 %all-to-all-start.16 = ((f32[16,32,256]{2,1,0:T(8,128)}), f32[16,32,256]{2,1,0:T(8,128)S(1)}, u32[]{:S(2)}, u32[]{:S(2)}) async-start(f32[16,32,256]{2,1,0:T(8,128)} %broadcast_in_dim.26), calls=%async_computation.16 | async-start | bytes 1048576 | tf_op jit(solution)/shard_map/all_to_all | solution.py:18
  342.1 17.0 %copy-start.5 = (s32[512,512]{1,0:T(8,128)S(1)}, s32[512,512]{1,0:T(8,128)}, u32[]{:S(2)}) copy-start(s32[512,512]{1,0:T(8,128)} %param.8) | copy-start | bytes 3145732
  (1 other events, 0.8 us)

commit v5 on v4

--- a/solution.py
+++ b/solution.py
@@ -46,6 +46,15 @@
     return whole[: len(lines)].reshape(x.shape)
 
 
+def exchanged_sum(x, axis):
+    count = lax.axis_size(axis)
+    bit = 1
+    while bit < count:
+        x = x + lax.ppermute(x, axis, [(i, i ^ bit) for i in range(count)])
+        bit *= 2
+    return x
+
+
 def product(left, right):
     return jnp.dot(left, right, precision=lax.Precision.HIGHEST, preferred_element_type=jnp.float32)
 
@@ -90,7 +99,7 @@
     topic_tile = gather_topics(topics)
     for iteration in range(ITERS):
         merged = latent + dual_latent
-        gram_topic = nested_sum(product_left(topic_tile, topic_tile), "word")
+        gram_topic = exchanged_sum(product_left(topic_tile, topic_tile), "word")
 
         def doc_term(first_row, row_count, merged=merged, topic_tile=topic_tile):
             return product(merged, topic_tile)
@@ -103,7 +112,7 @@
         inverse_topic = invert(gram_topic)
         doc_factor = product(doc_rhs, inverse_topic)
         doc_tile = product(doc_rhs_tile, inverse_topic)
-        gram_doc = nested_sum(product_left(doc_tile, doc_tile), "doc")
+        gram_doc = exchanged_sum(product_left(doc_tile, doc_tile), "doc")
         inverse_doc = invert(gram_doc)
 
         def word_term(first_row, row_count, merged=merged, doc_tile=doc_tile):

time: 369 us -> 345 us (0.935)
  the two profiles are of different devices: /device:TPU:65 before, /device:TPU:164 now
where the time goes in v5:
time: 345 us; the launch traced here: 339 us
  waiting for transfers between devices  122 us (35%)
  matrix products  100 us (29%)
  starting transfers between devices  96.3 us (28%)
  other arithmetic  8.4 us (2%)
  local copies, waits for them, and re-layouts  6.79 us (2%)
  between operations  5.03 us (1%)
    ppermute x16, waiting for transfers between devices, exchanged_sum(): x = x + lax.ppermute(x, axis, [(i, i ^ bit) for i in range(count)])  111 us
    dot_general x154, matrix products, product(): jnp.dot(left, right, precision=lax.Precision.HIGHEST, preferred_element_t...  81.8 us
    all_to_all x5, starting transfers between devices, copy_for_each(): lax.all_to_all(jnp.broadcast_to(x[None], (count, *x.shape)), axis, 0, 0,...  43.9 us
    all_to_all x4, starting transfers between devices, summed_on_arrival(): pieces = lax.all_to_all(split_up(x, dim, count), axis, 0, 0, tiled=True)  33.6 us
    ppermute x16, starting transfers between devices, exchanged_sum(): x = x + lax.ppermute(x, axis, [(i, i ^ bit) for i in range(count)])  18.8 us
    all_to_all x5, waiting for transfers between devices, copy_for_each(): lax.all_to_all(jnp.broadcast_to(x[None], (count, *x.shape)), axis, 0, 0,...  10.7 us
    dot_general x6, matrix products, product_left(): lax.dot_general(left, right, (((0,), (0,)), ((), ())), precision=lax.Prec...  9.89 us
    dot_general x2, matrix products, product_right(): lax.dot_general(left, right, (((1,), (1,)), ((), ())), precision=lax.Prec...  8.64 us
  transfers between devices with their start and end apart: 25, of which 14 were waited for; matrix products, arithmetic and copies ran while one was open for 28% of the time, Pallas kernels for 0%

profile of v5, /device:TPU:164, one launch (start us, length us, event | category | flops | bytes accessed | tf_op | source)
XLA Modules:
  0.0 338.9 jit_solution(628428899609671434)
XLA Ops:
  2.3 9.6 %all-to-all-start = ((f32[16,32,256]{2,1,0:T(8,128)}), f32[16,32,256]{2,1,0:T(8,128)S(1)}, u32[]{:S(2)}, u32[]{:S(2)}) async-start(f32[16,32,256]{2,1,0:T(8,128)} %broadcast_in_dim.10), calls=%async_computation | async-start | bytes 1048576 | tf_op jit(solution)/shard_map/all_to_all | solution.py:18
  13.4 10.7 %all-to-all-done = f32[16,32,256]{2,1,0:T(8,128)S(1)} async-done(((f32[16,32,256]{2,1,0:T(8,128)}), f32[16,32,256]{2,1,0:T(8,128)S(1)}, u32[]{:S(2)}, u32[]{:S(2)}) %all-to-all-start) | async-done | bytes 524320 | tf_op jit(solution)/shard_map/all_to_all | solution.py:18
  25.9 6.4 %all-to-all-start.1 = ((f32[16,32,256]{2,1,0:T(8,128)}), f32[16,32,256]{2,1,0:T(8,128)S(1)}, u32[]{:S(2)}, u32[]{:S(2)}) async-start(f32[16,32,256]{2,1,0:T(8,128)} %fusion.43), calls=%async_computation.1 | async-start | bytes 1048576 | tf_op jit(solution)/shard_map/all_to_all | solution.py:33
  33.5 14.0 %collective-permute-done = f32[256,256]{0,1:T(8,128)S(1)} collective-permute-done((f32[256,256]{0,1:T(8,128)S(1)}, f32[256,256]{0,1:T(8,128)S(1)}, u32[]{:S(2)}, u32[]{:S(2)}) %collective-permute-start) | collective-permute-done | bytes 262176 | tf_op jit(solution)/shard_map/ppermute | solution.py:53
  50.3 10.7 %collective-permute-done.1 = f32[256,256]{0,1:T(8,128)S(1)} collective-permute-done((f32[256,256]{0,1:T(8,128)S(1)}, f32[256,256]{0,1:T(8,128)S(1)}, u32[]{:S(2)}, u32[]{:S(2)}) %collective-permute-start.1) | collective-permute-done | bytes 262176 | tf_op jit(solution)/shard_map/ppermute | solution.py:53
  62.5 5.8 %collective-permute-done.2 = f32[256,256]{0,1:T(8,128)S(1)} collective-permute-done((f32[256,256]{0,1:T(8,128)S(1)}, f32[256,256]{0,1:T(8,128)S(1)}, u32[]{:S(2)}, u32[]{:S(2)}) %collective-permute-start.2) | collective-permute-done | bytes 262176 | tf_op jit(solution)/shard_map/ppermute | solution.py:53
  72.4 6.9 %all-to-all-start.2 = ((f32[16,32,256]{2,1,0:T(8,128)}), f32[16,32,256]{2,1,0:T(8,128)S(1)}, u32[]{:S(2)}, u32[]{:S(2)}) async-start(f32[16,32,256]{2,1,0:T(8,128)} %broadcast_in_dim.11), calls=%async_computation.2 | async-start | bytes 1048576 | tf_op jit(solution)/shard_map/all_to_all | solution.py:18
  102.6 11.0 %all-to-all-start.3 = ((f32[16,32,256]{2,1,0:T(8,128)}), f32[16,32,256]{2,1,0:T(8,128)S(1)}, u32[]{:S(2)}, u32[]{:S(2)}) async-start(f32[16,32,256]{2,1,0:T(8,128)} %bitcast.5), calls=%async_computation.3 | async-start | bytes 1048576 | tf_op jit(solution)/shard_map/all_to_all | solution.py:33
  117.5 9.6 %collective-permute-done.5 = f32[256,256]{0,1:T(8,128)S(1)} collective-permute-done((f32[256,256]{0,1:T(8,128)S(1)}, f32[256,256]{0,1:T(8,128)S(1)}, u32[]{:S(2)}, u32[]{:S(2)}) %collective-permute-start.5) | collective-permute-done | bytes 262176 | tf_op jit(solution)/shard_map/ppermute | solution.py:53
  127.8 9.3 %collective-permute-done.6 = f32[256,256]{0,1:T(8,128)S(1)} collective-permute-done((f32[256,256]{0,1:T(8,128)S(1)}, f32[256,256]{0,1:T(8,128)S(1)}, u32[]{:S(2)}, u32[]{:S(2)}) %collective-permute-start.6) | collective-permute-done | bytes 262176 | tf_op jit(solution)/shard_map/ppermute | solution.py:53
  138.7 9.8 %all-to-all-start.4 = ((f32[16,32,256]{2,1,0:T(8,128)}), f32[16,32,256]{2,1,0:T(8,128)S(1)}, u32[]{:S(2)}, u32[]{:S(2)}) async-start(f32[16,32,256]{2,1,0:T(8,128)} %broadcast_in_dim.12), calls=%async_computation.4 | async-start | bytes 1048576 | tf_op jit(solution)/shard_map/all_to_all | solution.py:18
  148.5 8.5 %collective-permute-done.7 = f32[256,256]{0,1:T(8,128)S(1)} collective-permute-done((f32[256,256]{0,1:T(8,128)S(1)}, f32[256,256]{0,1:T(8,128)S(1)}, u32[]{:S(2)}, u32[]{:S(2)}) %collective-permute-start.7) | collective-permute-done | bytes 262176 | tf_op jit(solution)/shard_map/ppermute | solution.py:53
  177.7 3.8 %fusion = (f32[512,512]{1,0:T(8,128)S(1)}, f32[512,512]{1,0:T(8,128)}) fusion(s32[512,512]{1,0:T(8,128)} %param.8, f32[512,512]{1,0:T(8,128)S(1)} %copy-done, f32[512,256]{1,0:T(8,128)S(1)} %fusion.61, f32[512,256]{1,0:T(8,128)S(1)} %fusion.81), kind=kOutput, calls=%fused_computation.84 | convolution fusion | flops 808189952 | bytes 5242880 | tf_op jit(solution)/shard_map/dot_general | solution.py:73
  183.2 6.4 %all-to-all-start.5 = ((f32[16,32,256]{2,1,0:T(8,128)}), f32[16,32,256]{2,1,0:T(8,128)S(1)}, u32[]{:S(2)}, u32[]{:S(2)}) async-start(f32[16,32,256]{2,1,0:T(8,128)} %bitcast.336), calls=%async_computation.5 | async-start | bytes 1048576 | tf_op jit(solution)/shard_map/all_to_all | solution.py:33
  190.8 9.9 %collective-permute-done.8 = f32[256,256]{0,1:T(8,128)S(1)} collective-permute-done((f32[256,256]{0,1:T(8,128)S(1)}, f32[256,256]{0,1:T(8,128)S(1)}, u32[]{:S(2)}, u32[]{:S(2)}) %collective-permute-start.8) | collective-permute-done | bytes 262176 | tf_op jit(solution)/shard_map/ppermute | solution.py:53
  203.8 6.7 %collective-permute-done.9 = f32[256,256]{0,1:T(8,128)S(1)} collective-permute-done((f32[256,256]{0,1:T(8,128)S(1)}, f32[256,256]{0,1:T(8,128)S(1)}, u32[]{:S(2)}, u32[]{:S(2)}) %collective-permute-start.9) | collective-permute-done | bytes 262176 | tf_op jit(solution)/shard_map/ppermute | solution.py:53
  212.2 6.6 %collective-permute-done.10 = f32[256,256]{0,1:T(8,128)S(1)} collective-permute-done((f32[256,256]{0,1:T(8,128)S(1)}, f32[256,256]{0,1:T(8,128)S(1)}, u32[]{:S(2)}, u32[]{:S(2)}) %collective-permute-start.10) | collective-permute-done | bytes 262176 | tf_op jit(solution)/shard_map/ppermute | solution.py:53
  223.5 7.3 %all-to-all-start.6 = ((f32[16,32,256]{2,1,0:T(8,128)}), f32[16,32,256]{2,1,0:T(8,128)S(1)}, u32[]{:S(2)}, u32[]{:S(2)}) async-start(f32[16,32,256]{2,1,0:T(8,128)} %broadcast_in_dim.13), calls=%async_computation.6 | async-start | bytes 1048576 | tf_op jit(solution)/shard_map/all_to_all | solution.py:18
  256.7 9.7 %all-to-all-start.7 = ((f32[16,32,256]{2,1,0:T(8,128)}), f32[16,32,256]{2,1,0:T(8,128)S(1)}, u32[]{:S(2)}, u32[]{:S(2)}) async-start(f32[16,32,256]{2,1,0:T(8,128)} %bitcast.335), calls=%async_computation.7 | async-start | bytes 1048576 | tf_op jit(solution)/shard_map/all_to_all | solution.py:33
  268.8 11.3 %collective-permute-done.13 = f32[256,256]{0,1:T(8,128)S(1)} collective-permute-done((f32[256,256]{0,1:T(8,128)S(1)}, f32[256,256]{0,1:T(8,128)S(1)}, u32[]{:S(2)}, u32[]{:S(2)}) %collective-permute-start.13) | collective-permute-done | bytes 262176 | tf_op jit(solution)/shard_map/ppermute | solution.py:53
  280.7 9.3 %collective-permute-done.14 = f32[256,256]{0,1:T(8,128)S(1)} collective-permute-done((f32[256,256]{0,1:T(8,128)S(1)}, f32[256,256]{0,1:T(8,128)S(1)}, u32[]{:S(2)}, u32[]{:S(2)}) %collective-permute-start.14) | collective-permute-done | bytes 262176 | tf_op jit(solution)/shard_map/ppermute | solution.py:53
  293.0 10.3 %all-to-all-start.8 = ((f32[16,32,256]{2,1,0:T(8,128)}), f32[16,32,256]{2,1,0:T(8,128)S(1)}, u32[]{:S(2)}, u32[]{:S(2)}) async-start(f32[16,32,256]{2,1,0:T(8,128)} %broadcast_in_dim.14), calls=%async_computation.8 | async-start | bytes 1048576 | tf_op jit(solution)/shard_map/all_to_all | solution.py:18
  303.4 8.3 %collective-permute-done.15 = f32[256,256]{0,1:T(8,128)} collective-permute-done((f32[256,256]{0,1:T(8,128)S(1)}, f32[256,256]{0,1:T(8,128)}, u32[]{:S(2)}, u32[]{:S(2)}) %collective-permute-start.15) | collective-permute-done | bytes 262176 | tf_op jit(solution)/shard_map/ppermute | solution.py:53
  333.8 4.9 %add_subtract_fusion = (f32[512,512]{1,0:T(8,128)}, f32[512,512]{1,0:T(8,128)}) fusion(f32[512,512]{1,0:T(8,128)} %get-tuple-element.23, f32[512,512]{1,0:T(8,128)S(1)} %copy-done, s32[512,512]{1,0:T(8,128)} %param.8, f32[512,256]{1,0:T(8,128)S(1)} %fusion.101, f32[512,256]{1,0:T(8,128)S(1)} %fusion.121), kind=kOutput, calls=%fused_computation.75 | convolution fusion | flops 810024960 | bytes 6291456 | tf_op jit(solution)/shard_map/dot_general | solution.py:73
  (242 shorter events, 127.1 us)
Async XLA Ops:
  2.3 21.8 %all-to-all-start = ((f32[16,32,256]{2,1,0:T(8,128)}), f32[16,32,256]{2,1,0:T(8,128)S(1)}, u32[]{:S(2)}, u32[]{:S(2)}) async-start(f32[16,32,256]{2,1,0:T(8,128)} %broadcast_in_dim.10), calls=%async_computation | async-start | bytes 1048576 | tf_op jit(solution)/shard_map/all_to_all | solution.py:18
  25.9 45.6 %all-to-all-start.1 = ((f32[16,32,256]{2,1,0:T(8,128)}), f32[16,32,256]{2,1,0:T(8,128)S(1)}, u32[]{:S(2)}, u32[]{:S(2)}) async-start(f32[16,32,256]{2,1,0:T(8,128)} %fusion.43), calls=%async_computation.1 | async-start | bytes 1048576 | tf_op jit(solution)/shard_map/all_to_all | solution.py:33
  33.3 14.2 %collective-permute-start = (f32[256,256]{0,1:T(8,128)S(1)}, f32[256,256]{0,1:T(8,128)S(1)}, u32[]{:S(2)}, u32[]{:S(2)}) collective-permute-start(f32[256,256]{0,1:T(8,128)S(1)} %convolution_bitcast_fusion), channel_id=1, source_target_pairs={{0,1},{1,0},{2,3},{3,2},{4,5},{5,4},{6,7},{7,6},{8,9},{9,8},{10,11... | collective-permute-start | bytes 786440 | tf_op jit(solution)/shard_map/ppermute | solution.py:53
  47.5 13.4 %collective-permute-start.1 = (f32[256,256]{0,1:T(8,128)S(1)}, f32[256,256]{0,1:T(8,128)S(1)}, u32[]{:S(2)}, u32[]{:S(2)}) collective-permute-start(f32[256,256]{0,1:T(8,128)S(1)} %add.116), channel_id=1, source_target_pairs={{0,2},{1,3},{2,0},{3,1},{4,6},{5,7},{6,4},{7,5},{8,10},{9,11},{10,... | collective-permute-start | bytes 786440 | tf_op jit(solution)/shard_map/ppermute | solution.py:53
  61.0 7.4 %collective-permute-start.2 = (f32[256,256]{0,1:T(8,128)S(1)}, f32[256,256]{0,1:T(8,128)S(1)}, u32[]{:S(2)}, u32[]{:S(2)}) collective-permute-start(f32[256,256]{0,1:T(8,128)S(1)} %add.117), channel_id=1, source_target_pairs={{0,4},{1,5},{2,6},{3,7},{4,0},{5,1},{6,2},{7,3},{8,12},{9,13},{10,... | collective-permute-start | bytes 786440 | tf_op jit(solution)/shard_map/ppermute | solution.py:53
  68.4 10.9 %collective-permute-start.3 = (f32[256,256]{0,1:T(8,128)S(1)}, f32[256,256]{0,1:T(8,128)S(1)}, u32[]{:S(2)}, u32[]{:S(2)}) collective-permute-start(f32[256,256]{0,1:T(8,128)S(1)} %add.118), channel_id=1, source_target_pairs={{0,8},{1,9},{2,10},{3,11},{4,12},{5,13},{6,14},{7,15},{8,0},{9,1},... | collective-permute-start | bytes 786440 | tf_op jit(solution)/shard_map/ppermute | solution.py:53
  72.4 26.9 %all-to-all-start.2 = ((f32[16,32,256]{2,1,0:T(8,128)}), f32[16,32,256]{2,1,0:T(8,128)S(1)}, u32[]{:S(2)}, u32[]{:S(2)}) async-start(f32[16,32,256]{2,1,0:T(8,128)} %broadcast_in_dim.11), calls=%async_computation.2 | async-start | bytes 1048576 | tf_op jit(solution)/shard_map/all_to_all | solution.py:18
  102.6 34.6 %all-to-all-start.3 = ((f32[16,32,256]{2,1,0:T(8,128)}), f32[16,32,256]{2,1,0:T(8,128)S(1)}, u32[]{:S(2)}, u32[]{:S(2)}) async-start(f32[16,32,256]{2,1,0:T(8,128)} %bitcast.5), calls=%async_computation.3 | async-start | bytes 1048576 | tf_op jit(solution)/shard_map/all_to_all | solution.py:33
  116.3 10.9 %collective-permute-start.5 = (f32[256,256]{0,1:T(8,128)S(1)}, f32[256,256]{0,1:T(8,128)S(1)}, u32[]{:S(2)}, u32[]{:S(2)}) collective-permute-start(f32[256,256]{0,1:T(8,128)S(1)} %add.122), channel_id=1, source_target_pairs={{0,32},{16,48},{32,0},{48,16},{64,96},{80,112},{96,64},{112,80},{1... | collective-permute-start | bytes 786440 | tf_op jit(solution)/shard_map/ppermute | solution.py:53
  127.2 9.9 %collective-permute-start.6 = (f32[256,256]{0,1:T(8,128)S(1)}, f32[256,256]{0,1:T(8,128)S(1)}, u32[]{:S(2)}, u32[]{:S(2)}) collective-permute-start(f32[256,256]{0,1:T(8,128)S(1)} %add.123), channel_id=1, source_target_pairs={{0,64},{16,80},{32,96},{48,112},{64,0},{80,16},{96,32},{112,48},{1... | collective-permute-start | bytes 786440 | tf_op jit(solution)/shard_map/ppermute | solution.py:53
  137.1 19.9 %collective-permute-start.7 = (f32[256,256]{0,1:T(8,128)S(1)}, f32[256,256]{0,1:T(8,128)S(1)}, u32[]{:S(2)}, u32[]{:S(2)}) collective-permute-start(f32[256,256]{0,1:T(8,128)S(1)} %add.124), channel_id=1, source_target_pairs={{0,128},{16,144},{32,160},{48,176},{64,192},{80,208},{96,224},{112... | collective-permute-start | bytes 786440 | tf_op jit(solution)/shard_map/ppermute | solution.py:53
  138.7 38.3 %all-to-all-start.4 = ((f32[16,32,256]{2,1,0:T(8,128)}), f32[16,32,256]{2,1,0:T(8,128)S(1)}, u32[]{:S(2)}, u32[]{:S(2)}) async-start(f32[16,32,256]{2,1,0:T(8,128)} %broadcast_in_dim.12), calls=%async_computation.4 | async-start | bytes 1048576 | tf_op jit(solution)/shard_map/all_to_all | solution.py:18
  183.2 38.5 %all-to-all-start.5 = ((f32[16,32,256]{2,1,0:T(8,128)}), f32[16,32,256]{2,1,0:T(8,128)S(1)}, u32[]{:S(2)}, u32[]{:S(2)}) async-start(f32[16,32,256]{2,1,0:T(8,128)} %bitcast.336), calls=%async_computation.5 | async-start | bytes 1048576 | tf_op jit(solution)/shard_map/all_to_all | solution.py:33
  190.7 10.1 %collective-permute-start.8 = (f32[256,256]{0,1:T(8,128)S(1)}, f32[256,256]{0,1:T(8,128)S(1)}, u32[]{:S(2)}, u32[]{:S(2)}) collective-permute-start(f32[256,256]{0,1:T(8,128)S(1)} %fusion.83), channel_id=1, source_target_pairs={{0,1},{1,0},{2,3},{3,2},{4,5},{5,4},{6,7},{7,6},{8,9},{9,8},{10,11... | collective-permute-start | bytes 786440 | tf_op jit(solution)/shard_map/ppermute | solution.py:53
  200.8 9.7 %collective-permute-start.9 = (f32[256,256]{0,1:T(8,128)S(1)}, f32[256,256]{0,1:T(8,128)S(1)}, u32[]{:S(2)}, u32[]{:S(2)}) collective-permute-start(f32[256,256]{0,1:T(8,128)S(1)} %add.133), channel_id=1, source_target_pairs={{0,2},{1,3},{2,0},{3,1},{4,6},{5,7},{6,4},{7,5},{8,10},{9,11},{10,... | collective-permute-start | bytes 786440 | tf_op jit(solution)/shard_map/ppermute | solution.py:53
  210.5 8.3 %collective-permute-start.10 = (f32[256,256]{0,1:T(8,128)S(1)}, f32[256,256]{0,1:T(8,128)S(1)}, u32[]{:S(2)}, u32[]{:S(2)}) collective-permute-start(f32[256,256]{0,1:T(8,128)S(1)} %add.134), channel_id=1, source_target_pairs={{0,4},{1,5},{2,6},{3,7},{4,0},{5,1},{6,2},{7,3},{8,12},{9,13},{10,... | collective-permute-start | bytes 786440 | tf_op jit(solution)/shard_map/ppermute | solution.py:53
  219.5 11.3 %collective-permute-start.11 = (f32[256,256]{0,1:T(8,128)}, f32[256,256]{0,1:T(8,128)}, u32[]{:S(2)}, u32[]{:S(2)}) collective-permute-start(f32[256,256]{0,1:T(8,128)} %add.135), channel_id=1, source_target_pairs={{0,8},{1,9},{2,10},{3,11},{4,12},{5,13},{6,14},{7,15},{8,0},{9,1},... | collective-permute-start | bytes 786440 | tf_op jit(solution)/shard_map/ppermute | solution.py:53
  223.5 28.3 %all-to-all-start.6 = ((f32[16,32,256]{2,1,0:T(8,128)}), f32[16,32,256]{2,1,0:T(8,128)S(1)}, u32[]{:S(2)}, u32[]{:S(2)}) async-start(f32[16,32,256]{2,1,0:T(8,128)} %broadcast_in_dim.13), calls=%async_computation.6 | async-start | bytes 1048576 | tf_op jit(solution)/shard_map/all_to_all | solution.py:18
  254.1 12.4 %collective-permute-start.12 = (f32[256,256]{0,1:T(8,128)}, f32[256,256]{0,1:T(8,128)}, u32[]{:S(2)}, u32[]{:S(2)}) collective-permute-start(f32[256,256]{0,1:T(8,128)} %fusion.103), channel_id=1, source_target_pairs={{0,16},{16,0},{32,48},{48,32},{64,80},{80,64},{96,112},{112,96},{1... | collective-permute-start | bytes 786440 | tf_op jit(solution)/shard_map/ppermute | solution.py:53
  256.7 34.3 %all-to-all-start.7 = ((f32[16,32,256]{2,1,0:T(8,128)}), f32[16,32,256]{2,1,0:T(8,128)S(1)}, u32[]{:S(2)}, u32[]{:S(2)}) async-start(f32[16,32,256]{2,1,0:T(8,128)} %bitcast.335), calls=%async_computation.7 | async-start | bytes 1048576 | tf_op jit(solution)/shard_map/all_to_all | solution.py:33
  267.5 12.5 %collective-permute-start.13 = (f32[256,256]{0,1:T(8,128)S(1)}, f32[256,256]{0,1:T(8,128)S(1)}, u32[]{:S(2)}, u32[]{:S(2)}) collective-permute-start(f32[256,256]{0,1:T(8,128)S(1)} %add.140), channel_id=1, source_target_pairs={{0,32},{16,48},{32,0},{48,16},{64,96},{80,112},{96,64},{112,80},{1... | collective-permute-start | bytes 786440 | tf_op jit(solution)/shard_map/ppermute | solution.py:53
  280.1 9.9 %collective-permute-start.14 = (f32[256,256]{0,1:T(8,128)S(1)}, f32[256,256]{0,1:T(8,128)S(1)}, u32[]{:S(2)}, u32[]{:S(2)}) collective-permute-start(f32[256,256]{0,1:T(8,128)S(1)} %add.141), channel_id=1, source_target_pairs={{0,64},{16,80},{32,96},{48,112},{64,0},{80,16},{96,32},{112,48},{1... | collective-permute-start | bytes 786440 | tf_op jit(solution)/shard_map/ppermute | solution.py:53
  290.0 21.6 %collective-permute-start.15 = (f32[256,256]{0,1:T(8,128)S(1)}, f32[256,256]{0,1:T(8,128)}, u32[]{:S(2)}, u32[]{:S(2)}) collective-permute-start(f32[256,256]{0,1:T(8,128)S(1)} %add.142), channel_id=1, source_target_pairs={{0,128},{16,144},{32,160},{48,176},{64,192},{80,208},{96,224},{112... | collective-permute-start | bytes 786440 | tf_op jit(solution)/shard_map/ppermute | solution.py:53
  293.0 40.2 %all-to-all-start.8 = ((f32[16,32,256]{2,1,0:T(8,128)}), f32[16,32,256]{2,1,0:T(8,128)S(1)}, u32[]{:S(2)}, u32[]{:S(2)}) async-start(f32[16,32,256]{2,1,0:T(8,128)} %broadcast_in_dim.14), calls=%async_computation.8 | async-start | bytes 1048576 | tf_op jit(solution)/shard_map/all_to_all | solution.py:18
  (12 other events, 36.3 us)

commit v6 on v5

--- a/solution.py
+++ b/solution.py
@@ -55,6 +55,14 @@
     return x
 
 
+def symmetric_sum(gram, axis):
+    half = gram.shape[0] // 2
+    upper = exchanged_sum(jnp.concatenate([gram[:half, :], gram[half:, half:]], axis=1), axis)
+    top = upper[:, : gram.shape[1]]
+    bottom = jnp.concatenate([top[:, half:].T, upper[:, gram.shape[1] :]], axis=1)
+    return jnp.concatenate([top, bottom], axis=0)
+
+
 def product(left, right):
     return jnp.dot(left, right, precision=lax.Precision.HIGHEST, preferred_element_type=jnp.float32)
 
@@ -99,7 +107,7 @@
     topic_tile = gather_topics(topics)
     for iteration in range(ITERS):
         merged = latent + dual_latent
-        gram_topic = exchanged_sum(product_left(topic_tile, topic_tile), "word")
+        gram_topic = symmetric_sum(product_left(topic_tile, topic_tile), "word")
 
         def doc_term(first_row, row_count, merged=merged, topic_tile=topic_tile):
             return product(merged, topic_tile)
@@ -112,7 +120,7 @@
         inverse_topic = invert(gram_topic)
         doc_factor = product(doc_rhs, inverse_topic)
         doc_tile = product(doc_rhs_tile, inverse_topic)
-        gram_doc = exchanged_sum(product_left(doc_tile, doc_tile), "doc")
+        gram_doc = symmetric_sum(product_left(doc_tile, doc_tile), "doc")
         inverse_doc = invert(gram_doc)
 
         def word_term(first_row, row_count, merged=merged, doc_tile=doc_tile):

time: 345 us -> 352 us (1.020)
  the two profiles are of different devices: /device:TPU:164 before, /device:TPU:65 now
where the time goes in v6:
time: 352 us; the launch traced here: 346 us
  waiting for transfers between devices  106 us (30%)
  matrix products  102 us (29%)
  starting transfers between devices  92 us (26%)
  blocking collectives  28.9 us (8%)
  other arithmetic  5.56 us (2%)
  local copies, waits for them, and re-layouts  5.44 us (2%)
  between operations  5.34 us (2%)
    dot_general x154, matrix products, product(): jnp.dot(left, right, precision=lax.Precision.HIGHEST, preferred_element_t...  85.5 us
    all_to_all x4, waiting for transfers between devices, copy_for_each(): lax.all_to_all(jnp.broadcast_to(x[None], (count, *x.shape)), axis, 0, 0,...  52 us
    ppermute x16, waiting for transfers between devices, exchanged_sum(): x = x + lax.ppermute(x, axis, [(i, i ^ bit) for i in range(count)])  51.9 us
    all_to_all x4, starting transfers between devices, summed_on_arrival(): pieces = lax.all_to_all(split_up(x, dim, count), axis, 0, 0, tiled=True)  37.9 us
    all_to_all x4, starting transfers between devices, copy_for_each(): lax.all_to_all(jnp.broadcast_to(x[None], (count, *x.shape)), axis, 0, 0,...  31.4 us
    all_to_all x1, blocking collectives, copy_for_each(): lax.all_to_all(jnp.broadcast_to(x[None], (count, *x.shape)), axis, 0, 0,...  28.9 us
    ppermute x16, starting transfers between devices, exchanged_sum(): x = x + lax.ppermute(x, axis, [(i, i ^ bit) for i in range(count)])  22.7 us
    dot_general x6, matrix products, product_left(): lax.dot_general(left, right, (((0,), (0,)), ((), ())), precision=lax.Prec...  9.2 us
  transfers between devices with their start and end apart: 24, of which 18 were waited for; matrix products, arithmetic and copies ran while one was open for 26% of the time, Pallas kernels for 0%

profile of v6, /device:TPU:65, one launch (start us, length us, event | category | flops | bytes accessed | tf_op | source)
XLA Modules:
  0.0 345.8 jit_solution(15093253382166108547)
XLA Ops:
  1.4 28.9 %all_to_all.45 = f32[16,32,256]{2,1,0:T(8,128)S(1)} all-to-all(f32[16,32,256]{2,1,0:T(8,128)S(1)} %broadcast_in_dim.10), channel_id=1, replica_groups=mesh['doc'=16,'word'=16] {'doc'}, dimensions={0} | all-to-all | bytes 1048576 | tf_op jit(solution)/shard_map/all_to_all | solution.py:18
  31.5 5.2 %collective-permute-done = f32[128,384]{0,1:T(8,128)S(1)} collective-permute-done((f32[128,384]{0,1:T(8,128)S(1)}, f32[128,384]{0,1:T(8,128)S(1)}, u32[]{:S(2)}, u32[]{:S(2)}) %collective-permute-start) | collective-permute-done | bytes 196640 | tf_op jit(solution)/shard_map/ppermute | solution.py:53
  37.6 7.9 %collective-permute-done.1 = f32[128,384]{0,1:T(8,128)S(1)} collective-permute-done((f32[128,384]{0,1:T(8,128)S(1)}, f32[128,384]{0,1:T(8,128)S(1)}, u32[]{:S(2)}, u32[]{:S(2)}) %collective-permute-start.1) | collective-permute-done | bytes 196640 | tf_op jit(solution)/shard_map/ppermute | solution.py:53
  47.1 3.4 collective-permute-done.2
  55.4 6.7 %all-to-all-start.1 = ((f32[16,32,256]{2,1,0:T(8,128)}), f32[16,32,256]{2,1,0:T(8,128)S(1)}, u32[]{:S(2)}, u32[]{:S(2)}) async-start(f32[16,32,256]{2,1,0:T(8,128)} %fusion.48), calls=%async_computation.1 | async-start | bytes 1048576 | tf_op jit(solution)/shard_map/all_to_all | solution.py:33
  81.6 7.0 %all-to-all-start.2 = ((f32[16,32,256]{2,1,0:T(8,128)}), f32[16,32,256]{2,1,0:T(8,128)}, u32[]{:S(2)}, u32[]{:S(2)}) async-start(f32[16,32,256]{2,1,0:T(8,128)} %broadcast_in_dim.11), calls=%async_computation.2 | async-start | bytes 1048576 | tf_op jit(solution)/shard_map/all_to_all | solution.py:18
  91.0 9.4 %all-to-all-done.2 = f32[16,32,256]{2,1,0:T(8,128)} async-done(((f32[16,32,256]{2,1,0:T(8,128)}), f32[16,32,256]{2,1,0:T(8,128)}, u32[]{:S(2)}, u32[]{:S(2)}) %all-to-all-start.2) | async-done | bytes 524320 | tf_op jit(solution)/shard_map/all_to_all | solution.py:18
  103.1 3.4 collective-permute-start.4
  108.9 4.9 %collective-permute-done.5 = f32[128,384]{0,1:T(8,128)S(1)} collective-permute-done((f32[128,384]{0,1:T(8,128)S(1)}, f32[128,384]{0,1:T(8,128)S(1)}, u32[]{:S(2)}, u32[]{:S(2)}) %collective-permute-start.5) | collective-permute-done | bytes 196640 | tf_op jit(solution)/shard_map/ppermute | solution.py:53
  116.7 4.0 %collective-permute-done.6 = f32[128,384]{0,1:T(8,128)S(1)} collective-permute-done((f32[128,384]{0,1:T(8,128)S(1)}, f32[128,384]{0,1:T(8,128)S(1)}, u32[]{:S(2)}, u32[]{:S(2)}) %collective-permute-start.6) | collective-permute-done | bytes 196640 | tf_op jit(solution)/shard_map/ppermute | solution.py:53
  123.7 11.8 %all-to-all-start.3 = ((f32[16,32,256]{2,1,0:T(8,128)}), f32[16,32,256]{2,1,0:T(8,128)S(1)}, u32[]{:S(2)}, u32[]{:S(2)}) async-start(f32[16,32,256]{2,1,0:T(8,128)} %bitcast.288), calls=%async_computation.3 | async-start | bytes 1048576 | tf_op jit(solution)/shard_map/all_to_all | solution.py:33
  155.6 9.0 %all-to-all-start.4 = ((f32[16,32,256]{2,1,0:T(8,128)}), f32[16,32,256]{2,1,0:T(8,128)S(1)}, u32[]{:S(2)}, u32[]{:S(2)}) async-start(f32[16,32,256]{2,1,0:T(8,128)} %broadcast_in_dim.12), calls=%async_computation.4 | async-start | bytes 1048576 | tf_op jit(solution)/shard_map/all_to_all | solution.py:18
  167.1 16.9 %all-to-all-done.4 = f32[16,32,256]{2,1,0:T(8,128)S(1)} async-done(((f32[16,32,256]{2,1,0:T(8,128)}), f32[16,32,256]{2,1,0:T(8,128)S(1)}, u32[]{:S(2)}, u32[]{:S(2)}) %all-to-all-start.4) | async-done | bytes 524320 | tf_op jit(solution)/shard_map/all_to_all | solution.py:18
  185.7 5.2 %collective-permute-done.8 = f32[128,384]{0,1:T(8,128)S(1)} collective-permute-done((f32[128,384]{0,1:T(8,128)S(1)}, f32[128,384]{0,1:T(8,128)S(1)}, u32[]{:S(2)}, u32[]{:S(2)}) %collective-permute-start.8) | collective-permute-done | bytes 196640 | tf_op jit(solution)/shard_map/ppermute | solution.py:53
  192.7 7.9 %collective-permute-done.9 = f32[128,384]{0,1:T(8,128)S(1)} collective-permute-done((f32[128,384]{0,1:T(8,128)S(1)}, f32[128,384]{0,1:T(8,128)S(1)}, u32[]{:S(2)}, u32[]{:S(2)}) %collective-permute-start.9) | collective-permute-done | bytes 196640 | tf_op jit(solution)/shard_map/ppermute | solution.py:53
  207.9 8.0 %all-to-all-start.5 = ((f32[16,32,256]{2,1,0:T(8,128)}), f32[16,32,256]{2,1,0:T(8,128)}, u32[]{:S(2)}, u32[]{:S(2)}) async-start(f32[16,32,256]{2,1,0:T(8,128)} %bitcast.9), calls=%async_computation.5 | async-start | bytes 1048576 | tf_op jit(solution)/shard_map/all_to_all | solution.py:33
  237.2 7.0 %all-to-all-start.6 = ((f32[16,32,256]{2,1,0:T(8,128)}), f32[16,32,256]{2,1,0:T(8,128)}, u32[]{:S(2)}, u32[]{:S(2)}) async-start(f32[16,32,256]{2,1,0:T(8,128)} %broadcast_in_dim.13), calls=%async_computation.6 | async-start | bytes 1048576 | tf_op jit(solution)/shard_map/all_to_all | solution.py:18
  246.7 9.4 %all-to-all-done.6 = f32[16,32,256]{2,1,0:T(8,128)} async-done(((f32[16,32,256]{2,1,0:T(8,128)}), f32[16,32,256]{2,1,0:T(8,128)}, u32[]{:S(2)}, u32[]{:S(2)}) %all-to-all-start.6) | async-done | bytes 524320 | tf_op jit(solution)/shard_map/all_to_all | solution.py:18
  258.7 3.4 collective-permute-start.12
  264.0 5.5 %collective-permute-done.13 = f32[128,384]{0,1:T(8,128)S(1)} collective-permute-done((f32[128,384]{0,1:T(8,128)S(1)}, f32[128,384]{0,1:T(8,128)S(1)}, u32[]{:S(2)}, u32[]{:S(2)}) %collective-permute-start.13) | collective-permute-done | bytes 196640 | tf_op jit(solution)/shard_map/ppermute | solution.py:53
  279.3 11.5 %all-to-all-start.7 = ((f32[16,32,256]{2,1,0:T(8,128)}), f32[16,32,256]{2,1,0:T(8,128)}, u32[]{:S(2)}, u32[]{:S(2)}) async-start(f32[16,32,256]{2,1,0:T(8,128)} %bitcast.287), calls=%async_computation.7 | async-start | bytes 1048576 | tf_op jit(solution)/shard_map/all_to_all | solution.py:33
  312.3 8.5 %all-to-all-start.8 = ((f32[16,32,256]{2,1,0:T(8,128)}), f32[16,32,256]{2,1,0:T(8,128)S(1)}, u32[]{:S(2)}, u32[]{:S(2)}) async-start(f32[16,32,256]{2,1,0:T(8,128)} %broadcast_in_dim.14), calls=%async_computation.8 | async-start | bytes 1048576 | tf_op jit(solution)/shard_map/all_to_all | solution.py:18
  323.7 16.4 %all-to-all-done.8 = f32[16,32,256]{2,1,0:T(8,128)S(1)} async-done(((f32[16,32,256]{2,1,0:T(8,128)}), f32[16,32,256]{2,1,0:T(8,128)S(1)}, u32[]{:S(2)}, u32[]{:S(2)}) %all-to-all-start.8) | async-done | bytes 524320 | tf_op jit(solution)/shard_map/all_to_all | solution.py:18
  340.7 4.9 %add_subtract_fusion = (f32[512,512]{1,0:T(8,128)}, f32[512,512]{1,0:T(8,128)}) fusion(f32[512,512]{1,0:T(8,128)} %get-tuple-element.23, f32[512,512]{1,0:T(8,128)S(1)} %copy-done, s32[512,512]{1,0:T(8,128)} %param.8, f32[512,256]{1,0:T(8,128)S(1)} %fusion.106, f32[512,256]{1,0:T(8,128)S(1)} %fusion.126), kind=kOutput, calls=%fused_computation.75 | convolution fusion | flops 810024960 | bytes 6291456 | tf_op jit(solution)/shard_map/dot_general | solution.py:81
  (265 shorter events, 134.3 us)
Async XLA Ops:
  31.4 5.3 %collective-permute-start = (f32[128,384]{0,1:T(8,128)S(1)}, f32[128,384]{0,1:T(8,128)S(1)}, u32[]{:S(2)}, u32[]{:S(2)}) collective-permute-start(f32[128,384]{0,1:T(8,128)S(1)} %pad_maximum_fusion), channel_id=1, source_target_pairs={{0,1},{1,0},{2,3},{3,2},{4,5},{5,4},{6,7},{7,6},{8,9},{9,8},{10,11... | collective-permute-start | bytes 589832 | tf_op jit(solution)/shard_map/ppermute | solution.py:53
  36.8 8.7 %collective-permute-start.1 = (f32[128,384]{0,1:T(8,128)S(1)}, f32[128,384]{0,1:T(8,128)S(1)}, u32[]{:S(2)}, u32[]{:S(2)}) collective-permute-start(f32[128,384]{0,1:T(8,128)S(1)} %fusion.46), channel_id=1, source_target_pairs={{0,2},{1,3},{2,0},{3,1},{4,6},{5,7},{6,4},{7,5},{8,10},{9,11},{10,... | collective-permute-start | bytes 589832 | tf_op jit(solution)/shard_map/ppermute | solution.py:53
  45.5 5.0 %collective-permute-start.2 = (f32[128,384]{0,1:T(8,128)S(1)}, f32[128,384]{0,1:T(8,128)S(1)}, u32[]{:S(2)}, u32[]{:S(2)}) collective-permute-start(f32[128,384]{0,1:T(8,128)S(1)} %add.117), channel_id=1, source_target_pairs={{0,4},{1,5},{2,6},{3,7},{4,0},{5,1},{6,2},{7,3},{8,12},{9,13},{10,... | collective-permute-start | bytes 589832 | tf_op jit(solution)/shard_map/ppermute | solution.py:53
  50.6 11.5 %collective-permute-start.3 = (f32[128,384]{0,1:T(8,128)S(1)}, f32[128,384]{0,1:T(8,128)S(1)}, u32[]{:S(2)}, u32[]{:S(2)}) collective-permute-start(f32[128,384]{0,1:T(8,128)S(1)} %add.118), channel_id=1, source_target_pairs={{0,8},{1,9},{2,10},{3,11},{4,12},{5,13},{6,14},{7,15},{8,0},{9,1},... | collective-permute-start | bytes 589832 | tf_op jit(solution)/shard_map/ppermute | solution.py:53
  55.4 24.6 %all-to-all-start.1 = ((f32[16,32,256]{2,1,0:T(8,128)}), f32[16,32,256]{2,1,0:T(8,128)S(1)}, u32[]{:S(2)}, u32[]{:S(2)}) async-start(f32[16,32,256]{2,1,0:T(8,128)} %fusion.48), calls=%async_computation.1 | async-start | bytes 1048576 | tf_op jit(solution)/shard_map/all_to_all | solution.py:33
  81.6 18.8 %all-to-all-start.2 = ((f32[16,32,256]{2,1,0:T(8,128)}), f32[16,32,256]{2,1,0:T(8,128)}, u32[]{:S(2)}, u32[]{:S(2)}) async-start(f32[16,32,256]{2,1,0:T(8,128)} %broadcast_in_dim.11), calls=%async_computation.2 | async-start | bytes 1048576 | tf_op jit(solution)/shard_map/all_to_all | solution.py:18
  103.1 4.5 %collective-permute-start.4 = (f32[128,384]{0,1:T(8,128)S(1)}, f32[128,384]{0,1:T(8,128)S(1)}, u32[]{:S(2)}, u32[]{:S(2)}) collective-permute-start(f32[128,384]{0,1:T(8,128)S(1)} %pad_maximum_fusion.1), channel_id=1, source_target_pairs={{0,16},{16,0},{32,48},{48,32},{64,80},{80,64},{96,112},{112,96},{1... | collective-permute-start | bytes 589832 | tf_op jit(solution)/shard_map/ppermute | solution.py:53
  107.6 6.2 %collective-permute-start.5 = (f32[128,384]{0,1:T(8,128)S(1)}, f32[128,384]{0,1:T(8,128)S(1)}, u32[]{:S(2)}, u32[]{:S(2)}) collective-permute-start(f32[128,384]{0,1:T(8,128)S(1)} %fusion.45), channel_id=1, source_target_pairs={{0,32},{16,48},{32,0},{48,16},{64,96},{80,112},{96,64},{112,80},{1... | collective-permute-start | bytes 589832 | tf_op jit(solution)/shard_map/ppermute | solution.py:53
  113.9 6.8 %collective-permute-start.6 = (f32[128,384]{0,1:T(8,128)S(1)}, f32[128,384]{0,1:T(8,128)S(1)}, u32[]{:S(2)}, u32[]{:S(2)}) collective-permute-start(f32[128,384]{0,1:T(8,128)S(1)} %add.123), channel_id=1, source_target_pairs={{0,64},{16,80},{32,96},{48,112},{64,0},{80,16},{96,32},{112,48},{1... | collective-permute-start | bytes 589832 | tf_op jit(solution)/shard_map/ppermute | solution.py:53
  120.7 14.8 %collective-permute-start.7 = (f32[128,384]{0,1:T(8,128)S(1)}, f32[128,384]{0,1:T(8,128)S(1)}, u32[]{:S(2)}, u32[]{:S(2)}) collective-permute-start(f32[128,384]{0,1:T(8,128)S(1)} %add.124), channel_id=1, source_target_pairs={{0,128},{16,144},{32,160},{48,176},{64,192},{80,208},{96,224},{112... | collective-permute-start | bytes 589832 | tf_op jit(solution)/shard_map/ppermute | solution.py:53
  123.7 30.9 %all-to-all-start.3 = ((f32[16,32,256]{2,1,0:T(8,128)}), f32[16,32,256]{2,1,0:T(8,128)S(1)}, u32[]{:S(2)}, u32[]{:S(2)}) async-start(f32[16,32,256]{2,1,0:T(8,128)} %bitcast.288), calls=%async_computation.3 | async-start | bytes 1048576 | tf_op jit(solution)/shard_map/all_to_all | solution.py:33
  155.6 28.4 %all-to-all-start.4 = ((f32[16,32,256]{2,1,0:T(8,128)}), f32[16,32,256]{2,1,0:T(8,128)S(1)}, u32[]{:S(2)}, u32[]{:S(2)}) async-start(f32[16,32,256]{2,1,0:T(8,128)} %broadcast_in_dim.12), calls=%async_computation.4 | async-start | bytes 1048576 | tf_op jit(solution)/shard_map/all_to_all | solution.py:18
  185.6 5.3 %collective-permute-start.8 = (f32[128,384]{0,1:T(8,128)S(1)}, f32[128,384]{0,1:T(8,128)S(1)}, u32[]{:S(2)}, u32[]{:S(2)}) collective-permute-start(f32[128,384]{0,1:T(8,128)S(1)} %pad_maximum_fusion.2), channel_id=1, source_target_pairs={{0,1},{1,0},{2,3},{3,2},{4,5},{5,4},{6,7},{7,6},{8,9},{9,8},{10,11... | collective-permute-start | bytes 589832 | tf_op jit(solution)/shard_map/ppermute | solution.py:53
  191.0 9.6 %collective-permute-start.9 = (f32[128,384]{0,1:T(8,128)S(1)}, f32[128,384]{0,1:T(8,128)S(1)}, u32[]{:S(2)}, u32[]{:S(2)}) collective-permute-start(f32[128,384]{0,1:T(8,128)S(1)} %fusion.44), channel_id=1, source_target_pairs={{0,2},{1,3},{2,0},{3,1},{4,6},{5,7},{6,4},{7,5},{8,10},{9,11},{10,... | collective-permute-start | bytes 589832 | tf_op jit(solution)/shard_map/ppermute | solution.py:53
  200.6 5.1 %collective-permute-start.10 = (f32[128,384]{0,1:T(8,128)S(1)}, f32[128,384]{0,1:T(8,128)S(1)}, u32[]{:S(2)}, u32[]{:S(2)}) collective-permute-start(f32[128,384]{0,1:T(8,128)S(1)} %add.134), channel_id=1, source_target_pairs={{0,4},{1,5},{2,6},{3,7},{4,0},{5,1},{6,2},{7,3},{8,12},{9,13},{10,... | collective-permute-start | bytes 589832 | tf_op jit(solution)/shard_map/ppermute | solution.py:53
  205.7 10.1 %collective-permute-start.11 = (f32[128,384]{0,1:T(8,128)S(1)}, f32[128,384]{0,1:T(8,128)S(1)}, u32[]{:S(2)}, u32[]{:S(2)}) collective-permute-start(f32[128,384]{0,1:T(8,128)S(1)} %add.135), channel_id=1, source_target_pairs={{0,8},{1,9},{2,10},{3,11},{4,12},{5,13},{6,14},{7,15},{8,0},{9,1},... | collective-permute-start | bytes 589832 | tf_op jit(solution)/shard_map/ppermute | solution.py:53
  207.9 25.8 %all-to-all-start.5 = ((f32[16,32,256]{2,1,0:T(8,128)}), f32[16,32,256]{2,1,0:T(8,128)}, u32[]{:S(2)}, u32[]{:S(2)}) async-start(f32[16,32,256]{2,1,0:T(8,128)} %bitcast.9), calls=%async_computation.5 | async-start | bytes 1048576 | tf_op jit(solution)/shard_map/all_to_all | solution.py:33
  237.2 18.8 %all-to-all-start.6 = ((f32[16,32,256]{2,1,0:T(8,128)}), f32[16,32,256]{2,1,0:T(8,128)}, u32[]{:S(2)}, u32[]{:S(2)}) async-start(f32[16,32,256]{2,1,0:T(8,128)} %broadcast_in_dim.13), calls=%async_computation.6 | async-start | bytes 1048576 | tf_op jit(solution)/shard_map/all_to_all | solution.py:18
  258.7 4.5 %collective-permute-start.12 = (f32[128,384]{0,1:T(8,128)S(1)}, f32[128,384]{0,1:T(8,128)S(1)}, u32[]{:S(2)}, u32[]{:S(2)}) collective-permute-start(f32[128,384]{0,1:T(8,128)S(1)} %pad_maximum_fusion.3), channel_id=1, source_target_pairs={{0,16},{16,0},{32,48},{48,32},{64,80},{80,64},{96,112},{112,96},{1... | collective-permute-start | bytes 589832 | tf_op jit(solution)/shard_map/ppermute | solution.py:53
  263.3 6.2 %collective-permute-start.13 = (f32[128,384]{0,1:T(8,128)S(1)}, f32[128,384]{0,1:T(8,128)S(1)}, u32[]{:S(2)}, u32[]{:S(2)}) collective-permute-start(f32[128,384]{0,1:T(8,128)S(1)} %fusion.43), channel_id=1, source_target_pairs={{0,32},{16,48},{32,0},{48,16},{64,96},{80,112},{96,64},{112,80},{1... | collective-permute-start | bytes 589832 | tf_op jit(solution)/shard_map/ppermute | solution.py:53
  269.5 6.8 %collective-permute-start.14 = (f32[128,384]{0,1:T(8,128)S(1)}, f32[128,384]{0,1:T(8,128)S(1)}, u32[]{:S(2)}, u32[]{:S(2)}) collective-permute-start(f32[128,384]{0,1:T(8,128)S(1)} %add.141), channel_id=1, source_target_pairs={{0,64},{16,80},{32,96},{48,112},{64,0},{80,16},{96,32},{112,48},{1... | collective-permute-start | bytes 589832 | tf_op jit(solution)/shard_map/ppermute | solution.py:53
  276.3 14.5 %collective-permute-start.15 = (f32[128,384]{0,1:T(8,128)S(1)}, f32[128,384]{0,1:T(8,128)S(1)}, u32[]{:S(2)}, u32[]{:S(2)}) collective-permute-start(f32[128,384]{0,1:T(8,128)S(1)} %add.142), channel_id=1, source_target_pairs={{0,128},{16,144},{32,160},{48,176},{64,192},{80,208},{96,224},{112... | collective-permute-start | bytes 589832 | tf_op jit(solution)/shard_map/ppermute | solution.py:53
  279.3 30.8 %all-to-all-start.7 = ((f32[16,32,256]{2,1,0:T(8,128)}), f32[16,32,256]{2,1,0:T(8,128)}, u32[]{:S(2)}, u32[]{:S(2)}) async-start(f32[16,32,256]{2,1,0:T(8,128)} %bitcast.287), calls=%async_computation.7 | async-start | bytes 1048576 | tf_op jit(solution)/shard_map/all_to_all | solution.py:33
  312.3 27.8 %all-to-all-start.8 = ((f32[16,32,256]{2,1,0:T(8,128)}), f32[16,32,256]{2,1,0:T(8,128)S(1)}, u32[]{:S(2)}, u32[]{:S(2)}) async-start(f32[16,32,256]{2,1,0:T(8,128)} %broadcast_in_dim.14), calls=%async_computation.8 | async-start | bytes 1048576 | tf_op jit(solution)/shard_map/all_to_all | solution.py:18
  (9 other events, 62.7 us)

commit v7 on v6

--- a/solution.py
+++ b/solution.py
@@ -107,7 +107,7 @@
     topic_tile = gather_topics(topics)
     for iteration in range(ITERS):
         merged = latent + dual_latent
-        gram_topic = symmetric_sum(product_left(topic_tile, topic_tile), "word")
+        gram_topic = exchanged_sum(product_left(topic_tile, topic_tile), "word")
 
         def doc_term(first_row, row_count, merged=merged, topic_tile=topic_tile):
             return product(merged, topic_tile)

time: 352 us -> 358 us (1.017)
  waiting for transfers between devices: 106 us -> 139 us
  blocking collectives: 28.9 us -> 0 us
    ppermute x16, waiting for transfers between devices: 51.9 us -> 87.1 us  [exchanged_sum(): x = x + lax.ppermute(x, axis, [(i, i ^ bit) for i in range(count)])]
    all_to_all x1 -> x0, blocking collectives: 28.9 us -> none  [copy_for_each(): lax.all_to_all(jnp.broadcast_to(x[None], (count, *x.shape)), axis, 0, 0,...]
    all_to_all x4 -> x5, starting transfers between devices: 31.4 us -> 40.8 us  [copy_for_each(): lax.all_to_all(jnp.broadcast_to(x[None], (count, *x.shape)), axis, 0, 0,...]
    all_to_all x4, starting transfers between devices: 37.9 us -> 31.3 us  [summed_on_arrival(): pieces = lax.all_to_all(split_up(x, dim, count), axis, 0, 0, tiled=True)]
    all_to_all x4 -> x5, waiting for transfers between devices: 52 us -> 51.6 us  [copy_for_each(): lax.all_to_all(jnp.broadcast_to(x[None], (count, *x.shape)), axis, 0, 0,...]
  transfers between devices with their start and end apart: 24 -> 25, of which waited for: 18 -> 18; matrix products, arithmetic and copies ran while one was open for 26% -> 26% of each run, Pallas kernels for 0% -> 0%
where the time goes in v7:
time: 358 us; the launch traced here: 352 us
  waiting for transfers between devices  139 us (39%)
  matrix products  100 us (28%)
  starting transfers between devices  94.5 us (26%)
  other arithmetic  6.62 us (2%)
  local copies, waits for them, and re-layouts  6.38 us (2%)
  between operations  5.2 us (1%)
    ppermute x16, waiting for transfers between devices, exchanged_sum(): x = x + lax.ppermute(x, axis, [(i, i ^ bit) for i in range(count)])  87.1 us
    dot_general x154, matrix products, product(): jnp.dot(left, right, precision=lax.Precision.HIGHEST, preferred_element_t...  82.2 us
    all_to_all x5, waiting for transfers between devices, copy_for_each(): lax.all_to_all(jnp.broadcast_to(x[None], (count, *x.shape)), axis, 0, 0,...  51.6 us
    all_to_all x5, starting transfers between devices, copy_for_each(): lax.all_to_all(jnp.broadcast_to(x[None], (count, *x.shape)), axis, 0, 0,...  40.8 us
    all_to_all x4, starting transfers between devices, summed_on_arrival(): pieces = lax.all_to_all(split_up(x, dim, count), axis, 0, 0, tiled=True)  31.3 us
    ppermute x16, starting transfers between devices, exchanged_sum(): x = x + lax.ppermute(x, axis, [(i, i ^ bit) for i in range(count)])  22.5 us
    dot_general x6, matrix products, product_left(): lax.dot_general(left, right, (((0,), (0,)), ((), ())), precision=lax.Prec...  9.2 us
    dot_general x2, matrix products, product_right(): lax.dot_general(left, right, (((1,), (1,)), ((), ())), precision=lax.Prec...  8.64 us
  transfers between devices with their start and end apart: 25, of which 18 were waited for; matrix products, arithmetic and copies ran while one was open for 26% of the time, Pallas kernels for 0%

profile of v7, /device:TPU:65, one launch (start us, length us, event | category | flops | bytes accessed | tf_op | source)
XLA Modules:
  0.0 352.1 jit_solution(10645094681798029355)
XLA Ops:
  2.3 9.8 %all-to-all-start = ((f32[16,32,256]{2,1,0:T(8,128)}), f32[16,32,256]{2,1,0:T(8,128)S(1)}, u32[]{:S(2)}, u32[]{:S(2)}) async-start(f32[16,32,256]{2,1,0:T(8,128)} %broadcast_in_dim.10), calls=%async_computation | async-start | bytes 1048576 | tf_op jit(solution)/shard_map/all_to_all | solution.py:18
  13.6 17.9 %all-to-all-done = f32[16,32,256]{2,1,0:T(8,128)S(1)} async-done(((f32[16,32,256]{2,1,0:T(8,128)}), f32[16,32,256]{2,1,0:T(8,128)S(1)}, u32[]{:S(2)}, u32[]{:S(2)}) %all-to-all-start) | async-done | bytes 524320 | tf_op jit(solution)/shard_map/all_to_all | solution.py:18
  33.3 6.3 %all-to-all-start.1 = ((f32[16,32,256]{2,1,0:T(8,128)}), f32[16,32,256]{2,1,0:T(8,128)S(1)}, u32[]{:S(2)}, u32[]{:S(2)}) async-start(f32[16,32,256]{2,1,0:T(8,128)} %fusion.45), calls=%async_computation.1 | async-start | bytes 1048576 | tf_op jit(solution)/shard_map/all_to_all | solution.py:33
  41.8 12.5 %collective-permute-done = f32[256,256]{0,1:T(8,128)S(1)} collective-permute-done((f32[256,256]{0,1:T(8,128)S(1)}, f32[256,256]{0,1:T(8,128)S(1)}, u32[]{:S(2)}, u32[]{:S(2)}) %collective-permute-start) | collective-permute-done | bytes 262176 | tf_op jit(solution)/shard_map/ppermute | solution.py:53
  55.6 11.3 %collective-permute-done.1 = f32[256,256]{0,1:T(8,128)S(1)} collective-permute-done((f32[256,256]{0,1:T(8,128)S(1)}, f32[256,256]{0,1:T(8,128)S(1)}, u32[]{:S(2)}, u32[]{:S(2)}) %collective-permute-start.1) | collective-permute-done | bytes 262176 | tf_op jit(solution)/shard_map/ppermute | solution.py:53
  68.1 6.3 %collective-permute-done.2 = f32[256,256]{0,1:T(8,128)S(1)} collective-permute-done((f32[256,256]{0,1:T(8,128)S(1)}, f32[256,256]{0,1:T(8,128)S(1)}, u32[]{:S(2)}, u32[]{:S(2)}) %collective-permute-start.2) | collective-permute-done | bytes 262176 | tf_op jit(solution)/shard_map/ppermute | solution.py:53
  78.0 7.0 %all-to-all-start.2 = ((f32[16,32,256]{2,1,0:T(8,128)}), f32[16,32,256]{2,1,0:T(8,128)S(1)}, u32[]{:S(2)}, u32[]{:S(2)}) async-start(f32[16,32,256]{2,1,0:T(8,128)} %broadcast_in_dim.11), calls=%async_computation.2 | async-start | bytes 1048576 | tf_op jit(solution)/shard_map/all_to_all | solution.py:18
  111.5 6.1 %collective-permute-done.5 = f32[128,384]{0,1:T(8,128)S(1)} collective-permute-done((f32[128,384]{0,1:T(8,128)S(1)}, f32[128,384]{0,1:T(8,128)S(1)}, u32[]{:S(2)}, u32[]{:S(2)}) %collective-permute-start.5) | collective-permute-done | bytes 196640 | tf_op jit(solution)/shard_map/ppermute | solution.py:53
  118.9 5.6 %collective-permute-done.6 = f32[128,384]{0,1:T(8,128)S(1)} collective-permute-done((f32[128,384]{0,1:T(8,128)S(1)}, f32[128,384]{0,1:T(8,128)S(1)}, u32[]{:S(2)}, u32[]{:S(2)}) %collective-permute-start.6) | collective-permute-done | bytes 196640 | tf_op jit(solution)/shard_map/ppermute | solution.py:53
  127.5 10.2 %all-to-all-start.3 = ((f32[16,32,256]{2,1,0:T(8,128)}), f32[16,32,256]{2,1,0:T(8,128)S(1)}, u32[]{:S(2)}, u32[]{:S(2)}) async-start(f32[16,32,256]{2,1,0:T(8,128)} %bitcast.5), calls=%async_computation.3 | async-start | bytes 1048576 | tf_op jit(solution)/shard_map/all_to_all | solution.py:33
  158.5 8.3 %all-to-all-start.4 = ((f32[16,32,256]{2,1,0:T(8,128)}), f32[16,32,256]{2,1,0:T(8,128)S(1)}, u32[]{:S(2)}, u32[]{:S(2)}) async-start(f32[16,32,256]{2,1,0:T(8,128)} %broadcast_in_dim.12), calls=%async_computation.4 | async-start | bytes 1048576 | tf_op jit(solution)/shard_map/all_to_all | solution.py:18
  169.3 16.8 %all-to-all-done.4 = f32[16,32,256]{2,1,0:T(8,128)S(1)} async-done(((f32[16,32,256]{2,1,0:T(8,128)}), f32[16,32,256]{2,1,0:T(8,128)S(1)}, u32[]{:S(2)}, u32[]{:S(2)}) %all-to-all-start.4) | async-done | bytes 524320 | tf_op jit(solution)/shard_map/all_to_all | solution.py:18
  186.7 3.8 %fusion = (f32[512,512]{1,0:T(8,128)S(1)}, f32[512,512]{1,0:T(8,128)}) fusion(s32[512,512]{1,0:T(8,128)} %param.8, f32[512,512]{1,0:T(8,128)S(1)} %copy-done, f32[512,256]{1,0:T(8,128)S(1)} %fusion.63, f32[512,256]{1,0:T(8,128)S(1)} %fusion.83), kind=kOutput, calls=%fused_computation.84 | convolution fusion | flops 808189952 | bytes 5242880 | tf_op jit(solution)/shard_map/dot_general | solution.py:81
  192.3 5.8 %all-to-all-start.5 = ((f32[16,32,256]{2,1,0:T(8,128)}), f32[16,32,256]{2,1,0:T(8,128)S(1)}, u32[]{:S(2)}, u32[]{:S(2)}) async-start(f32[16,32,256]{2,1,0:T(8,128)} %bitcast.303), calls=%async_computation.5 | async-start | bytes 1048576 | tf_op jit(solution)/shard_map/all_to_all | solution.py:33
  200.3 12.5 %collective-permute-done.8 = f32[256,256]{0,1:T(8,128)S(1)} collective-permute-done((f32[256,256]{0,1:T(8,128)S(1)}, f32[256,256]{0,1:T(8,128)S(1)}, u32[]{:S(2)}, u32[]{:S(2)}) %collective-permute-start.8) | collective-permute-done | bytes 262176 | tf_op jit(solution)/shard_map/ppermute | solution.py:53
  214.1 11.3 %collective-permute-done.9 = f32[256,256]{0,1:T(8,128)S(1)} collective-permute-done((f32[256,256]{0,1:T(8,128)S(1)}, f32[256,256]{0,1:T(8,128)S(1)}, u32[]{:S(2)}, u32[]{:S(2)}) %collective-permute-start.9) | collective-permute-done | bytes 262176 | tf_op jit(solution)/shard_map/ppermute | solution.py:53
  226.8 6.3 %collective-permute-done.10 = f32[256,256]{0,1:T(8,128)S(1)} collective-permute-done((f32[256,256]{0,1:T(8,128)S(1)}, f32[256,256]{0,1:T(8,128)S(1)}, u32[]{:S(2)}, u32[]{:S(2)}) %collective-permute-start.10) | collective-permute-done | bytes 262176 | tf_op jit(solution)/shard_map/ppermute | solution.py:53
  237.6 6.8 %all-to-all-start.6 = ((f32[16,32,256]{2,1,0:T(8,128)}), f32[16,32,256]{2,1,0:T(8,128)S(1)}, u32[]{:S(2)}, u32[]{:S(2)}) async-start(f32[16,32,256]{2,1,0:T(8,128)} %broadcast_in_dim.13), calls=%async_computation.6 | async-start | bytes 1048576 | tf_op jit(solution)/shard_map/all_to_all | solution.py:18
  270.7 6.1 %collective-permute-done.13 = f32[128,384]{0,1:T(8,128)S(1)} collective-permute-done((f32[128,384]{0,1:T(8,128)S(1)}, f32[128,384]{0,1:T(8,128)S(1)}, u32[]{:S(2)}, u32[]{:S(2)}) %collective-permute-start.13) | collective-permute-done | bytes 196640 | tf_op jit(solution)/shard_map/ppermute | solution.py:53
  279.0 4.7 %collective-permute-done.14 = f32[128,384]{0,1:T(8,128)S(1)} collective-permute-done((f32[128,384]{0,1:T(8,128)S(1)}, f32[128,384]{0,1:T(8,128)S(1)}, u32[]{:S(2)}, u32[]{:S(2)}) %collective-permute-start.14) | collective-permute-done | bytes 196640 | tf_op jit(solution)/shard_map/ppermute | solution.py:53
  288.0 9.0 %all-to-all-start.7 = ((f32[16,32,256]{2,1,0:T(8,128)}), f32[16,32,256]{2,1,0:T(8,128)S(1)}, u32[]{:S(2)}, u32[]{:S(2)}) async-start(f32[16,32,256]{2,1,0:T(8,128)} %bitcast.10), calls=%async_computation.7 | async-start | bytes 1048576 | tf_op jit(solution)/shard_map/all_to_all | solution.py:33
  317.9 8.8 %all-to-all-start.8 = ((f32[16,32,256]{2,1,0:T(8,128)}), f32[16,32,256]{2,1,0:T(8,128)S(1)}, u32[]{:S(2)}, u32[]{:S(2)}) async-start(f32[16,32,256]{2,1,0:T(8,128)} %broadcast_in_dim.14), calls=%async_computation.8 | async-start | bytes 1048576 | tf_op jit(solution)/shard_map/all_to_all | solution.py:18
  329.6 16.9 %all-to-all-done.8 = f32[16,32,256]{2,1,0:T(8,128)S(1)} async-done(((f32[16,32,256]{2,1,0:T(8,128)}), f32[16,32,256]{2,1,0:T(8,128)S(1)}, u32[]{:S(2)}, u32[]{:S(2)}) %all-to-all-start.8) | async-done | bytes 524320 | tf_op jit(solution)/shard_map/all_to_all | solution.py:18
  347.1 4.9 %add_subtract_fusion = (f32[512,512]{1,0:T(8,128)}, f32[512,512]{1,0:T(8,128)}) fusion(f32[512,512]{1,0:T(8,128)} %get-tuple-element.23, f32[512,512]{1,0:T(8,128)S(1)} %copy-done, s32[512,512]{1,0:T(8,128)} %param.8, f32[512,256]{1,0:T(8,128)S(1)} %fusion.103, f32[512,256]{1,0:T(8,128)S(1)} %fusion.123), kind=kOutput, calls=%fused_computation.75 | convolution fusion | flops 810024960 | bytes 6291456 | tf_op jit(solution)/shard_map/dot_general | solution.py:81
  (256 shorter events, 131.9 us)
Async XLA Ops:
  2.3 29.1 %all-to-all-start = ((f32[16,32,256]{2,1,0:T(8,128)}), f32[16,32,256]{2,1,0:T(8,128)S(1)}, u32[]{:S(2)}, u32[]{:S(2)}) async-start(f32[16,32,256]{2,1,0:T(8,128)} %broadcast_in_dim.10), calls=%async_computation | async-start | bytes 1048576 | tf_op jit(solution)/shard_map/all_to_all | solution.py:18
  33.3 43.9 %all-to-all-start.1 = ((f32[16,32,256]{2,1,0:T(8,128)}), f32[16,32,256]{2,1,0:T(8,128)S(1)}, u32[]{:S(2)}, u32[]{:S(2)}) async-start(f32[16,32,256]{2,1,0:T(8,128)} %fusion.45), calls=%async_computation.1 | async-start | bytes 1048576 | tf_op jit(solution)/shard_map/all_to_all | solution.py:33
  40.5 13.8 %collective-permute-start = (f32[256,256]{0,1:T(8,128)S(1)}, f32[256,256]{0,1:T(8,128)S(1)}, u32[]{:S(2)}, u32[]{:S(2)}) collective-permute-start(f32[256,256]{0,1:T(8,128)S(1)} %convolution_bitcast_fusion), channel_id=1, source_target_pairs={{0,1},{1,0},{2,3},{3,2},{4,5},{5,4},{6,7},{7,6},{8,9},{9,8},{10,11... | collective-permute-start | bytes 786440 | tf_op jit(solution)/shard_map/ppermute | solution.py:53
  54.4 12.5 %collective-permute-start.1 = (f32[256,256]{0,1:T(8,128)S(1)}, f32[256,256]{0,1:T(8,128)S(1)}, u32[]{:S(2)}, u32[]{:S(2)}) collective-permute-start(f32[256,256]{0,1:T(8,128)S(1)} %add.116), channel_id=1, source_target_pairs={{0,2},{1,3},{2,0},{3,1},{4,6},{5,7},{6,4},{7,5},{8,10},{9,11},{10,... | collective-permute-start | bytes 786440 | tf_op jit(solution)/shard_map/ppermute | solution.py:53
  66.9 7.5 %collective-permute-start.2 = (f32[256,256]{0,1:T(8,128)S(1)}, f32[256,256]{0,1:T(8,128)S(1)}, u32[]{:S(2)}, u32[]{:S(2)}) collective-permute-start(f32[256,256]{0,1:T(8,128)S(1)} %add.117), channel_id=1, source_target_pairs={{0,4},{1,5},{2,6},{3,7},{4,0},{5,1},{6,2},{7,3},{8,12},{9,13},{10,... | collective-permute-start | bytes 786440 | tf_op jit(solution)/shard_map/ppermute | solution.py:53
  74.5 10.6 %collective-permute-start.3 = (f32[256,256]{0,1:T(8,128)S(1)}, f32[256,256]{0,1:T(8,128)}, u32[]{:S(2)}, u32[]{:S(2)}) collective-permute-start(f32[256,256]{0,1:T(8,128)S(1)} %add.118), channel_id=1, source_target_pairs={{0,8},{1,9},{2,10},{3,11},{4,12},{5,13},{6,14},{7,15},{8,0},{9,1},... | collective-permute-start | bytes 786440 | tf_op jit(solution)/shard_map/ppermute | solution.py:53
  78.0 28.0 %all-to-all-start.2 = ((f32[16,32,256]{2,1,0:T(8,128)}), f32[16,32,256]{2,1,0:T(8,128)S(1)}, u32[]{:S(2)}, u32[]{:S(2)}) async-start(f32[16,32,256]{2,1,0:T(8,128)} %broadcast_in_dim.11), calls=%async_computation.2 | async-start | bytes 1048576 | tf_op jit(solution)/shard_map/all_to_all | solution.py:18
  111.4 6.2 %collective-permute-start.5 = (f32[128,384]{0,1:T(8,128)S(1)}, f32[128,384]{0,1:T(8,128)S(1)}, u32[]{:S(2)}, u32[]{:S(2)}) collective-permute-start(f32[128,384]{0,1:T(8,128)S(1)} %fusion.44), channel_id=1, source_target_pairs={{0,32},{16,48},{32,0},{48,16},{64,96},{80,112},{96,64},{112,80},{1... | collective-permute-start | bytes 589832 | tf_op jit(solution)/shard_map/ppermute | solution.py:53
  117.6 6.8 %collective-permute-start.6 = (f32[128,384]{0,1:T(8,128)S(1)}, f32[128,384]{0,1:T(8,128)S(1)}, u32[]{:S(2)}, u32[]{:S(2)}) collective-permute-start(f32[128,384]{0,1:T(8,128)S(1)} %add.123), channel_id=1, source_target_pairs={{0,64},{16,80},{32,96},{48,112},{64,0},{80,16},{96,32},{112,48},{1... | collective-permute-start | bytes 589832 | tf_op jit(solution)/shard_map/ppermute | solution.py:53
  124.4 14.6 %collective-permute-start.7 = (f32[128,384]{0,1:T(8,128)S(1)}, f32[128,384]{0,1:T(8,128)S(1)}, u32[]{:S(2)}, u32[]{:S(2)}) collective-permute-start(f32[128,384]{0,1:T(8,128)S(1)} %add.124), channel_id=1, source_target_pairs={{0,128},{16,144},{32,160},{48,176},{64,192},{80,208},{96,224},{112... | collective-permute-start | bytes 589832 | tf_op jit(solution)/shard_map/ppermute | solution.py:53
  127.5 29.4 %all-to-all-start.3 = ((f32[16,32,256]{2,1,0:T(8,128)}), f32[16,32,256]{2,1,0:T(8,128)S(1)}, u32[]{:S(2)}, u32[]{:S(2)}) async-start(f32[16,32,256]{2,1,0:T(8,128)} %bitcast.5), calls=%async_computation.3 | async-start | bytes 1048576 | tf_op jit(solution)/shard_map/all_to_all | solution.py:33
  158.5 27.6 %all-to-all-start.4 = ((f32[16,32,256]{2,1,0:T(8,128)}), f32[16,32,256]{2,1,0:T(8,128)S(1)}, u32[]{:S(2)}, u32[]{:S(2)}) async-start(f32[16,32,256]{2,1,0:T(8,128)} %broadcast_in_dim.12), calls=%async_computation.4 | async-start | bytes 1048576 | tf_op jit(solution)/shard_map/all_to_all | solution.py:18
  192.3 43.5 %all-to-all-start.5 = ((f32[16,32,256]{2,1,0:T(8,128)}), f32[16,32,256]{2,1,0:T(8,128)S(1)}, u32[]{:S(2)}, u32[]{:S(2)}) async-start(f32[16,32,256]{2,1,0:T(8,128)} %bitcast.303), calls=%async_computation.5 | async-start | bytes 1048576 | tf_op jit(solution)/shard_map/all_to_all | solution.py:33
  199.1 13.8 %collective-permute-start.8 = (f32[256,256]{0,1:T(8,128)S(1)}, f32[256,256]{0,1:T(8,128)S(1)}, u32[]{:S(2)}, u32[]{:S(2)}) collective-permute-start(f32[256,256]{0,1:T(8,128)S(1)} %fusion.85), channel_id=1, source_target_pairs={{0,1},{1,0},{2,3},{3,2},{4,5},{5,4},{6,7},{7,6},{8,9},{9,8},{10,11... | collective-permute-start | bytes 786440 | tf_op jit(solution)/shard_map/ppermute | solution.py:53
  212.9 12.5 %collective-permute-start.9 = (f32[256,256]{0,1:T(8,128)S(1)}, f32[256,256]{0,1:T(8,128)S(1)}, u32[]{:S(2)}, u32[]{:S(2)}) collective-permute-start(f32[256,256]{0,1:T(8,128)S(1)} %add.133), channel_id=1, source_target_pairs={{0,2},{1,3},{2,0},{3,1},{4,6},{5,7},{6,4},{7,5},{8,10},{9,11},{10,... | collective-permute-start | bytes 786440 | tf_op jit(solution)/shard_map/ppermute | solution.py:53
  225.5 7.6 %collective-permute-start.10 = (f32[256,256]{0,1:T(8,128)S(1)}, f32[256,256]{0,1:T(8,128)S(1)}, u32[]{:S(2)}, u32[]{:S(2)}) collective-permute-start(f32[256,256]{0,1:T(8,128)S(1)} %add.134), channel_id=1, source_target_pairs={{0,4},{1,5},{2,6},{3,7},{4,0},{5,1},{6,2},{7,3},{8,12},{9,13},{10,... | collective-permute-start | bytes 786440 | tf_op jit(solution)/shard_map/ppermute | solution.py:53
  233.2 11.2 %collective-permute-start.11 = (f32[256,256]{0,1:T(8,128)S(1)}, f32[256,256]{0,1:T(8,128)}, u32[]{:S(2)}, u32[]{:S(2)}) collective-permute-start(f32[256,256]{0,1:T(8,128)S(1)} %add.135), channel_id=1, source_target_pairs={{0,8},{1,9},{2,10},{3,11},{4,12},{5,13},{6,14},{7,15},{8,0},{9,1},... | collective-permute-start | bytes 786440 | tf_op jit(solution)/shard_map/ppermute | solution.py:53
  237.6 27.8 %all-to-all-start.6 = ((f32[16,32,256]{2,1,0:T(8,128)}), f32[16,32,256]{2,1,0:T(8,128)S(1)}, u32[]{:S(2)}, u32[]{:S(2)}) async-start(f32[16,32,256]{2,1,0:T(8,128)} %broadcast_in_dim.13), calls=%async_computation.6 | async-start | bytes 1048576 | tf_op jit(solution)/shard_map/all_to_all | solution.py:18
  267.0 3.6 %collective-permute-start.12 = (f32[128,384]{0,1:T(8,128)S(1)}, f32[128,384]{0,1:T(8,128)S(1)}, u32[]{:S(2)}, u32[]{:S(2)}) collective-permute-start(f32[128,384]{0,1:T(8,128)S(1)} %pad_maximum_fusion.1), channel_id=1, source_target_pairs={{0,16},{16,0},{32,48},{48,32},{64,80},{80,64},{96,112},{112,96},{1... | collective-permute-start | bytes 589832 | tf_op jit(solution)/shard_map/ppermute | solution.py:53
  270.6 6.2 %collective-permute-start.13 = (f32[128,384]{0,1:T(8,128)S(1)}, f32[128,384]{0,1:T(8,128)S(1)}, u32[]{:S(2)}, u32[]{:S(2)}) collective-permute-start(f32[128,384]{0,1:T(8,128)S(1)} %fusion.43), channel_id=1, source_target_pairs={{0,32},{16,48},{32,0},{48,16},{64,96},{80,112},{96,64},{112,80},{1... | collective-permute-start | bytes 589832 | tf_op jit(solution)/shard_map/ppermute | solution.py:53
  276.9 6.8 %collective-permute-start.14 = (f32[128,384]{0,1:T(8,128)S(1)}, f32[128,384]{0,1:T(8,128)S(1)}, u32[]{:S(2)}, u32[]{:S(2)}) collective-permute-start(f32[128,384]{0,1:T(8,128)S(1)} %add.141), channel_id=1, source_target_pairs={{0,64},{16,80},{32,96},{48,112},{64,0},{80,16},{96,32},{112,48},{1... | collective-permute-start | bytes 589832 | tf_op jit(solution)/shard_map/ppermute | solution.py:53
  283.7 14.1 %collective-permute-start.15 = (f32[128,384]{0,1:T(8,128)S(1)}, f32[128,384]{0,1:T(8,128)S(1)}, u32[]{:S(2)}, u32[]{:S(2)}) collective-permute-start(f32[128,384]{0,1:T(8,128)S(1)} %add.142), channel_id=1, source_target_pairs={{0,128},{16,144},{32,160},{48,176},{64,192},{80,208},{96,224},{112... | collective-permute-start | bytes 589832 | tf_op jit(solution)/shard_map/ppermute | solution.py:53
  288.0 28.6 %all-to-all-start.7 = ((f32[16,32,256]{2,1,0:T(8,128)}), f32[16,32,256]{2,1,0:T(8,128)S(1)}, u32[]{:S(2)}, u32[]{:S(2)}) async-start(f32[16,32,256]{2,1,0:T(8,128)} %bitcast.10), calls=%async_computation.7 | async-start | bytes 1048576 | tf_op jit(solution)/shard_map/all_to_all | solution.py:33
  317.9 28.6 %all-to-all-start.8 = ((f32[16,32,256]{2,1,0:T(8,128)}), f32[16,32,256]{2,1,0:T(8,128)S(1)}, u32[]{:S(2)}, u32[]{:S(2)}) async-start(f32[16,32,256]{2,1,0:T(8,128)} %broadcast_in_dim.14), calls=%async_computation.8 | async-start | bytes 1048576 | tf_op jit(solution)/shard_map/all_to_all | solution.py:18
  (12 other events, 52.3 us)

commit v8 on v5

--- a/solution.py
+++ b/solution.py
@@ -48,10 +48,10 @@
 
 def exchanged_sum(x, axis):
     count = lax.axis_size(axis)
-    bit = 1
-    while bit < count:
+    bit = count // 2
+    while bit >= 1:
         x = x + lax.ppermute(x, axis, [(i, i ^ bit) for i in range(count)])
-        bit *= 2
+        bit //= 2
     return x
 
 

time: 345 us -> 351 us (1.017)
  the two profiles are of different devices: /device:TPU:164 before, /device:TPU:65 now
where the time goes in v8:
time: 351 us; the launch traced here: 344 us
  waiting for transfers between devices  124 us (35%)
  starting transfers between devices  100 us (28%)
  matrix products  100 us (28%)
  other arithmetic  8.4 us (2%)
  local copies, waits for them, and re-layouts  6.19 us (2%)
  between operations  5.07 us (1%)
    ppermute x16, waiting for transfers between devices, exchanged_sum(): x = x + lax.ppermute(x, axis, [(i, i ^ bit) for i in range(count)])  106 us
    dot_general x154, matrix products, product(): jnp.dot(left, right, precision=lax.Precision.HIGHEST, preferred_element_t...  81.8 us
    ppermute x16, starting transfers between devices, exchanged_sum(): x = x + lax.ppermute(x, axis, [(i, i ^ bit) for i in range(count)])  42 us
    all_to_all x5, starting transfers between devices, copy_for_each(): lax.all_to_all(jnp.broadcast_to(x[None], (count, *x.shape)), axis, 0, 0,...  35.4 us
    all_to_all x4, starting transfers between devices, summed_on_arrival(): pieces = lax.all_to_all(split_up(x, dim, count), axis, 0, 0, tiled=True)  22.6 us
    all_to_all x5, waiting for transfers between devices, copy_for_each(): lax.all_to_all(jnp.broadcast_to(x[None], (count, *x.shape)), axis, 0, 0,...  17.9 us
    dot_general x6, matrix products, product_left(): lax.dot_general(left, right, (((0,), (0,)), ((), ())), precision=lax.Prec...  9.89 us
    dot_general x2, matrix products, product_right(): lax.dot_general(left, right, (((1,), (1,)), ((), ())), precision=lax.Prec...  8.64 us
  transfers between devices with their start and end apart: 25, of which 13 were waited for; matrix products, arithmetic and copies ran while one was open for 27% of the time, Pallas kernels for 0%

profile of v8, /device:TPU:65, one launch (start us, length us, event | category | flops | bytes accessed | tf_op | source)
XLA Modules:
  0.0 343.6 jit_solution(5797732463827703273)
XLA Ops:
  2.3 9.8 %all-to-all-start = ((f32[16,32,256]{2,1,0:T(8,128)}), f32[16,32,256]{2,1,0:T(8,128)S(1)}, u32[]{:S(2)}, u32[]{:S(2)}) async-start(f32[16,32,256]{2,1,0:T(8,128)} %broadcast_in_dim.10), calls=%async_computation | async-start | bytes 1048576 | tf_op jit(solution)/shard_map/all_to_all | solution.py:18
  13.6 17.9 %all-to-all-done = f32[16,32,256]{2,1,0:T(8,128)S(1)} async-done(((f32[16,32,256]{2,1,0:T(8,128)}), f32[16,32,256]{2,1,0:T(8,128)S(1)}, u32[]{:S(2)}, u32[]{:S(2)}) %all-to-all-start) | async-done | bytes 524320 | tf_op jit(solution)/shard_map/all_to_all | solution.py:18
  33.3 6.3 %all-to-all-start.1 = ((f32[16,32,256]{2,1,0:T(8,128)}), f32[16,32,256]{2,1,0:T(8,128)S(1)}, u32[]{:S(2)}, u32[]{:S(2)}) async-start(f32[16,32,256]{2,1,0:T(8,128)} %fusion.43), calls=%async_computation.1 | async-start | bytes 1048576 | tf_op jit(solution)/shard_map/all_to_all | solution.py:33
  43.3 9.9 %collective-permute-done = f32[256,256]{0,1:T(8,128)S(1)} collective-permute-done((f32[256,256]{0,1:T(8,128)S(1)}, f32[256,256]{0,1:T(8,128)S(1)}, u32[]{:S(2)}, u32[]{:S(2)}) %collective-permute-start) | collective-permute-done | bytes 262176 | tf_op jit(solution)/shard_map/ppermute | solution.py:53
  55.2 4.6 %collective-permute-done.1 = f32[256,256]{0,1:T(8,128)S(1)} collective-permute-done((f32[256,256]{0,1:T(8,128)S(1)}, f32[256,256]{0,1:T(8,128)S(1)}, u32[]{:S(2)}, u32[]{:S(2)}) %collective-permute-start.1) | collective-permute-done | bytes 262176 | tf_op jit(solution)/shard_map/ppermute | solution.py:53
  60.7 10.4 %collective-permute-done.2 = f32[256,256]{0,1:T(8,128)S(1)} collective-permute-done((f32[256,256]{0,1:T(8,128)S(1)}, f32[256,256]{0,1:T(8,128)S(1)}, u32[]{:S(2)}, u32[]{:S(2)}) %collective-permute-start.2) | collective-permute-done | bytes 262176 | tf_op jit(solution)/shard_map/ppermute | solution.py:53
  71.1 4.6 %collective-permute-start.3 = (f32[256,256]{0,1:T(8,128)S(1)}, f32[256,256]{0,1:T(8,128)S(1)}, u32[]{:S(2)}, u32[]{:S(2)}) collective-permute-start(f32[256,256]{0,1:T(8,128)S(1)} %add.118), channel_id=1, source_target_pairs={{0,1},{1,0},{2,3},{3,2},{4,5},{5,4},{6,7},{7,6},{8,9},{9,8},{10,11... | collective-permute-start | bytes 786440 | tf_op jit(solution)/shard_map/ppermute | solution.py:53
  76.7 6.2 %all-to-all-start.2 = ((f32[16,32,256]{2,1,0:T(8,128)}), f32[16,32,256]{2,1,0:T(8,128)S(1)}, u32[]{:S(2)}, u32[]{:S(2)}) async-start(f32[16,32,256]{2,1,0:T(8,128)} %broadcast_in_dim.11), calls=%async_computation.2 | async-start | bytes 1048576 | tf_op jit(solution)/shard_map/all_to_all | solution.py:18
  106.2 4.9 %all-to-all-start.3 = ((f32[16,32,256]{2,1,0:T(8,128)}), f32[16,32,256]{2,1,0:T(8,128)S(1)}, u32[]{:S(2)}, u32[]{:S(2)}) async-start(f32[16,32,256]{2,1,0:T(8,128)} %bitcast.5), calls=%async_computation.3 | async-start | bytes 1048576 | tf_op jit(solution)/shard_map/all_to_all | solution.py:33
  112.1 5.4 %collective-permute-start.4 = (f32[256,256]{0,1:T(8,128)S(1)}, f32[256,256]{0,1:T(8,128)S(1)}, u32[]{:S(2)}, u32[]{:S(2)}) collective-permute-start(f32[256,256]{0,1:T(8,128)S(1)} %fusion.63), channel_id=1, source_target_pairs={{0,128},{16,144},{32,160},{48,176},{64,192},{80,208},{96,224},{112... | collective-permute-start | bytes 786440 | tf_op jit(solution)/shard_map/ppermute | solution.py:53
  117.5 22.6 %collective-permute-done.4 = f32[256,256]{0,1:T(8,128)S(1)} collective-permute-done((f32[256,256]{0,1:T(8,128)S(1)}, f32[256,256]{0,1:T(8,128)S(1)}, u32[]{:S(2)}, u32[]{:S(2)}) %collective-permute-start.4) | collective-permute-done | bytes 262176 | tf_op jit(solution)/shard_map/ppermute | solution.py:53
  142.9 6.1 %collective-permute-done.5 = f32[256,256]{0,1:T(8,128)S(1)} collective-permute-done((f32[256,256]{0,1:T(8,128)S(1)}, f32[256,256]{0,1:T(8,128)S(1)}, u32[]{:S(2)}, u32[]{:S(2)}) %collective-permute-start.5) | collective-permute-done | bytes 262176 | tf_op jit(solution)/shard_map/ppermute | solution.py:53
  150.3 5.1 %collective-permute-done.6 = f32[256,256]{0,1:T(8,128)S(1)} collective-permute-done((f32[256,256]{0,1:T(8,128)S(1)}, f32[256,256]{0,1:T(8,128)S(1)}, u32[]{:S(2)}, u32[]{:S(2)}) %collective-permute-start.6) | collective-permute-done | bytes 262176 | tf_op jit(solution)/shard_map/ppermute | solution.py:53
  158.9 5.0 %all-to-all-start.4 = ((f32[16,32,256]{2,1,0:T(8,128)}), f32[16,32,256]{2,1,0:T(8,128)S(1)}, u32[]{:S(2)}, u32[]{:S(2)}) async-start(f32[16,32,256]{2,1,0:T(8,128)} %broadcast_in_dim.12), calls=%async_computation.4 | async-start | bytes 1048576 | tf_op jit(solution)/shard_map/all_to_all | solution.py:18
  190.1 5.7 %all-to-all-start.5 = ((f32[16,32,256]{2,1,0:T(8,128)}), f32[16,32,256]{2,1,0:T(8,128)S(1)}, u32[]{:S(2)}, u32[]{:S(2)}) async-start(f32[16,32,256]{2,1,0:T(8,128)} %bitcast.336), calls=%async_computation.5 | async-start | bytes 1048576 | tf_op jit(solution)/shard_map/all_to_all | solution.py:33
  199.6 11.4 %collective-permute-done.8 = f32[256,256]{0,1:T(8,128)S(1)} collective-permute-done((f32[256,256]{0,1:T(8,128)S(1)}, f32[256,256]{0,1:T(8,128)S(1)}, u32[]{:S(2)}, u32[]{:S(2)}) %collective-permute-start.8) | collective-permute-done | bytes 262176 | tf_op jit(solution)/shard_map/ppermute | solution.py:53
  211.2 7.2 %collective-permute-done.9 = f32[256,256]{0,1:T(8,128)S(1)} collective-permute-done((f32[256,256]{0,1:T(8,128)S(1)}, f32[256,256]{0,1:T(8,128)S(1)}, u32[]{:S(2)}, u32[]{:S(2)}) %collective-permute-start.9) | collective-permute-done | bytes 262176 | tf_op jit(solution)/shard_map/ppermute | solution.py:53
  218.6 10.7 %collective-permute-done.10 = f32[256,256]{0,1:T(8,128)S(1)} collective-permute-done((f32[256,256]{0,1:T(8,128)S(1)}, f32[256,256]{0,1:T(8,128)S(1)}, u32[]{:S(2)}, u32[]{:S(2)}) %collective-permute-start.10) | collective-permute-done | bytes 262176 | tf_op jit(solution)/shard_map/ppermute | solution.py:53
  263.4 6.2 %collective-permute-start.12 = (f32[256,256]{0,1:T(8,128)}, f32[256,256]{0,1:T(8,128)}, u32[]{:S(2)}, u32[]{:S(2)}) collective-permute-start(f32[256,256]{0,1:T(8,128)} %fusion.103), channel_id=1, source_target_pairs={{0,128},{16,144},{32,160},{48,176},{64,192},{80,208},{96,224},{112... | collective-permute-start | bytes 786440 | tf_op jit(solution)/shard_map/ppermute | solution.py:53
  272.3 5.7 %all-to-all-start.7 = ((f32[16,32,256]{2,1,0:T(8,128)}), f32[16,32,256]{2,1,0:T(8,128)S(1)}, u32[]{:S(2)}, u32[]{:S(2)}) async-start(f32[16,32,256]{2,1,0:T(8,128)} %bitcast.335), calls=%async_computation.7 | async-start | bytes 1048576 | tf_op jit(solution)/shard_map/all_to_all | solution.py:33
  285.7 8.4 %collective-permute-done.13 = f32[256,256]{0,1:T(8,128)S(1)} collective-permute-done((f32[256,256]{0,1:T(8,128)S(1)}, f32[256,256]{0,1:T(8,128)S(1)}, u32[]{:S(2)}, u32[]{:S(2)}) %collective-permute-start.13) | collective-permute-done | bytes 262176 | tf_op jit(solution)/shard_map/ppermute | solution.py:53
  295.5 5.6 %collective-permute-done.14 = f32[256,256]{0,1:T(8,128)S(1)} collective-permute-done((f32[256,256]{0,1:T(8,128)S(1)}, f32[256,256]{0,1:T(8,128)S(1)}, u32[]{:S(2)}, u32[]{:S(2)}) %collective-permute-start.14) | collective-permute-done | bytes 262176 | tf_op jit(solution)/shard_map/ppermute | solution.py:53
  306.1 10.3 %all-to-all-start.8 = ((f32[16,32,256]{2,1,0:T(8,128)}), f32[16,32,256]{2,1,0:T(8,128)S(1)}, u32[]{:S(2)}, u32[]{:S(2)}) async-start(f32[16,32,256]{2,1,0:T(8,128)} %broadcast_in_dim.14), calls=%async_computation.8 | async-start | bytes 1048576 | tf_op jit(solution)/shard_map/all_to_all | solution.py:18
  338.5 4.9 %add_subtract_fusion = (f32[512,512]{1,0:T(8,128)}, f32[512,512]{1,0:T(8,128)}) fusion(f32[512,512]{1,0:T(8,128)} %get-tuple-element.23, f32[512,512]{1,0:T(8,128)S(1)} %copy-done, s32[512,512]{1,0:T(8,128)} %param.8, f32[512,256]{1,0:T(8,128)S(1)} %fusion.101, f32[512,256]{1,0:T(8,128)S(1)} %fusion.121), kind=kOutput, calls=%fused_computation.75 | convolution fusion | flops 810024960 | bytes 6291456 | tf_op jit(solution)/shard_map/dot_general | solution.py:73
  (242 shorter events, 143.6 us)
Async XLA Ops:
  2.3 29.1 %all-to-all-start = ((f32[16,32,256]{2,1,0:T(8,128)}), f32[16,32,256]{2,1,0:T(8,128)S(1)}, u32[]{:S(2)}, u32[]{:S(2)}) async-start(f32[16,32,256]{2,1,0:T(8,128)} %broadcast_in_dim.10), calls=%async_computation | async-start | bytes 1048576 | tf_op jit(solution)/shard_map/all_to_all | solution.py:18
  33.3 42.5 %all-to-all-start.1 = ((f32[16,32,256]{2,1,0:T(8,128)}), f32[16,32,256]{2,1,0:T(8,128)S(1)}, u32[]{:S(2)}, u32[]{:S(2)}) async-start(f32[16,32,256]{2,1,0:T(8,128)} %fusion.43), calls=%async_computation.1 | async-start | bytes 1048576 | tf_op jit(solution)/shard_map/all_to_all | solution.py:33
  40.5 12.7 %collective-permute-start = (f32[256,256]{0,1:T(8,128)S(1)}, f32[256,256]{0,1:T(8,128)S(1)}, u32[]{:S(2)}, u32[]{:S(2)}) collective-permute-start(f32[256,256]{0,1:T(8,128)S(1)} %convolution_bitcast_fusion), channel_id=1, source_target_pairs={{0,8},{1,9},{2,10},{3,11},{4,12},{5,13},{6,14},{7,15},{8,0},{9,1},... | collective-permute-start | bytes 786440 | tf_op jit(solution)/shard_map/ppermute | solution.py:53
  53.2 6.5 %collective-permute-start.1 = (f32[256,256]{0,1:T(8,128)S(1)}, f32[256,256]{0,1:T(8,128)S(1)}, u32[]{:S(2)}, u32[]{:S(2)}) collective-permute-start(f32[256,256]{0,1:T(8,128)S(1)} %add.116), channel_id=1, source_target_pairs={{0,4},{1,5},{2,6},{3,7},{4,0},{5,1},{6,2},{7,3},{8,12},{9,13},{10,... | collective-permute-start | bytes 786440 | tf_op jit(solution)/shard_map/ppermute | solution.py:53
  59.8 11.3 %collective-permute-start.2 = (f32[256,256]{0,1:T(8,128)S(1)}, f32[256,256]{0,1:T(8,128)S(1)}, u32[]{:S(2)}, u32[]{:S(2)}) collective-permute-start(f32[256,256]{0,1:T(8,128)S(1)} %add.117), channel_id=1, source_target_pairs={{0,2},{1,3},{2,0},{3,1},{4,6},{5,7},{6,4},{7,5},{8,10},{9,11},{10,... | collective-permute-start | bytes 786440 | tf_op jit(solution)/shard_map/ppermute | solution.py:53
  71.1 11.8 %collective-permute-start.3 = (f32[256,256]{0,1:T(8,128)S(1)}, f32[256,256]{0,1:T(8,128)S(1)}, u32[]{:S(2)}, u32[]{:S(2)}) collective-permute-start(f32[256,256]{0,1:T(8,128)S(1)} %add.118), channel_id=1, source_target_pairs={{0,1},{1,0},{2,3},{3,2},{4,5},{5,4},{6,7},{7,6},{8,9},{9,8},{10,11... | collective-permute-start | bytes 786440 | tf_op jit(solution)/shard_map/ppermute | solution.py:53
  76.7 26.2 %all-to-all-start.2 = ((f32[16,32,256]{2,1,0:T(8,128)}), f32[16,32,256]{2,1,0:T(8,128)S(1)}, u32[]{:S(2)}, u32[]{:S(2)}) async-start(f32[16,32,256]{2,1,0:T(8,128)} %broadcast_in_dim.11), calls=%async_computation.2 | async-start | bytes 1048576 | tf_op jit(solution)/shard_map/all_to_all | solution.py:18
  106.2 51.8 %all-to-all-start.3 = ((f32[16,32,256]{2,1,0:T(8,128)}), f32[16,32,256]{2,1,0:T(8,128)S(1)}, u32[]{:S(2)}, u32[]{:S(2)}) async-start(f32[16,32,256]{2,1,0:T(8,128)} %bitcast.5), calls=%async_computation.3 | async-start | bytes 1048576 | tf_op jit(solution)/shard_map/all_to_all | solution.py:33
  112.1 28.0 %collective-permute-start.4 = (f32[256,256]{0,1:T(8,128)S(1)}, f32[256,256]{0,1:T(8,128)S(1)}, u32[]{:S(2)}, u32[]{:S(2)}) collective-permute-start(f32[256,256]{0,1:T(8,128)S(1)} %fusion.63), channel_id=1, source_target_pairs={{0,128},{16,144},{32,160},{48,176},{64,192},{80,208},{96,224},{112... | collective-permute-start | bytes 786440 | tf_op jit(solution)/shard_map/ppermute | solution.py:53
  140.1 8.8 %collective-permute-start.5 = (f32[256,256]{0,1:T(8,128)S(1)}, f32[256,256]{0,1:T(8,128)S(1)}, u32[]{:S(2)}, u32[]{:S(2)}) collective-permute-start(f32[256,256]{0,1:T(8,128)S(1)} %add.122), channel_id=1, source_target_pairs={{0,64},{16,80},{32,96},{48,112},{64,0},{80,16},{96,32},{112,48},{1... | collective-permute-start | bytes 786440 | tf_op jit(solution)/shard_map/ppermute | solution.py:53
  155.5 8.4 %collective-permute-start.7 = (f32[256,256]{0,1:T(8,128)S(1)}, f32[256,256]{0,1:T(8,128)S(1)}, u32[]{:S(2)}, u32[]{:S(2)}) collective-permute-start(f32[256,256]{0,1:T(8,128)S(1)} %add.124), channel_id=1, source_target_pairs={{0,16},{16,0},{32,48},{48,32},{64,80},{80,64},{96,112},{112,96},{1... | collective-permute-start | bytes 786440 | tf_op jit(solution)/shard_map/ppermute | solution.py:53
  158.9 25.0 %all-to-all-start.4 = ((f32[16,32,256]{2,1,0:T(8,128)}), f32[16,32,256]{2,1,0:T(8,128)S(1)}, u32[]{:S(2)}, u32[]{:S(2)}) async-start(f32[16,32,256]{2,1,0:T(8,128)} %broadcast_in_dim.12), calls=%async_computation.4 | async-start | bytes 1048576 | tf_op jit(solution)/shard_map/all_to_all | solution.py:18
  190.1 44.1 %all-to-all-start.5 = ((f32[16,32,256]{2,1,0:T(8,128)}), f32[16,32,256]{2,1,0:T(8,128)S(1)}, u32[]{:S(2)}, u32[]{:S(2)}) async-start(f32[16,32,256]{2,1,0:T(8,128)} %bitcast.336), calls=%async_computation.5 | async-start | bytes 1048576 | tf_op jit(solution)/shard_map/all_to_all | solution.py:33
  196.9 14.2 %collective-permute-start.8 = (f32[256,256]{0,1:T(8,128)S(1)}, f32[256,256]{0,1:T(8,128)S(1)}, u32[]{:S(2)}, u32[]{:S(2)}) collective-permute-start(f32[256,256]{0,1:T(8,128)S(1)} %fusion.83), channel_id=1, source_target_pairs={{0,8},{1,9},{2,10},{3,11},{4,12},{5,13},{6,14},{7,15},{8,0},{9,1},... | collective-permute-start | bytes 786440 | tf_op jit(solution)/shard_map/ppermute | solution.py:53
  211.1 7.4 %collective-permute-start.9 = (f32[256,256]{0,1:T(8,128)S(1)}, f32[256,256]{0,1:T(8,128)S(1)}, u32[]{:S(2)}, u32[]{:S(2)}) collective-permute-start(f32[256,256]{0,1:T(8,128)S(1)} %add.133), channel_id=1, source_target_pairs={{0,4},{1,5},{2,6},{3,7},{4,0},{5,1},{6,2},{7,3},{8,12},{9,13},{10,... | collective-permute-start | bytes 786440 | tf_op jit(solution)/shard_map/ppermute | solution.py:53
  218.5 10.8 %collective-permute-start.10 = (f32[256,256]{0,1:T(8,128)S(1)}, f32[256,256]{0,1:T(8,128)S(1)}, u32[]{:S(2)}, u32[]{:S(2)}) collective-permute-start(f32[256,256]{0,1:T(8,128)S(1)} %add.134), channel_id=1, source_target_pairs={{0,2},{1,3},{2,0},{3,1},{4,6},{5,7},{6,4},{7,5},{8,10},{9,11},{10,... | collective-permute-start | bytes 786440 | tf_op jit(solution)/shard_map/ppermute | solution.py:53
  230.0 10.1 %collective-permute-start.11 = (f32[256,256]{0,1:T(8,128)}, f32[256,256]{0,1:T(8,128)}, u32[]{:S(2)}, u32[]{:S(2)}) collective-permute-start(f32[256,256]{0,1:T(8,128)} %add.135), channel_id=1, source_target_pairs={{0,1},{1,0},{2,3},{3,2},{4,5},{5,4},{6,7},{7,6},{8,9},{9,8},{10,11... | collective-permute-start | bytes 786440 | tf_op jit(solution)/shard_map/ppermute | solution.py:53
  236.0 25.1 %all-to-all-start.6 = ((f32[16,32,256]{2,1,0:T(8,128)}), f32[16,32,256]{2,1,0:T(8,128)S(1)}, u32[]{:S(2)}, u32[]{:S(2)}) async-start(f32[16,32,256]{2,1,0:T(8,128)} %broadcast_in_dim.13), calls=%async_computation.6 | async-start | bytes 1048576 | tf_op jit(solution)/shard_map/all_to_all | solution.py:18
  263.4 18.2 %collective-permute-start.12 = (f32[256,256]{0,1:T(8,128)}, f32[256,256]{0,1:T(8,128)}, u32[]{:S(2)}, u32[]{:S(2)}) collective-permute-start(f32[256,256]{0,1:T(8,128)} %fusion.103), channel_id=1, source_target_pairs={{0,128},{16,144},{32,160},{48,176},{64,192},{80,208},{96,224},{112... | collective-permute-start | bytes 786440 | tf_op jit(solution)/shard_map/ppermute | solution.py:53
  272.3 31.8 %all-to-all-start.7 = ((f32[16,32,256]{2,1,0:T(8,128)}), f32[16,32,256]{2,1,0:T(8,128)S(1)}, u32[]{:S(2)}, u32[]{:S(2)}) async-start(f32[16,32,256]{2,1,0:T(8,128)} %bitcast.335), calls=%async_computation.7 | async-start | bytes 1048576 | tf_op jit(solution)/shard_map/all_to_all | solution.py:33
  282.7 11.5 %collective-permute-start.13 = (f32[256,256]{0,1:T(8,128)S(1)}, f32[256,256]{0,1:T(8,128)S(1)}, u32[]{:S(2)}, u32[]{:S(2)}) collective-permute-start(f32[256,256]{0,1:T(8,128)S(1)} %add.140), channel_id=1, source_target_pairs={{0,64},{16,80},{32,96},{48,112},{64,0},{80,16},{96,32},{112,48},{1... | collective-permute-start | bytes 786440 | tf_op jit(solution)/shard_map/ppermute | solution.py:53
  294.2 6.8 %collective-permute-start.14 = (f32[256,256]{0,1:T(8,128)S(1)}, f32[256,256]{0,1:T(8,128)S(1)}, u32[]{:S(2)}, u32[]{:S(2)}) collective-permute-start(f32[256,256]{0,1:T(8,128)S(1)} %add.141), channel_id=1, source_target_pairs={{0,32},{16,48},{32,0},{48,16},{64,96},{80,112},{96,64},{112,80},{1... | collective-permute-start | bytes 786440 | tf_op jit(solution)/shard_map/ppermute | solution.py:53
  301.1 15.2 %collective-permute-start.15 = (f32[256,256]{0,1:T(8,128)S(1)}, f32[256,256]{0,1:T(8,128)}, u32[]{:S(2)}, u32[]{:S(2)}) collective-permute-start(f32[256,256]{0,1:T(8,128)S(1)} %add.142), channel_id=1, source_target_pairs={{0,16},{16,0},{32,48},{48,32},{64,80},{80,64},{96,112},{112,96},{1... | collective-permute-start | bytes 786440 | tf_op jit(solution)/shard_map/ppermute | solution.py:53
  306.1 31.9 %all-to-all-start.8 = ((f32[16,32,256]{2,1,0:T(8,128)}), f32[16,32,256]{2,1,0:T(8,128)S(1)}, u32[]{:S(2)}, u32[]{:S(2)}) async-start(f32[16,32,256]{2,1,0:T(8,128)} %broadcast_in_dim.14), calls=%async_computation.8 | async-start | bytes 1048576 | tf_op jit(solution)/shard_map/all_to_all | solution.py:18
  (12 other events, 48.9 us)

commit v9 on v8

--- a/solution.py
+++ b/solution.py
@@ -48,10 +48,9 @@
 
 def exchanged_sum(x, axis):
     count = lax.axis_size(axis)
-    bit = count // 2
-    while bit >= 1:
+    bits = [1 << j for j in range(count.bit_length() - 1)]
+    for bit in bits if axis == "doc" else bits[::-1]:
         x = x + lax.ppermute(x, axis, [(i, i ^ bit) for i in range(count)])
-        bit //= 2
     return x
 
 

time: 351 us -> 339 us (0.966)
  the two profiles are of different devices: /device:TPU:65 before, /device:TPU:164 now
where the time goes in v9:
time: 339 us; the launch traced here: 334 us
  waiting for transfers between devices  114 us (34%)
  matrix products  100 us (29%)
  starting transfers between devices  98.9 us (29%)
  other arithmetic  8.4 us (2%)
  local copies, waits for them, and re-layouts  6.79 us (2%)
  between operations  5.05 us (1%)
    ppermute x16, waiting for transfers between devices, exchanged_sum(): x = x + lax.ppermute(x, axis, [(i, i ^ bit) for i in range(count)])  103 us
    dot_general x154, matrix products, product(): jnp.dot(left, right, precision=lax.Precision.HIGHEST, preferred_element_t...  81.8 us
    all_to_all x5, starting transfers between devices, copy_for_each(): lax.all_to_all(jnp.broadcast_to(x[None], (count, *x.shape)), axis, 0, 0,...  42.6 us
    all_to_all x4, starting transfers between devices, summed_on_arrival(): pieces = lax.all_to_all(split_up(x, dim, count), axis, 0, 0, tiled=True)  35.2 us
    ppermute x16, starting transfers between devices, exchanged_sum(): x = x + lax.ppermute(x, axis, [(i, i ^ bit) for i in range(count)])  21.2 us
    all_to_all x5, waiting for transfers between devices, copy_for_each(): lax.all_to_all(jnp.broadcast_to(x[None], (count, *x.shape)), axis, 0, 0,...  10.7 us
    dot_general x6, matrix products, product_left(): lax.dot_general(left, right, (((0,), (0,)), ((), ())), precision=lax.Prec...  9.89 us
    dot_general x2, matrix products, product_right(): lax.dot_general(left, right, (((1,), (1,)), ((), ())), precision=lax.Prec...  8.63 us
  transfers between devices with their start and end apart: 25, of which 14 were waited for; matrix products, arithmetic and copies ran while one was open for 28% of the time, Pallas kernels for 0%

profile of v9, /device:TPU:164, one launch (start us, length us, event | category | flops | bytes accessed | tf_op | source)
XLA Modules:
  0.0 333.6 jit_solution(10882247579211348414)
XLA Ops:
  2.3 9.6 %all-to-all-start = ((f32[16,32,256]{2,1,0:T(8,128)}), f32[16,32,256]{2,1,0:T(8,128)S(1)}, u32[]{:S(2)}, u32[]{:S(2)}) async-start(f32[16,32,256]{2,1,0:T(8,128)} %broadcast_in_dim.10), calls=%async_computation | async-start | bytes 1048576 | tf_op jit(solution)/shard_map/all_to_all | solution.py:18
  13.4 10.7 %all-to-all-done = f32[16,32,256]{2,1,0:T(8,128)S(1)} async-done(((f32[16,32,256]{2,1,0:T(8,128)}), f32[16,32,256]{2,1,0:T(8,128)S(1)}, u32[]{:S(2)}, u32[]{:S(2)}) %all-to-all-start) | async-done | bytes 524320 | tf_op jit(solution)/shard_map/all_to_all | solution.py:18
  25.9 6.4 %all-to-all-start.1 = ((f32[16,32,256]{2,1,0:T(8,128)}), f32[16,32,256]{2,1,0:T(8,128)S(1)}, u32[]{:S(2)}, u32[]{:S(2)}) async-start(f32[16,32,256]{2,1,0:T(8,128)} %fusion.43), calls=%async_computation.1 | async-start | bytes 1048576 | tf_op jit(solution)/shard_map/all_to_all | solution.py:33
  36.4 11.2 %collective-permute-done = f32[256,256]{0,1:T(8,128)S(1)} collective-permute-done((f32[256,256]{0,1:T(8,128)S(1)}, f32[256,256]{0,1:T(8,128)S(1)}, u32[]{:S(2)}, u32[]{:S(2)}) %collective-permute-start) | collective-permute-done | bytes 262176 | tf_op jit(solution)/shard_map/ppermute | solution.py:53
  48.6 7.0 %collective-permute-done.1 = f32[256,256]{0,1:T(8,128)S(1)} collective-permute-done((f32[256,256]{0,1:T(8,128)S(1)}, f32[256,256]{0,1:T(8,128)S(1)}, u32[]{:S(2)}, u32[]{:S(2)}) %collective-permute-start.1) | collective-permute-done | bytes 262176 | tf_op jit(solution)/shard_map/ppermute | solution.py:53
  57.9 10.1 %collective-permute-done.2 = f32[256,256]{0,1:T(8,128)S(1)} collective-permute-done((f32[256,256]{0,1:T(8,128)S(1)}, f32[256,256]{0,1:T(8,128)S(1)}, u32[]{:S(2)}, u32[]{:S(2)}) %collective-permute-start.2) | collective-permute-done | bytes 262176 | tf_op jit(solution)/shard_map/ppermute | solution.py:53
  70.9 5.1 %all-to-all-start.2 = ((f32[16,32,256]{2,1,0:T(8,128)}), f32[16,32,256]{2,1,0:T(8,128)S(1)}, u32[]{:S(2)}, u32[]{:S(2)}) async-start(f32[16,32,256]{2,1,0:T(8,128)} %broadcast_in_dim.11), calls=%async_computation.2 | async-start | bytes 1048576 | tf_op jit(solution)/shard_map/all_to_all | solution.py:18
  99.3 10.8 %all-to-all-start.3 = ((f32[16,32,256]{2,1,0:T(8,128)}), f32[16,32,256]{2,1,0:T(8,128)S(1)}, u32[]{:S(2)}, u32[]{:S(2)}) async-start(f32[16,32,256]{2,1,0:T(8,128)} %bitcast.5), calls=%async_computation.3 | async-start | bytes 1048576 | tf_op jit(solution)/shard_map/all_to_all | solution.py:33
  114.0 9.6 %collective-permute-done.5 = f32[256,256]{0,1:T(8,128)S(1)} collective-permute-done((f32[256,256]{0,1:T(8,128)S(1)}, f32[256,256]{0,1:T(8,128)S(1)}, u32[]{:S(2)}, u32[]{:S(2)}) %collective-permute-start.5) | collective-permute-done | bytes 262176 | tf_op jit(solution)/shard_map/ppermute | solution.py:53
  124.5 9.0 %collective-permute-done.6 = f32[256,256]{0,1:T(8,128)S(1)} collective-permute-done((f32[256,256]{0,1:T(8,128)S(1)}, f32[256,256]{0,1:T(8,128)S(1)}, u32[]{:S(2)}, u32[]{:S(2)}) %collective-permute-start.6) | collective-permute-done | bytes 262176 | tf_op jit(solution)/shard_map/ppermute | solution.py:53
  135.2 9.8 %all-to-all-start.4 = ((f32[16,32,256]{2,1,0:T(8,128)}), f32[16,32,256]{2,1,0:T(8,128)S(1)}, u32[]{:S(2)}, u32[]{:S(2)}) async-start(f32[16,32,256]{2,1,0:T(8,128)} %broadcast_in_dim.12), calls=%async_computation.4 | async-start | bytes 1048576 | tf_op jit(solution)/shard_map/all_to_all | solution.py:18
  145.0 7.0 %collective-permute-done.7 = f32[256,256]{0,1:T(8,128)S(1)} collective-permute-done((f32[256,256]{0,1:T(8,128)S(1)}, f32[256,256]{0,1:T(8,128)S(1)}, u32[]{:S(2)}, u32[]{:S(2)}) %collective-permute-start.7) | collective-permute-done | bytes 262176 | tf_op jit(solution)/shard_map/ppermute | solution.py:53
  172.6 3.8 %fusion = (f32[512,512]{1,0:T(8,128)S(1)}, f32[512,512]{1,0:T(8,128)}) fusion(s32[512,512]{1,0:T(8,128)} %param.8, f32[512,512]{1,0:T(8,128)S(1)} %copy-done, f32[512,256]{1,0:T(8,128)S(1)} %fusion.61, f32[512,256]{1,0:T(8,128)S(1)} %fusion.81), kind=kOutput, calls=%fused_computation.84 | convolution fusion | flops 808189952 | bytes 5242880 | tf_op jit(solution)/shard_map/dot_general | solution.py:72
  178.1 7.3 %all-to-all-start.5 = ((f32[16,32,256]{2,1,0:T(8,128)}), f32[16,32,256]{2,1,0:T(8,128)S(1)}, u32[]{:S(2)}, u32[]{:S(2)}) async-start(f32[16,32,256]{2,1,0:T(8,128)} %bitcast.336), calls=%async_computation.5 | async-start | bytes 1048576 | tf_op jit(solution)/shard_map/all_to_all | solution.py:33
  189.5 7.8 %collective-permute-done.8 = f32[256,256]{0,1:T(8,128)S(1)} collective-permute-done((f32[256,256]{0,1:T(8,128)S(1)}, f32[256,256]{0,1:T(8,128)S(1)}, u32[]{:S(2)}, u32[]{:S(2)}) %collective-permute-start.8) | collective-permute-done | bytes 262176 | tf_op jit(solution)/shard_map/ppermute | solution.py:53
  198.7 5.1 %collective-permute-done.9 = f32[256,256]{0,1:T(8,128)S(1)} collective-permute-done((f32[256,256]{0,1:T(8,128)S(1)}, f32[256,256]{0,1:T(8,128)S(1)}, u32[]{:S(2)}, u32[]{:S(2)}) %collective-permute-start.9) | collective-permute-done | bytes 262176 | tf_op jit(solution)/shard_map/ppermute | solution.py:53
  205.4 6.4 %collective-permute-done.10 = f32[256,256]{0,1:T(8,128)S(1)} collective-permute-done((f32[256,256]{0,1:T(8,128)S(1)}, f32[256,256]{0,1:T(8,128)S(1)}, u32[]{:S(2)}, u32[]{:S(2)}) %collective-permute-start.10) | collective-permute-done | bytes 262176 | tf_op jit(solution)/shard_map/ppermute | solution.py:53
  216.8 7.8 %all-to-all-start.6 = ((f32[16,32,256]{2,1,0:T(8,128)}), f32[16,32,256]{2,1,0:T(8,128)S(1)}, u32[]{:S(2)}, u32[]{:S(2)}) async-start(f32[16,32,256]{2,1,0:T(8,128)} %broadcast_in_dim.13), calls=%async_computation.6 | async-start | bytes 1048576 | tf_op jit(solution)/shard_map/all_to_all | solution.py:18
  250.4 10.7 %all-to-all-start.7 = ((f32[16,32,256]{2,1,0:T(8,128)}), f32[16,32,256]{2,1,0:T(8,128)S(1)}, u32[]{:S(2)}, u32[]{:S(2)}) async-start(f32[16,32,256]{2,1,0:T(8,128)} %bitcast.335), calls=%async_computation.7 | async-start | bytes 1048576 | tf_op jit(solution)/shard_map/all_to_all | solution.py:33
  263.5 11.3 %collective-permute-done.13 = f32[256,256]{0,1:T(8,128)S(1)} collective-permute-done((f32[256,256]{0,1:T(8,128)S(1)}, f32[256,256]{0,1:T(8,128)S(1)}, u32[]{:S(2)}, u32[]{:S(2)}) %collective-permute-start.13) | collective-permute-done | bytes 262176 | tf_op jit(solution)/shard_map/ppermute | solution.py:53
  275.4 9.3 %collective-permute-done.14 = f32[256,256]{0,1:T(8,128)S(1)} collective-permute-done((f32[256,256]{0,1:T(8,128)S(1)}, f32[256,256]{0,1:T(8,128)S(1)}, u32[]{:S(2)}, u32[]{:S(2)}) %collective-permute-start.14) | collective-permute-done | bytes 262176 | tf_op jit(solution)/shard_map/ppermute | solution.py:53
  287.7 10.3 %all-to-all-start.8 = ((f32[16,32,256]{2,1,0:T(8,128)}), f32[16,32,256]{2,1,0:T(8,128)S(1)}, u32[]{:S(2)}, u32[]{:S(2)}) async-start(f32[16,32,256]{2,1,0:T(8,128)} %broadcast_in_dim.14), calls=%async_computation.8 | async-start | bytes 1048576 | tf_op jit(solution)/shard_map/all_to_all | solution.py:18
  298.0 8.3 %collective-permute-done.15 = f32[256,256]{0,1:T(8,128)} collective-permute-done((f32[256,256]{0,1:T(8,128)S(1)}, f32[256,256]{0,1:T(8,128)}, u32[]{:S(2)}, u32[]{:S(2)}) %collective-permute-start.15) | collective-permute-done | bytes 262176 | tf_op jit(solution)/shard_map/ppermute | solution.py:53
  328.5 4.9 %add_subtract_fusion = (f32[512,512]{1,0:T(8,128)}, f32[512,512]{1,0:T(8,128)}) fusion(f32[512,512]{1,0:T(8,128)} %get-tuple-element.23, f32[512,512]{1,0:T(8,128)S(1)} %copy-done, s32[512,512]{1,0:T(8,128)} %param.8, f32[512,256]{1,0:T(8,128)S(1)} %fusion.101, f32[512,256]{1,0:T(8,128)S(1)} %fusion.121), kind=kOutput, calls=%fused_computation.75 | convolution fusion | flops 810024960 | bytes 6291456 | tf_op jit(solution)/shard_map/dot_general | solution.py:72
  (242 shorter events, 129.5 us)
Async XLA Ops:
  2.3 21.8 %all-to-all-start = ((f32[16,32,256]{2,1,0:T(8,128)}), f32[16,32,256]{2,1,0:T(8,128)S(1)}, u32[]{:S(2)}, u32[]{:S(2)}) async-start(f32[16,32,256]{2,1,0:T(8,128)} %broadcast_in_dim.10), calls=%async_computation | async-start | bytes 1048576 | tf_op jit(solution)/shard_map/all_to_all | solution.py:18
  25.9 44.1 %all-to-all-start.1 = ((f32[16,32,256]{2,1,0:T(8,128)}), f32[16,32,256]{2,1,0:T(8,128)S(1)}, u32[]{:S(2)}, u32[]{:S(2)}) async-start(f32[16,32,256]{2,1,0:T(8,128)} %fusion.43), calls=%async_computation.1 | async-start | bytes 1048576 | tf_op jit(solution)/shard_map/all_to_all | solution.py:33
  33.3 14.2 %collective-permute-start = (f32[256,256]{0,1:T(8,128)S(1)}, f32[256,256]{0,1:T(8,128)S(1)}, u32[]{:S(2)}, u32[]{:S(2)}) collective-permute-start(f32[256,256]{0,1:T(8,128)S(1)} %convolution_bitcast_fusion), channel_id=1, source_target_pairs={{0,8},{1,9},{2,10},{3,11},{4,12},{5,13},{6,14},{7,15},{8,0},{9,1},... | collective-permute-start | bytes 786440 | tf_op jit(solution)/shard_map/ppermute | solution.py:53
  47.6 8.0 %collective-permute-start.1 = (f32[256,256]{0,1:T(8,128)S(1)}, f32[256,256]{0,1:T(8,128)S(1)}, u32[]{:S(2)}, u32[]{:S(2)}) collective-permute-start(f32[256,256]{0,1:T(8,128)S(1)} %add.116), channel_id=1, source_target_pairs={{0,4},{1,5},{2,6},{3,7},{4,0},{5,1},{6,2},{7,3},{8,12},{9,13},{10,... | collective-permute-start | bytes 786440 | tf_op jit(solution)/shard_map/ppermute | solution.py:53
  55.6 12.4 %collective-permute-start.2 = (f32[256,256]{0,1:T(8,128)S(1)}, f32[256,256]{0,1:T(8,128)S(1)}, u32[]{:S(2)}, u32[]{:S(2)}) collective-permute-start(f32[256,256]{0,1:T(8,128)S(1)} %add.117), channel_id=1, source_target_pairs={{0,2},{1,3},{2,0},{3,1},{4,6},{5,7},{6,4},{7,5},{8,10},{9,11},{10,... | collective-permute-start | bytes 786440 | tf_op jit(solution)/shard_map/ppermute | solution.py:53
  68.1 7.9 %collective-permute-start.3 = (f32[256,256]{0,1:T(8,128)S(1)}, f32[256,256]{0,1:T(8,128)S(1)}, u32[]{:S(2)}, u32[]{:S(2)}) collective-permute-start(f32[256,256]{0,1:T(8,128)S(1)} %add.118), channel_id=1, source_target_pairs={{0,1},{1,0},{2,3},{3,2},{4,5},{5,4},{6,7},{7,6},{8,9},{9,8},{10,11... | collective-permute-start | bytes 786440 | tf_op jit(solution)/shard_map/ppermute | solution.py:53
  70.9 25.1 %all-to-all-start.2 = ((f32[16,32,256]{2,1,0:T(8,128)}), f32[16,32,256]{2,1,0:T(8,128)S(1)}, u32[]{:S(2)}, u32[]{:S(2)}) async-start(f32[16,32,256]{2,1,0:T(8,128)} %broadcast_in_dim.11), calls=%async_computation.2 | async-start | bytes 1048576 | tf_op jit(solution)/shard_map/all_to_all | solution.py:18
  99.3 34.4 %all-to-all-start.3 = ((f32[16,32,256]{2,1,0:T(8,128)}), f32[16,32,256]{2,1,0:T(8,128)S(1)}, u32[]{:S(2)}, u32[]{:S(2)}) async-start(f32[16,32,256]{2,1,0:T(8,128)} %bitcast.5), calls=%async_computation.3 | async-start | bytes 1048576 | tf_op jit(solution)/shard_map/all_to_all | solution.py:33
  112.7 10.9 %collective-permute-start.5 = (f32[256,256]{0,1:T(8,128)S(1)}, f32[256,256]{0,1:T(8,128)S(1)}, u32[]{:S(2)}, u32[]{:S(2)}) collective-permute-start(f32[256,256]{0,1:T(8,128)S(1)} %add.122), channel_id=1, source_target_pairs={{0,32},{16,48},{32,0},{48,16},{64,96},{80,112},{96,64},{112,80},{1... | collective-permute-start | bytes 786440 | tf_op jit(solution)/shard_map/ppermute | solution.py:53
  123.6 9.9 %collective-permute-start.6 = (f32[256,256]{0,1:T(8,128)S(1)}, f32[256,256]{0,1:T(8,128)S(1)}, u32[]{:S(2)}, u32[]{:S(2)}) collective-permute-start(f32[256,256]{0,1:T(8,128)S(1)} %add.123), channel_id=1, source_target_pairs={{0,64},{16,80},{32,96},{48,112},{64,0},{80,16},{96,32},{112,48},{1... | collective-permute-start | bytes 786440 | tf_op jit(solution)/shard_map/ppermute | solution.py:53
  133.6 18.4 %collective-permute-start.7 = (f32[256,256]{0,1:T(8,128)S(1)}, f32[256,256]{0,1:T(8,128)S(1)}, u32[]{:S(2)}, u32[]{:S(2)}) collective-permute-start(f32[256,256]{0,1:T(8,128)S(1)} %add.124), channel_id=1, source_target_pairs={{0,128},{16,144},{32,160},{48,176},{64,192},{80,208},{96,224},{112... | collective-permute-start | bytes 786440 | tf_op jit(solution)/shard_map/ppermute | solution.py:53
  135.2 36.7 %all-to-all-start.4 = ((f32[16,32,256]{2,1,0:T(8,128)}), f32[16,32,256]{2,1,0:T(8,128)S(1)}, u32[]{:S(2)}, u32[]{:S(2)}) async-start(f32[16,32,256]{2,1,0:T(8,128)} %broadcast_in_dim.12), calls=%async_computation.4 | async-start | bytes 1048576 | tf_op jit(solution)/shard_map/all_to_all | solution.py:18
  178.1 36.9 %all-to-all-start.5 = ((f32[16,32,256]{2,1,0:T(8,128)}), f32[16,32,256]{2,1,0:T(8,128)S(1)}, u32[]{:S(2)}, u32[]{:S(2)}) async-start(f32[16,32,256]{2,1,0:T(8,128)} %bitcast.336), calls=%async_computation.5 | async-start | bytes 1048576 | tf_op jit(solution)/shard_map/all_to_all | solution.py:33
  186.4 10.8 %collective-permute-start.8 = (f32[256,256]{0,1:T(8,128)S(1)}, f32[256,256]{0,1:T(8,128)S(1)}, u32[]{:S(2)}, u32[]{:S(2)}) collective-permute-start(f32[256,256]{0,1:T(8,128)S(1)} %fusion.83), channel_id=1, source_target_pairs={{0,8},{1,9},{2,10},{3,11},{4,12},{5,13},{6,14},{7,15},{8,0},{9,1},... | collective-permute-start | bytes 786440 | tf_op jit(solution)/shard_map/ppermute | solution.py:53
  197.3 6.5 %collective-permute-start.9 = (f32[256,256]{0,1:T(8,128)S(1)}, f32[256,256]{0,1:T(8,128)S(1)}, u32[]{:S(2)}, u32[]{:S(2)}) collective-permute-start(f32[256,256]{0,1:T(8,128)S(1)} %add.133), channel_id=1, source_target_pairs={{0,4},{1,5},{2,6},{3,7},{4,0},{5,1},{6,2},{7,3},{8,12},{9,13},{10,... | collective-permute-start | bytes 786440 | tf_op jit(solution)/shard_map/ppermute | solution.py:53
  203.8 8.0 %collective-permute-start.10 = (f32[256,256]{0,1:T(8,128)S(1)}, f32[256,256]{0,1:T(8,128)S(1)}, u32[]{:S(2)}, u32[]{:S(2)}) collective-permute-start(f32[256,256]{0,1:T(8,128)S(1)} %add.134), channel_id=1, source_target_pairs={{0,2},{1,3},{2,0},{3,1},{4,6},{5,7},{6,4},{7,5},{8,10},{9,11},{10,... | collective-permute-start | bytes 786440 | tf_op jit(solution)/shard_map/ppermute | solution.py:53
  212.5 12.0 %collective-permute-start.11 = (f32[256,256]{0,1:T(8,128)}, f32[256,256]{0,1:T(8,128)}, u32[]{:S(2)}, u32[]{:S(2)}) collective-permute-start(f32[256,256]{0,1:T(8,128)} %add.135), channel_id=1, source_target_pairs={{0,1},{1,0},{2,3},{3,2},{4,5},{5,4},{6,7},{7,6},{8,9},{9,8},{10,11... | collective-permute-start | bytes 786440 | tf_op jit(solution)/shard_map/ppermute | solution.py:53
  216.8 28.8 %all-to-all-start.6 = ((f32[16,32,256]{2,1,0:T(8,128)}), f32[16,32,256]{2,1,0:T(8,128)S(1)}, u32[]{:S(2)}, u32[]{:S(2)}) async-start(f32[16,32,256]{2,1,0:T(8,128)} %broadcast_in_dim.13), calls=%async_computation.6 | async-start | bytes 1048576 | tf_op jit(solution)/shard_map/all_to_all | solution.py:18
  247.8 13.3 %collective-permute-start.12 = (f32[256,256]{0,1:T(8,128)}, f32[256,256]{0,1:T(8,128)}, u32[]{:S(2)}, u32[]{:S(2)}) collective-permute-start(f32[256,256]{0,1:T(8,128)} %fusion.103), channel_id=1, source_target_pairs={{0,16},{16,0},{32,48},{48,32},{64,80},{80,64},{96,112},{112,96},{1... | collective-permute-start | bytes 786440 | tf_op jit(solution)/shard_map/ppermute | solution.py:53
  250.4 35.3 %all-to-all-start.7 = ((f32[16,32,256]{2,1,0:T(8,128)}), f32[16,32,256]{2,1,0:T(8,128)S(1)}, u32[]{:S(2)}, u32[]{:S(2)}) async-start(f32[16,32,256]{2,1,0:T(8,128)} %bitcast.335), calls=%async_computation.7 | async-start | bytes 1048576 | tf_op jit(solution)/shard_map/all_to_all | solution.py:33
  262.2 12.5 %collective-permute-start.13 = (f32[256,256]{0,1:T(8,128)S(1)}, f32[256,256]{0,1:T(8,128)S(1)}, u32[]{:S(2)}, u32[]{:S(2)}) collective-permute-start(f32[256,256]{0,1:T(8,128)S(1)} %add.140), channel_id=1, source_target_pairs={{0,32},{16,48},{32,0},{48,16},{64,96},{80,112},{96,64},{112,80},{1... | collective-permute-start | bytes 786440 | tf_op jit(solution)/shard_map/ppermute | solution.py:53
  274.8 9.9 %collective-permute-start.14 = (f32[256,256]{0,1:T(8,128)S(1)}, f32[256,256]{0,1:T(8,128)S(1)}, u32[]{:S(2)}, u32[]{:S(2)}) collective-permute-start(f32[256,256]{0,1:T(8,128)S(1)} %add.141), channel_id=1, source_target_pairs={{0,64},{16,80},{32,96},{48,112},{64,0},{80,16},{96,32},{112,48},{1... | collective-permute-start | bytes 786440 | tf_op jit(solution)/shard_map/ppermute | solution.py:53
  284.7 21.6 %collective-permute-start.15 = (f32[256,256]{0,1:T(8,128)S(1)}, f32[256,256]{0,1:T(8,128)}, u32[]{:S(2)}, u32[]{:S(2)}) collective-permute-start(f32[256,256]{0,1:T(8,128)S(1)} %add.142), channel_id=1, source_target_pairs={{0,128},{16,144},{32,160},{48,176},{64,192},{80,208},{96,224},{112... | collective-permute-start | bytes 786440 | tf_op jit(solution)/shard_map/ppermute | solution.py:53
  287.7 40.2 %all-to-all-start.8 = ((f32[16,32,256]{2,1,0:T(8,128)}), f32[16,32,256]{2,1,0:T(8,128)S(1)}, u32[]{:S(2)}, u32[]{:S(2)}) async-start(f32[16,32,256]{2,1,0:T(8,128)} %broadcast_in_dim.14), calls=%async_computation.8 | async-start | bytes 1048576 | tf_op jit(solution)/shard_map/all_to_all | solution.py:18
  (12 other events, 34.3 us)
